TPU v7x, 256 devices: a whole 4x4x8 slice. The times are simulated.
256 devices in a mesh: seq: 32 (over z, y), head: 8 (over x, core).
Axes of the slice: x: 4, y: 4, z: 8, core: 2. Of those that a mesh axis runs over, the one named last changes fastest.
Arguments:
- x_in: bfloat16 [16384, 5120], P('seq', 'head'), may hold values from -6 to 6
- z_gate: bfloat16 [16384, 5120], P('seq', 'head'), may hold values from -6 to 6
- step_size: float32 [80, 16384], P('head', 'seq'), may hold values from 0.005 to 0.05
- log_decay: float32 [80, 16384], P('head', 'seq'), may hold values from -1 to 0
- b_proj: bfloat16 [16384, 128], P('seq'), may hold values from -6 to 6
- c_proj: bfloat16 [16384, 128], P('seq'), may hold values from -0.5 to 0.5
- d_skip: float32 [80], P('head'), may hold values from 0.5 to 1.5
- norm_weight: float32 [5120], P('head'), may hold values from 0.5 to 1.5
- w_out: bfloat16 [5120, 2560], P('head'), may hold values from -0.125 to 0.125
- resid: bfloat16 [2560, 16384], P('head', 'seq'), may hold values from -6 to 6
- masked_pos: int32 [8192], P('seq'), may hold values from 0 to 16383, as said below
- owner: int32 [8192], P('seq'), may hold values from 0 to 31, as said below
Outputs:
- block_out: bfloat16 [2560, 16384], P('head', 'seq')
- targets: bfloat16 [2560, 16384], P('head', 'seq')
Inputs may be any that keep to these rules, and one draw needn't show every extreme that they name: `masked_pos`: the 256 entries listed by device i of seq are distinct positions from i * 512 to (i + 1) * 512 - 1. Among the 256 entries of each device of seq, no owner is named more than 16 times; one owner, the same for all devices, is named exactly 16 times by each device.
All inputs are finite; a program needn't handle non-finite values.
Results may differ from a plain program's by a relative error of at most 0.025.
Values may be sent and summed in bfloat16 or wider, within the bound.
No kernel may reach another device: no remote copies, remote signals or barrier semaphores. Data moves between devices by JAX's collectives and lax.ppermute only.
A program may use at most 64 MiB of HBM per device.

v0:
```python
import jax
import jax.numpy as jnp
from jax import lax
from jax.sharding import PartitionSpec as P

BLOCK = 256


EPS = 1e-05


def from_behind(value, axis, steps):
    count = lax.axis_size(axis)
    leading, last = (max(0, -steps), min(count, count - steps))
    return lax.ppermute(value, axis, [(source, source + steps) for source in range(leading, last)])


def body(
    x_in,
    z_gate,
    step_size,
    log_decay,
    b_proj,
    c_proj,
    d_skip,
    norm_weight,
    w_out,
    resid,
    masked_pos,
    owner,
):
    rows_here = x_in.shape[0]
    heads_here = step_size.shape[0]
    channels = x_in.shape[1]
    head_size = channels // heads_here
    state_size = b_proj.shape[1]
    blocks = rows_here // BLOCK
    x_all = x_in.reshape(blocks, BLOCK, heads_here, head_size)
    b_all = b_proj.reshape(blocks, BLOCK, state_size)
    c_all = c_proj.reshape(blocks, BLOCK, state_size)
    dt_all = step_size.reshape(heads_here, blocks, BLOCK)
    cum_all = jnp.cumsum(log_decay.reshape(heads_here, blocks, BLOCK), axis=-1)
    lower = jnp.arange(BLOCK)[:, None] >= jnp.arange(BLOCK)[None, :]
    gram = jnp.einsum("ctn,csn->cts", c_all, b_all, preferred_element_type=jnp.float32)
    spread = cum_all[:, :, :, None] - cum_all[:, :, None, :]
    decay = jnp.where(lower[None, None], jnp.exp(jnp.where(lower[None, None], spread, 0.0)), 0.0)
    weights = (gram[None] * decay * dt_all[:, :, None, :]).astype(jnp.bfloat16)
    inner = jnp.einsum("hcts,cshp->cthp", weights, x_all, preferred_element_type=jnp.float32)
    end_weight = jnp.exp(cum_all[:, :, -1:] - cum_all) * dt_all
    keyed = (end_weight[..., None] * b_all.astype(jnp.float32)[None]).astype(jnp.bfloat16)
    block_states = jnp.einsum("hcsn,cshp->chpn", keyed, x_all, preferred_element_type=jnp.float32)
    block_decay = jnp.exp(cum_all[:, :, -1])
    running = jnp.zeros((heads_here, head_size, state_size), jnp.float32)
    reach = jnp.ones((heads_here,), jnp.float32)
    starts = []
    reaches = []
    for number in range(blocks):
        starts.append(running)
        reaches.append(reach)
        running = block_decay[:, number][:, None, None] * running + block_states[number]
        reach = reach * block_decay[:, number]
    empty_state = jnp.zeros((heads_here, head_size, state_size), jnp.float32)

    def relay_step(turn, pair):
        arrived = from_behind(pair[1].astype(jnp.bfloat16), "seq", 1).astype(jnp.float32)
        return (arrived, reach[:, None, None] * arrived + running)

    incoming, _ = lax.fori_loop(0, lax.axis_size("seq") - 1, relay_step, (empty_state, running))
    start_states = jnp.stack(starts) + jnp.stack(reaches)[:, :, None, None] * incoming[None]
    carried = jnp.einsum(
        "ctn,chpn->cthp",
        c_all.astype(jnp.float32),
        start_states,
        precision=lax.Precision.HIGHEST,
        preferred_element_type=jnp.float32,
    )
    carried = carried * jnp.transpose(jnp.exp(cum_all), (1, 2, 0))[:, :, :, None]
    mixed = inner + carried + d_skip[None, None, :, None] * x_all.astype(jnp.float32)
    mixed = mixed.reshape(rows_here, channels)
    gated = mixed * jax.nn.silu(z_gate.astype(jnp.float32))
    squares = lax.psum(jnp.sum(gated * gated, axis=-1), "head")
    mean_sq = squares / (channels * lax.axis_size("head"))
    hidden = (gated * lax.rsqrt(mean_sq + EPS)[:, None] * norm_weight[None, :]).astype(jnp.bfloat16)
    proj = lax.psum_scatter(
        jnp.einsum("kd,tk->dt", w_out, hidden, preferred_element_type=jnp.float32).astype(
            jnp.bfloat16
        ),
        "head",
        scatter_dimension=0,
        tiled=True,
    ).astype(jnp.float32)
    block_out = (resid.astype(jnp.float32) + proj).astype(jnp.bfloat16)
    features = resid.shape[0] * lax.axis_size("head")
    seq_count = lax.axis_size("seq")
    masked_here = masked_pos.shape[0]
    slot_cap = 2 * masked_here // seq_count
    local_pos = masked_pos % rows_here
    owner_hot = (owner[:, None] == jnp.arange(seq_count, dtype=jnp.int32)[None, :]).astype(
        jnp.bfloat16
    )
    strictly = (jnp.arange(masked_here)[:, None] > jnp.arange(masked_here)[None, :]).astype(
        jnp.bfloat16
    )
    earlier = jnp.dot(strictly, owner_hot, preferred_element_type=jnp.float32)
    ranks = jnp.sum(earlier * owner_hot.astype(jnp.float32), axis=-1).astype(jnp.int32)
    placed = owner * slot_cap + ranks
    local_feat = resid.shape[0]
    out_wide = block_out.astype(jnp.float32)
    totals = lax.psum((jnp.sum(out_wide, axis=0), jnp.sum(out_wide * out_wide, axis=0)), "head")
    mean_col = totals[0] / features
    variance = totals[1] / features - mean_col * mean_col
    normed = ((out_wide - mean_col[None, :]) * lax.rsqrt(variance + EPS)[None, :]).astype(
        jnp.bfloat16
    )
    buffer = (
        jnp.zeros((local_feat, seq_count * slot_cap), jnp.bfloat16)
        .at[:, placed]
        .set(normed[:, local_pos])
    )
    received = lax.all_to_all(
        buffer.reshape(local_feat, seq_count, slot_cap),
        "seq",
        split_axis=1,
        concat_axis=1,
        tiled=True,
    )
    targets = received.reshape(local_feat, seq_count * slot_cap)
    return (block_out, targets)


def solution(mesh):
    placed = (
        P("seq", "head"),
        P("seq", "head"),
        P("head", "seq"),
        P("head", "seq"),
        P("seq", None),
        P("seq", None),
        P("head"),
        P("head"),
        P("head", None),
        P("head", "seq"),
        P("seq"),
        P("seq"),
    )
    return jax.shard_map(
        body,
        mesh=mesh,
        in_specs=placed,
        out_specs=(P("head", "seq"), P("head", "seq")),
        check_vma=False,
    )
```

profile of v0, /device:TPU:32, one launch (start us, length us, event | category | flops | bytes accessed | tf_op | source)
XLA Modules:
  0.0 544.3 jit_solution(9776107336804343024)
XLA Ops:
  27.7 358.7 %while.12 = (s32[]{:T(128)}, f32[10,64,128]{2,1,0:T(8,128)}, bf16[10,64,128]{2,1,0:T(8,128)(2,1)}, f32[10]{0:T(128)S(1)}, f32[10,64,128]{2,1,0:T(8,128)}, /*index=5*/s32[]{:T(128)}) while((s32[]{:T(128)}, f32[10,64,128]{2,1,0:T(8,128)}, bf16[10,64,128]{2,1,0:T(8,128)(2,1)}, f32[10]{0:T(128)S(1)}, f32[10,64,128]{2,1,0:T(8,128)}, ...), condition=%wide.region_3.4_spmd, body=%wide.region_2.3_spmd.sunk | while | flops 327682 | bytes 1638549 | solution.py:68
  52.9 7.6 %collective-permute-done = bf16[10,64,128]{2,1,0:T(8,128)(2,1)S(1)} collective-permute-done((bf16[10,64,128]{2,1,0:T(8,128)(2,1)}, bf16[10,64,128]{2,1,0:T(8,128)(2,1)S(1)}, u32[]{:S(2)}, u32[]{:S(2)}) %collective-permute-start) | collective-permute-done | bytes 163872 | tf_op jit(solution)/shard_map/while/body/eval_jaxpr/ppermute | solution.py:15
  64.2 7.6 %collective-permute-done = bf16[10,64,128]{2,1,0:T(8,128)(2,1)S(1)} collective-permute-done((bf16[10,64,128]{2,1,0:T(8,128)(2,1)}, bf16[10,64,128]{2,1,0:T(8,128)(2,1)S(1)}, u32[]{:S(2)}, u32[]{:S(2)}) %collective-permute-start) | collective-permute-done | bytes 163872 | tf_op jit(solution)/shard_map/while/body/eval_jaxpr/ppermute | solution.py:15
  86.7 7.6 %collective-permute-done = bf16[10,64,128]{2,1,0:T(8,128)(2,1)S(1)} collective-permute-done((bf16[10,64,128]{2,1,0:T(8,128)(2,1)}, bf16[10,64,128]{2,1,0:T(8,128)(2,1)S(1)}, u32[]{:S(2)}, u32[]{:S(2)}) %collective-permute-start) | collective-permute-done | bytes 163872 | tf_op jit(solution)/shard_map/while/body/eval_jaxpr/ppermute | solution.py:15
  98.0 7.6 %collective-permute-done = bf16[10,64,128]{2,1,0:T(8,128)(2,1)S(1)} collective-permute-done((bf16[10,64,128]{2,1,0:T(8,128)(2,1)}, bf16[10,64,128]{2,1,0:T(8,128)(2,1)S(1)}, u32[]{:S(2)}, u32[]{:S(2)}) %collective-permute-start) | collective-permute-done | bytes 163872 | tf_op jit(solution)/shard_map/while/body/eval_jaxpr/ppermute | solution.py:15
  109.3 8.1 %collective-permute-done = bf16[10,64,128]{2,1,0:T(8,128)(2,1)S(1)} collective-permute-done((bf16[10,64,128]{2,1,0:T(8,128)(2,1)}, bf16[10,64,128]{2,1,0:T(8,128)(2,1)S(1)}, u32[]{:S(2)}, u32[]{:S(2)}) %collective-permute-start) | collective-permute-done | bytes 163872 | tf_op jit(solution)/shard_map/while/body/eval_jaxpr/ppermute | solution.py:15
  121.1 9.3 %collective-permute-done = bf16[10,64,128]{2,1,0:T(8,128)(2,1)S(1)} collective-permute-done((bf16[10,64,128]{2,1,0:T(8,128)(2,1)}, bf16[10,64,128]{2,1,0:T(8,128)(2,1)S(1)}, u32[]{:S(2)}, u32[]{:S(2)}) %collective-permute-start) | collective-permute-done | bytes 163872 | tf_op jit(solution)/shard_map/while/body/eval_jaxpr/ppermute | solution.py:15
  134.0 8.5 %collective-permute-done = bf16[10,64,128]{2,1,0:T(8,128)(2,1)S(1)} collective-permute-done((bf16[10,64,128]{2,1,0:T(8,128)(2,1)}, bf16[10,64,128]{2,1,0:T(8,128)(2,1)S(1)}, u32[]{:S(2)}, u32[]{:S(2)}) %collective-permute-start) | collective-permute-done | bytes 163872 | tf_op jit(solution)/shard_map/while/body/eval_jaxpr/ppermute | solution.py:15
  146.2 7.6 %collective-permute-done = bf16[10,64,128]{2,1,0:T(8,128)(2,1)S(1)} collective-permute-done((bf16[10,64,128]{2,1,0:T(8,128)(2,1)}, bf16[10,64,128]{2,1,0:T(8,128)(2,1)S(1)}, u32[]{:S(2)}, u32[]{:S(2)}) %collective-permute-start) | collective-permute-done | bytes 163872 | tf_op jit(solution)/shard_map/while/body/eval_jaxpr/ppermute | solution.py:15
  168.8 7.6 %collective-permute-done = bf16[10,64,128]{2,1,0:T(8,128)(2,1)S(1)} collective-permute-done((bf16[10,64,128]{2,1,0:T(8,128)(2,1)}, bf16[10,64,128]{2,1,0:T(8,128)(2,1)S(1)}, u32[]{:S(2)}, u32[]{:S(2)}) %collective-permute-start) | collective-permute-done | bytes 163872 | tf_op jit(solution)/shard_map/while/body/eval_jaxpr/ppermute | solution.py:15
  191.4 7.6 %collective-permute-done = bf16[10,64,128]{2,1,0:T(8,128)(2,1)S(1)} collective-permute-done((bf16[10,64,128]{2,1,0:T(8,128)(2,1)}, bf16[10,64,128]{2,1,0:T(8,128)(2,1)S(1)}, u32[]{:S(2)}, u32[]{:S(2)}) %collective-permute-start) | collective-permute-done | bytes 163872 | tf_op jit(solution)/shard_map/while/body/eval_jaxpr/ppermute | solution.py:15
  202.6 7.6 %collective-permute-done = bf16[10,64,128]{2,1,0:T(8,128)(2,1)S(1)} collective-permute-done((bf16[10,64,128]{2,1,0:T(8,128)(2,1)}, bf16[10,64,128]{2,1,0:T(8,128)(2,1)S(1)}, u32[]{:S(2)}, u32[]{:S(2)}) %collective-permute-start) | collective-permute-done | bytes 163872 | tf_op jit(solution)/shard_map/while/body/eval_jaxpr/ppermute | solution.py:15
  225.2 8.7 %collective-permute-done = bf16[10,64,128]{2,1,0:T(8,128)(2,1)S(1)} collective-permute-done((bf16[10,64,128]{2,1,0:T(8,128)(2,1)}, bf16[10,64,128]{2,1,0:T(8,128)(2,1)S(1)}, u32[]{:S(2)}, u32[]{:S(2)}) %collective-permute-start) | collective-permute-done | bytes 163872 | tf_op jit(solution)/shard_map/while/body/eval_jaxpr/ppermute | solution.py:15
  237.6 8.9 %collective-permute-done = bf16[10,64,128]{2,1,0:T(8,128)(2,1)S(1)} collective-permute-done((bf16[10,64,128]{2,1,0:T(8,128)(2,1)}, bf16[10,64,128]{2,1,0:T(8,128)(2,1)S(1)}, u32[]{:S(2)}, u32[]{:S(2)}) %collective-permute-start) | collective-permute-done | bytes 163872 | tf_op jit(solution)/shard_map/while/body/eval_jaxpr/ppermute | solution.py:15
  250.1 8.0 %collective-permute-done = bf16[10,64,128]{2,1,0:T(8,128)(2,1)S(1)} collective-permute-done((bf16[10,64,128]{2,1,0:T(8,128)(2,1)}, bf16[10,64,128]{2,1,0:T(8,128)(2,1)S(1)}, u32[]{:S(2)}, u32[]{:S(2)}) %collective-permute-start) | collective-permute-done | bytes 163872 | tf_op jit(solution)/shard_map/while/body/eval_jaxpr/ppermute | solution.py:15
  261.8 7.6 %collective-permute-done = bf16[10,64,128]{2,1,0:T(8,128)(2,1)S(1)} collective-permute-done((bf16[10,64,128]{2,1,0:T(8,128)(2,1)}, bf16[10,64,128]{2,1,0:T(8,128)(2,1)S(1)}, u32[]{:S(2)}, u32[]{:S(2)}) %collective-permute-start) | collective-permute-done | bytes 163872 | tf_op jit(solution)/shard_map/while/body/eval_jaxpr/ppermute | solution.py:15
  295.6 7.6 %collective-permute-done = bf16[10,64,128]{2,1,0:T(8,128)(2,1)S(1)} collective-permute-done((bf16[10,64,128]{2,1,0:T(8,128)(2,1)}, bf16[10,64,128]{2,1,0:T(8,128)(2,1)S(1)}, u32[]{:S(2)}, u32[]{:S(2)}) %collective-permute-start) | collective-permute-done | bytes 163872 | tf_op jit(solution)/shard_map/while/body/eval_jaxpr/ppermute | solution.py:15
  329.5 8.3 %collective-permute-done = bf16[10,64,128]{2,1,0:T(8,128)(2,1)S(1)} collective-permute-done((bf16[10,64,128]{2,1,0:T(8,128)(2,1)}, bf16[10,64,128]{2,1,0:T(8,128)(2,1)S(1)}, u32[]{:S(2)}, u32[]{:S(2)}) %collective-permute-start) | collective-permute-done | bytes 163872 | tf_op jit(solution)/shard_map/while/body/eval_jaxpr/ppermute | solution.py:15
  341.5 9.3 %collective-permute-done = bf16[10,64,128]{2,1,0:T(8,128)(2,1)S(1)} collective-permute-done((bf16[10,64,128]{2,1,0:T(8,128)(2,1)}, bf16[10,64,128]{2,1,0:T(8,128)(2,1)S(1)}, u32[]{:S(2)}, u32[]{:S(2)}) %collective-permute-start) | collective-permute-done | bytes 163872 | tf_op jit(solution)/shard_map/while/body/eval_jaxpr/ppermute | solution.py:15
  395.2 12.4 %psum.21 = f32[512]{0:T(512)S(1)} all-reduce(f32[512]{0:T(512)S(1)} %multiply_reduce_fusion), channel_id=1, replica_groups=mesh['seq'=32,'head'=8] {'head'}, use_global_device_ids=true, to_apply=%region_5.6 | all-reduce | flops 512 | bytes 4096 | tf_op jit(solution)/shard_map/psum | solution.py:81
  419.6 68.4 %reduce-scatter.4.cloned.1.call-done = bf16[320,512]{1,0:T(8,128)(2,1)} async-done(((bf16[2560,512]{1,0:T(8,128)(2,1)}), bf16[320,512]{1,0:T(8,128)(2,1)}) %reduce-scatter.4.cloned.1.call-update) | async-done | bytes 327696
  491.9 13.1 %all-reduce.2 = (f32[512]{0:T(512)S(1)}, f32[512]{0:T(512)S(1)}) all-reduce(f32[512]{0:T(512)S(1)} %get-tuple-element.36, f32[512]{0:T(512)S(1)} %get-tuple-element.35), channel_id=1, replica_groups=mesh['seq'=32,'head'=8] {'head'}, use_global_device_ids=true, to_apply=%region_11.12 | all-reduce | flops 1024 | bytes 8192 | tf_op jit(solution)/shard_map/psum | solution.py:109
  511.2 10.1 %all-to-all-start = ((bf16[320,32,16]{0,2,1:T(8,128)(2,1)}), bf16[320,32,16]{0,2,1:T(8,128)(2,1)}, u32[]{:S(2)}, u32[]{:S(2)}) async-start(bf16[320,32,16]{0,2,1:T(8,128)(2,1)} %bitcast.63), calls=%async_computation | async-start | bytes 786432 | tf_op jit(solution)/shard_map/all_to_all | solution.py:120
  523.2 12.4 %all-to-all-done = bf16[320,32,16]{0,2,1:T(8,128)(2,1)} async-done(((bf16[320,32,16]{0,2,1:T(8,128)(2,1)}), bf16[320,32,16]{0,2,1:T(8,128)(2,1)}, u32[]{:S(2)}, u32[]{:S(2)}) %all-to-all-start) | async-done | bytes 327712 | tf_op jit(solution)/shard_map/all_to_all | solution.py:120
  (147 shorter events, 268.3 us)
Async XLA Ops:
  7.2 480.9 %reduce-scatter.4.cloned.1.call-start = ((), (), s32[]{:S(2)}) async-start(), calls=%async_computation.2 | async-start | bytes 2949120
  27.7 10.3 %collective-permute-start = (bf16[10,64,128]{2,1,0:T(8,128)(2,1)}, bf16[10,64,128]{2,1,0:T(8,128)(2,1)S(1)}, u32[]{:S(2)}, u32[]{:S(2)}) collective-permute-start(bf16[10,64,128]{2,1,0:T(8,128)(2,1)} %get-tuple-element.103), channel_id=1, source_target_pairs={{0,8},{8,16},{16,24},{24,32},{32,40},{40,48},{48,56},{56,64},{64,7... | collective-permute-start | bytes 491528 | tf_op jit(solution)/shard_map/while/body/eval_jaxpr/ppermute | solution.py:15
  39.7 9.5 %collective-permute-start = (bf16[10,64,128]{2,1,0:T(8,128)(2,1)}, bf16[10,64,128]{2,1,0:T(8,128)(2,1)S(1)}, u32[]{:S(2)}, u32[]{:S(2)}) collective-permute-start(bf16[10,64,128]{2,1,0:T(8,128)(2,1)} %get-tuple-element.103), channel_id=1, source_target_pairs={{0,8},{8,16},{16,24},{24,32},{32,40},{40,48},{48,56},{56,64},{64,7... | collective-permute-start | bytes 491528 | tf_op jit(solution)/shard_map/while/body/eval_jaxpr/ppermute | solution.py:15
  51.0 9.5 %collective-permute-start = (bf16[10,64,128]{2,1,0:T(8,128)(2,1)}, bf16[10,64,128]{2,1,0:T(8,128)(2,1)S(1)}, u32[]{:S(2)}, u32[]{:S(2)}) collective-permute-start(bf16[10,64,128]{2,1,0:T(8,128)(2,1)} %get-tuple-element.103), channel_id=1, source_target_pairs={{0,8},{8,16},{16,24},{24,32},{32,40},{40,48},{48,56},{56,64},{64,7... | collective-permute-start | bytes 491528 | tf_op jit(solution)/shard_map/while/body/eval_jaxpr/ppermute | solution.py:15
  62.3 9.5 %collective-permute-start = (bf16[10,64,128]{2,1,0:T(8,128)(2,1)}, bf16[10,64,128]{2,1,0:T(8,128)(2,1)S(1)}, u32[]{:S(2)}, u32[]{:S(2)}) collective-permute-start(bf16[10,64,128]{2,1,0:T(8,128)(2,1)} %get-tuple-element.103), channel_id=1, source_target_pairs={{0,8},{8,16},{16,24},{24,32},{32,40},{40,48},{48,56},{56,64},{64,7... | collective-permute-start | bytes 491528 | tf_op jit(solution)/shard_map/while/body/eval_jaxpr/ppermute | solution.py:15
  73.5 9.5 %collective-permute-start = (bf16[10,64,128]{2,1,0:T(8,128)(2,1)}, bf16[10,64,128]{2,1,0:T(8,128)(2,1)S(1)}, u32[]{:S(2)}, u32[]{:S(2)}) collective-permute-start(bf16[10,64,128]{2,1,0:T(8,128)(2,1)} %get-tuple-element.103), channel_id=1, source_target_pairs={{0,8},{8,16},{16,24},{24,32},{32,40},{40,48},{48,56},{56,64},{64,7... | collective-permute-start | bytes 491528 | tf_op jit(solution)/shard_map/while/body/eval_jaxpr/ppermute | solution.py:15
  84.8 9.5 %collective-permute-start = (bf16[10,64,128]{2,1,0:T(8,128)(2,1)}, bf16[10,64,128]{2,1,0:T(8,128)(2,1)S(1)}, u32[]{:S(2)}, u32[]{:S(2)}) collective-permute-start(bf16[10,64,128]{2,1,0:T(8,128)(2,1)} %get-tuple-element.103), channel_id=1, source_target_pairs={{0,8},{8,16},{16,24},{24,32},{32,40},{40,48},{48,56},{56,64},{64,7... | collective-permute-start | bytes 491528 | tf_op jit(solution)/shard_map/while/body/eval_jaxpr/ppermute | solution.py:15
  96.1 9.5 %collective-permute-start = (bf16[10,64,128]{2,1,0:T(8,128)(2,1)}, bf16[10,64,128]{2,1,0:T(8,128)(2,1)S(1)}, u32[]{:S(2)}, u32[]{:S(2)}) collective-permute-start(bf16[10,64,128]{2,1,0:T(8,128)(2,1)} %get-tuple-element.103), channel_id=1, source_target_pairs={{0,8},{8,16},{16,24},{24,32},{32,40},{40,48},{48,56},{56,64},{64,7... | collective-permute-start | bytes 491528 | tf_op jit(solution)/shard_map/while/body/eval_jaxpr/ppermute | solution.py:15
  107.4 10.0 %collective-permute-start = (bf16[10,64,128]{2,1,0:T(8,128)(2,1)}, bf16[10,64,128]{2,1,0:T(8,128)(2,1)S(1)}, u32[]{:S(2)}, u32[]{:S(2)}) collective-permute-start(bf16[10,64,128]{2,1,0:T(8,128)(2,1)} %get-tuple-element.103), channel_id=1, source_target_pairs={{0,8},{8,16},{16,24},{24,32},{32,40},{40,48},{48,56},{56,64},{64,7... | collective-permute-start | bytes 491528 | tf_op jit(solution)/shard_map/while/body/eval_jaxpr/ppermute | solution.py:15
  119.2 11.2 %collective-permute-start = (bf16[10,64,128]{2,1,0:T(8,128)(2,1)}, bf16[10,64,128]{2,1,0:T(8,128)(2,1)S(1)}, u32[]{:S(2)}, u32[]{:S(2)}) collective-permute-start(bf16[10,64,128]{2,1,0:T(8,128)(2,1)} %get-tuple-element.103), channel_id=1, source_target_pairs={{0,8},{8,16},{16,24},{24,32},{32,40},{40,48},{48,56},{56,64},{64,7... | collective-permute-start | bytes 491528 | tf_op jit(solution)/shard_map/while/body/eval_jaxpr/ppermute | solution.py:15
  132.1 10.4 %collective-permute-start = (bf16[10,64,128]{2,1,0:T(8,128)(2,1)}, bf16[10,64,128]{2,1,0:T(8,128)(2,1)S(1)}, u32[]{:S(2)}, u32[]{:S(2)}) collective-permute-start(bf16[10,64,128]{2,1,0:T(8,128)(2,1)} %get-tuple-element.103), channel_id=1, source_target_pairs={{0,8},{8,16},{16,24},{24,32},{32,40},{40,48},{48,56},{56,64},{64,7... | collective-permute-start | bytes 491528 | tf_op jit(solution)/shard_map/while/body/eval_jaxpr/ppermute | solution.py:15
  144.3 9.6 %collective-permute-start = (bf16[10,64,128]{2,1,0:T(8,128)(2,1)}, bf16[10,64,128]{2,1,0:T(8,128)(2,1)S(1)}, u32[]{:S(2)}, u32[]{:S(2)}) collective-permute-start(bf16[10,64,128]{2,1,0:T(8,128)(2,1)} %get-tuple-element.103), channel_id=1, source_target_pairs={{0,8},{8,16},{16,24},{24,32},{32,40},{40,48},{48,56},{56,64},{64,7... | collective-permute-start | bytes 491528 | tf_op jit(solution)/shard_map/while/body/eval_jaxpr/ppermute | solution.py:15
  155.6 9.5 %collective-permute-start = (bf16[10,64,128]{2,1,0:T(8,128)(2,1)}, bf16[10,64,128]{2,1,0:T(8,128)(2,1)S(1)}, u32[]{:S(2)}, u32[]{:S(2)}) collective-permute-start(bf16[10,64,128]{2,1,0:T(8,128)(2,1)} %get-tuple-element.103), channel_id=1, source_target_pairs={{0,8},{8,16},{16,24},{24,32},{32,40},{40,48},{48,56},{56,64},{64,7... | collective-permute-start | bytes 491528 | tf_op jit(solution)/shard_map/while/body/eval_jaxpr/ppermute | solution.py:15
  166.9 9.5 %collective-permute-start = (bf16[10,64,128]{2,1,0:T(8,128)(2,1)}, bf16[10,64,128]{2,1,0:T(8,128)(2,1)S(1)}, u32[]{:S(2)}, u32[]{:S(2)}) collective-permute-start(bf16[10,64,128]{2,1,0:T(8,128)(2,1)} %get-tuple-element.103), channel_id=1, source_target_pairs={{0,8},{8,16},{16,24},{24,32},{32,40},{40,48},{48,56},{56,64},{64,7... | collective-permute-start | bytes 491528 | tf_op jit(solution)/shard_map/while/body/eval_jaxpr/ppermute | solution.py:15
  178.2 9.5 %collective-permute-start = (bf16[10,64,128]{2,1,0:T(8,128)(2,1)}, bf16[10,64,128]{2,1,0:T(8,128)(2,1)S(1)}, u32[]{:S(2)}, u32[]{:S(2)}) collective-permute-start(bf16[10,64,128]{2,1,0:T(8,128)(2,1)} %get-tuple-element.103), channel_id=1, source_target_pairs={{0,8},{8,16},{16,24},{24,32},{32,40},{40,48},{48,56},{56,64},{64,7... | collective-permute-start | bytes 491528 | tf_op jit(solution)/shard_map/while/body/eval_jaxpr/ppermute | solution.py:15
  189.4 9.5 %collective-permute-start = (bf16[10,64,128]{2,1,0:T(8,128)(2,1)}, bf16[10,64,128]{2,1,0:T(8,128)(2,1)S(1)}, u32[]{:S(2)}, u32[]{:S(2)}) collective-permute-start(bf16[10,64,128]{2,1,0:T(8,128)(2,1)} %get-tuple-element.103), channel_id=1, source_target_pairs={{0,8},{8,16},{16,24},{24,32},{32,40},{40,48},{48,56},{56,64},{64,7... | collective-permute-start | bytes 491528 | tf_op jit(solution)/shard_map/while/body/eval_jaxpr/ppermute | solution.py:15
  200.7 9.5 %collective-permute-start = (bf16[10,64,128]{2,1,0:T(8,128)(2,1)}, bf16[10,64,128]{2,1,0:T(8,128)(2,1)S(1)}, u32[]{:S(2)}, u32[]{:S(2)}) collective-permute-start(bf16[10,64,128]{2,1,0:T(8,128)(2,1)} %get-tuple-element.103), channel_id=1, source_target_pairs={{0,8},{8,16},{16,24},{24,32},{32,40},{40,48},{48,56},{56,64},{64,7... | collective-permute-start | bytes 491528 | tf_op jit(solution)/shard_map/while/body/eval_jaxpr/ppermute | solution.py:15
  212.0 9.5 %collective-permute-start = (bf16[10,64,128]{2,1,0:T(8,128)(2,1)}, bf16[10,64,128]{2,1,0:T(8,128)(2,1)S(1)}, u32[]{:S(2)}, u32[]{:S(2)}) collective-permute-start(bf16[10,64,128]{2,1,0:T(8,128)(2,1)} %get-tuple-element.103), channel_id=1, source_target_pairs={{0,8},{8,16},{16,24},{24,32},{32,40},{40,48},{48,56},{56,64},{64,7... | collective-permute-start | bytes 491528 | tf_op jit(solution)/shard_map/while/body/eval_jaxpr/ppermute | solution.py:15
  223.3 10.6 %collective-permute-start = (bf16[10,64,128]{2,1,0:T(8,128)(2,1)}, bf16[10,64,128]{2,1,0:T(8,128)(2,1)S(1)}, u32[]{:S(2)}, u32[]{:S(2)}) collective-permute-start(bf16[10,64,128]{2,1,0:T(8,128)(2,1)} %get-tuple-element.103), channel_id=1, source_target_pairs={{0,8},{8,16},{16,24},{24,32},{32,40},{40,48},{48,56},{56,64},{64,7... | collective-permute-start | bytes 491528 | tf_op jit(solution)/shard_map/while/body/eval_jaxpr/ppermute | solution.py:15
  235.6 10.8 %collective-permute-start = (bf16[10,64,128]{2,1,0:T(8,128)(2,1)}, bf16[10,64,128]{2,1,0:T(8,128)(2,1)S(1)}, u32[]{:S(2)}, u32[]{:S(2)}) collective-permute-start(bf16[10,64,128]{2,1,0:T(8,128)(2,1)} %get-tuple-element.103), channel_id=1, source_target_pairs={{0,8},{8,16},{16,24},{24,32},{32,40},{40,48},{48,56},{56,64},{64,7... | collective-permute-start | bytes 491528 | tf_op jit(solution)/shard_map/while/body/eval_jaxpr/ppermute | solution.py:15
  248.2 9.9 %collective-permute-start = (bf16[10,64,128]{2,1,0:T(8,128)(2,1)}, bf16[10,64,128]{2,1,0:T(8,128)(2,1)S(1)}, u32[]{:S(2)}, u32[]{:S(2)}) collective-permute-start(bf16[10,64,128]{2,1,0:T(8,128)(2,1)} %get-tuple-element.103), channel_id=1, source_target_pairs={{0,8},{8,16},{16,24},{24,32},{32,40},{40,48},{48,56},{56,64},{64,7... | collective-permute-start | bytes 491528 | tf_op jit(solution)/shard_map/while/body/eval_jaxpr/ppermute | solution.py:15
  327.6 10.2 %collective-permute-start = (bf16[10,64,128]{2,1,0:T(8,128)(2,1)}, bf16[10,64,128]{2,1,0:T(8,128)(2,1)S(1)}, u32[]{:S(2)}, u32[]{:S(2)}) collective-permute-start(bf16[10,64,128]{2,1,0:T(8,128)(2,1)} %get-tuple-element.103), channel_id=1, source_target_pairs={{0,8},{8,16},{16,24},{24,32},{32,40},{40,48},{48,56},{56,64},{64,7... | collective-permute-start | bytes 491528 | tf_op jit(solution)/shard_map/while/body/eval_jaxpr/ppermute | solution.py:15
  339.6 11.2 %collective-permute-start = (bf16[10,64,128]{2,1,0:T(8,128)(2,1)}, bf16[10,64,128]{2,1,0:T(8,128)(2,1)S(1)}, u32[]{:S(2)}, u32[]{:S(2)}) collective-permute-start(bf16[10,64,128]{2,1,0:T(8,128)(2,1)} %get-tuple-element.103), channel_id=1, source_target_pairs={{0,8},{8,16},{16,24},{24,32},{32,40},{40,48},{48,56},{56,64},{64,7... | collective-permute-start | bytes 491528 | tf_op jit(solution)/shard_map/while/body/eval_jaxpr/ppermute | solution.py:15
  511.2 24.4 %all-to-all-start = ((bf16[320,32,16]{0,2,1:T(8,128)(2,1)}), bf16[320,32,16]{0,2,1:T(8,128)(2,1)}, u32[]{:S(2)}, u32[]{:S(2)}) async-start(bf16[320,32,16]{0,2,1:T(8,128)(2,1)} %bitcast.63), calls=%async_computation | async-start | bytes 786432 | tf_op jit(solution)/shard_map/all_to_all | solution.py:120
  (17 other events, 1229.7 us)
Sparse Core Ops, SparseCore 0:
  417.6 70.4 reduce-scatter.3
where the time goes:
time: 547 us; the launch traced here: 544 us
  waiting for transfers between devices  324 us (59%)
  starting transfers between devices  71 us (13%)
  other arithmetic  64.7 us (12%)
  local copies, waits for them, and re-layouts  30.2 us (6%)
  blocking collectives  25.5 us (5%)
  matrix products  14.5 us (3%)
  between operations  14.2 us (3%)
    ppermute x31, waiting for transfers between devices, from_behind(): lax.ppermute(value, axis, [(source, source + steps) for source in range(l...  243 us
    unnamed x2, waiting for transfers between devices  68.4 us
    ppermute x31, starting transfers between devices, from_behind(): lax.ppermute(value, axis, [(source, source + steps) for source in range(l...  60.8 us
    add x31, other arithmetic, relay_step(): return (arrived, reach[:, None, None] * arrived + running)  54.5 us
    unnamed x24, local copies, waits for them, and re-layouts  17.5 us
    psum x1, blocking collectives, body(): lax.psum((jnp.sum(out_wide, axis=0), jnp.sum(out_wide * out_wide, axis=0)...  13.1 us
    psum x1, blocking collectives, body(): squares = lax.psum(jnp.sum(gated * gated, axis=-1), 'head')  12.4 us
    all_to_all x1, waiting for transfers between devices, body(): lax.all_to_all(buffer.reshape(local_feat, seq_count, slot_cap), 'seq', sp...  12.4 us
  transfers between devices with their start and end apart: 33, of which 33 were waited for; matrix products, arithmetic and copies ran while one was open for 1% of the time, Pallas kernels for 0%

commit v1 on v0

--- a/solution.py
+++ b/solution.py
@@ -59,13 +59,22 @@
         reaches.append(reach)
         running = block_decay[:, number][:, None, None] * running + block_states[number]
         reach = reach * block_decay[:, number]
-    empty_state = jnp.zeros((heads_here, head_size, state_size), jnp.float32)
-
-    def relay_step(turn, pair):
-        arrived = from_behind(pair[1].astype(jnp.bfloat16), "seq", 1).astype(jnp.float32)
-        return (arrived, reach[:, None, None] * arrived + running)
-
-    incoming, _ = lax.fori_loop(0, lax.axis_size("seq") - 1, relay_step, (empty_state, running))
+    seq_count = lax.axis_size("seq")
+    me = lax.axis_index("seq")
+    log_total = jnp.sum(cum_all[:, :, -1], axis=1)
+    all_states = lax.all_gather(running.astype(jnp.bfloat16), "seq", tiled=False)
+    all_logs = lax.all_gather(log_total, "seq", tiled=False)
+    index = jnp.arange(seq_count)
+    between = (index[:, None] < index[None, :]) & (index[None, :] < me)
+    spans = jnp.sum(jnp.where(between[:, :, None], all_logs[None, :, :], 0.0), axis=1)
+    gains = jnp.where((index < me)[:, None], jnp.exp(spans), 0.0)
+    incoming = jnp.einsum(
+        "jh,jhpn->hpn",
+        gains,
+        all_states.astype(jnp.float32),
+        precision=lax.Precision.HIGHEST,
+        preferred_element_type=jnp.float32,
+    )
     start_states = jnp.stack(starts) + jnp.stack(reaches)[:, :, None, None] * incoming[None]
     carried = jnp.einsum(
         "ctn,chpn->cthp",
@@ -91,7 +100,6 @@
     ).astype(jnp.float32)
     block_out = (resid.astype(jnp.float32) + proj).astype(jnp.bfloat16)
     features = resid.shape[0] * lax.axis_size("head")
-    seq_count = lax.axis_size("seq")
     masked_here = masked_pos.shape[0]
     slot_cap = 2 * masked_here // seq_count
     local_pos = masked_pos % rows_here

time: 547 us -> 233 us (0.43)
  waiting for transfers between devices: 324 us -> 46.2 us
  blocking collectives: 25.5 us -> 98.5 us
  starting transfers between devices: 71 us -> 10.3 us
  other arithmetic: 64.7 us -> 8.21 us
    ppermute x31 -> x0, waiting for transfers between devices: 243 us -> none  [from_behind(): lax.ppermute(value, axis, [(source, source + steps) for source in range(l...]
    unnamed x0 -> x1, blocking collectives: none -> 73 us
    ppermute x31 -> x0, starting transfers between devices: 60.8 us -> none  [from_behind(): lax.ppermute(value, axis, [(source, source + steps) for source in range(l...]
    add x32 -> x0, other arithmetic: 55.3 us -> none  [the longest x31 54.5 us: relay_step(): return (arrived, reach[:, None, None] * arrived + running)]
    unnamed x2 -> x3, waiting for transfers between devices: 68.4 us -> 32.8 us
    dot_general x0 -> x1, matrix products: none -> 7 us  [body(): jnp.einsum('jh,jhpn->hpn', gains, all_states.astype(jnp.float32), precisi...]
    unnamed x24 -> x47, local copies, waits for them, and re-layouts: 17.5 us -> 18.5 us
  transfers between devices with their start and end apart: 33 -> 3, of which waited for: 33 -> 3; matrix products, arithmetic and copies ran while one was open for 1% -> 7% of each run, Pallas kernels for 0% -> 0%
where the time goes in v1:
time: 233 us; the launch traced here: 232 us
  blocking collectives  98.5 us (42%)
  waiting for transfers between devices  46.2 us (20%)
  local copies, waits for them, and re-layouts  34 us (15%)
  matrix products  19.9 us (9%)
  between operations  15 us (6%)
  starting transfers between devices  10.3 us (4%)
  other arithmetic  8.21 us (4%)
    unnamed x1, blocking collectives  73 us
    unnamed x3, waiting for transfers between devices  32.8 us
    unnamed x47, local copies, waits for them, and re-layouts  18.5 us
    psum x1, blocking collectives, body(): lax.psum((jnp.sum(out_wide, axis=0), jnp.sum(out_wide * out_wide, axis=0)...  12.9 us
    psum x1, blocking collectives, body(): squares = lax.psum(jnp.sum(gated * gated, axis=-1), 'head')  12.6 us
    all_to_all x1, waiting for transfers between devices, body(): lax.all_to_all(buffer.reshape(local_feat, seq_count, slot_cap), 'seq', sp...  12.4 us
    all_to_all x1, starting transfers between devices, body(): lax.all_to_all(buffer.reshape(local_feat, seq_count, slot_cap), 'seq', sp...  10.2 us
    dot_general x1, matrix products, body(): jnp.einsum('jh,jhpn->hpn', gains, all_states.astype(jnp.float32), precisi...  7 us
  transfers between devices with their start and end apart: 3, of which 3 were waited for; matrix products, arithmetic and copies ran while one was open for 7% of the time, Pallas kernels for 0%

profile of v1, /device:TPU:32, one launch (start us, length us, event | category | flops | bytes accessed | tf_op | source)
XLA Modules:
  0.0 232.1 jit_solution(14744911185681328026)
XLA Ops:
  11.6 2.2 copy.74
  13.8 2.7 %reshape.143 = bf16[2,256,10,64]{1,0,3,2:T(2,128)(2,1)} reshape(bf16[512,640]{0,1:T(8,128)(2,1)} %copy.74) | data formatting | bytes 1310720 | tf_op jit(solution)/shard_map/reshape | solution.py:38
  17.1 2.2 fusion.21
  20.2 1.3 copy.71
  21.6 1.3 copy.73
  24.4 73.0 %all-reduce.2 = f32[320]{0:T(512)} all-reduce(f32[320]{0:T(512)S(1)} %dynamic-update-slice), channel_id=2, replica_groups=mesh['seq'=32,'head'=8] {'seq'}, use_global_device_ids=true, to_apply=%add.2 | all-reduce | flops 320 | bytes 2560
  98.8 1.3 copy.81
  100.2 2.2 copy.84
  102.8 4.0 %fusion.10 = f32[2,256,10,64]{1,3,2,0:T(8,128)} fusion(f32[10,2,256]{2,0,1:T(8,128)} %copy.73, f32[10,2,256]{2,0,1:T(8,128)} %copy.71, f32[2,256,256]{2,1,0:T(8,128)S(1)} %fusion.47, pred[256,256]{1,0:T(8,128)(4,1)S(1)} %iota_compare_fusion.1, bf16[2,256,10,64]{1,0,3,2:T(2,128)(2,1)} %reshape.143), kind=kOutput, calls=%fused_computation.17 | convolution fusion | flops 175636480 | bytes 2596864 | tf_op jit(solution)/shard_map/hcts,cshp->cthp/dot_general | solution.py:48
  107.8 7.0 %fusion = f32[10,1,64,128]{3,1,2,0:T(1,128)S(1)} fusion(bf16[32,10,64,128]{3,2,1,0:T(8,128)(2,1)} %all-gather.3.cloned.1.call-done, f32[32,10,1,1]{0,1,2,3:T(8,128)S(1)} %select_bitcast_fusion), kind=kOutput, calls=%fused_computation.2 | convolution fusion | flops 31457280 | bytes 5571840 | tf_op jit(solution)/shard_map/jh,jhpn->hpn/dot_general | solution.py:71
  118.5 12.6 %psum.21 = f32[512]{0:T(512)S(1)} all-reduce(f32[512]{0:T(512)S(1)} %multiply_reduce_fusion), channel_id=1, replica_groups=mesh['seq'=32,'head'=8] {'head'}, use_global_device_ids=true, to_apply=%region_5.6 | all-reduce | flops 512 | bytes 4096 | tf_op jit(solution)/shard_map/psum | solution.py:90
  131.2 5.4 %fusion.2 = bf16[2560,512]{0,1:T(8,128)(2,1)} fusion(bf16[640,2560]{1,0:T(8,128)(2,1)S(1)} %copy-done, f32[640]{0:T(1024)S(1)} %copy-done.16, f32[512]{0:T(512)S(1)} %add_rsqrt_fusion.1, f32[512,640]{0,1:T(8,128)} %bitcast.51, bf16[512,640]{0,1:T(8,128)(2,1)} %copy.84), kind=kOutput, calls=%fused_computation.6 | convolution fusion | flops 1681981440 | bytes 7868928 | tf_op jit(solution)/shard_map/kd,tk->dt/dot_general | solution.py:94
  136.6 4.4 %copy.91 = bf16[2560,512]{1,0:T(8,128)(2,1)} copy(bf16[2560,512]{0,1:T(8,128)(2,1)} %fusion.2) | data formatting | bytes 5242880
  141.0 1.9 copy.66
  143.1 32.8 %reduce-scatter.4.cloned.1.call-done = bf16[320,512]{1,0:T(8,128)(2,1)} async-done(((bf16[2560,512]{1,0:T(8,128)(2,1)}), bf16[320,512]{1,0:T(8,128)(2,1)}) %reduce-scatter.4.cloned.1.call-update) | async-done | bytes 327696
  175.9 1.9 copy.92
  177.8 2.0 convert_reduce_fusion
  179.8 12.9 %all-reduce.3 = (f32[512]{0:T(512)S(1)}, f32[512]{0:T(512)S(1)}) all-reduce(f32[512]{0:T(512)S(1)} %get-tuple-element.11, f32[512]{0:T(512)S(1)} %get-tuple-element.10), channel_id=1, replica_groups=mesh['seq'=32,'head'=8] {'head'}, use_global_device_ids=true, to_apply=%region_11.12 | all-reduce | flops 1024 | bytes 8192 | tf_op jit(solution)/shard_map/psum | solution.py:117
  192.7 2.0 fusion.24
  194.6 4.2 %scatter_custom_fusion = bf16[320,512]{0,1:T(8,128)(2,1)} fusion(s32[256]{0:T(256)S(1)} %compare_select_fusion.1, bf16[320,512]{0,1:T(8,128)(2,1)} %fusion.24, s32[1024]{0:T(1024)S(1)} %pad_clamp_fusion, bf16[]{:T(256)} %constant.41.clone.1), kind=kCustom, calls=%fused_computation.55 | custom fusion | bytes 328192 | tf_op jit(solution)/shard_map/scatter | solution.py:126
  198.9 10.2 %all-to-all-start = ((bf16[320,32,16]{0,2,1:T(8,128)(2,1)}), bf16[320,32,16]{0,2,1:T(8,128)(2,1)}, u32[]{:S(2)}, u32[]{:S(2)}) async-start(bf16[320,32,16]{0,2,1:T(8,128)(2,1)} %bitcast.53), calls=%async_computation | async-start | bytes 786432 | tf_op jit(solution)/shard_map/all_to_all | solution.py:128
  209.1 1.9 copy.85
  210.9 12.4 %all-to-all-done = bf16[320,32,16]{0,2,1:T(8,128)(2,1)} async-done(((bf16[320,32,16]{0,2,1:T(8,128)(2,1)}), bf16[320,32,16]{0,2,1:T(8,128)(2,1)}, u32[]{:S(2)}, u32[]{:S(2)}) %all-to-all-start) | async-done | bytes 327712 | tf_op jit(solution)/shard_map/all_to_all | solution.py:128
  223.4 1.9 copy.86
  (84 shorter events, 13.5 us)
Async XLA Ops:
  7.2 124.0 %copy-start = (bf16[640,2560]{1,0:T(8,128)(2,1)S(1)}, bf16[640,2560]{1,0:T(8,128)(2,1)}, u32[]{:S(2)}) copy-start(bf16[640,2560]{1,0:T(8,128)(2,1)} %param.20) | copy-start | bytes 9830404
  7.2 100.6 %all-gather.3.cloned.1.call-start = ((), (), s32[]{:S(2)}) async-start(), calls=%async_computation.2 | async-start | bytes 5406720 | tf_op jit(solution)/shard_map/all_gather | solution.py:65
  9.7 1.9 copy-start.8
  10.9 0.6 copy-start.9
  11.6 4.9 %copy-start.6 = (bf16[512,128]{1,0:T(8,128)(2,1)S(1)}, bf16[512,128]{1,0:T(8,128)(2,1)}, u32[]{:S(2)}) copy-start(bf16[512,128]{1,0:T(8,128)(2,1)} %param.16) | copy-start | bytes 393220
  17.1 5.8 %copy-start.17 = (u32[256]{0:T(256)S(1)}, u32[256]{0:T(256)}, u32[]{:S(2)}) copy-start(u32[256]{0:T(256)} %constant.56) | copy-start | bytes 3076
  19.3 83.3 %copy-start.7 = (bf16[512,128]{1,0:T(8,128)(2,1)S(1)}, bf16[512,128]{1,0:T(8,128)(2,1)}, u32[]{:S(2)}) copy-start(bf16[512,128]{1,0:T(8,128)(2,1)} %param.17) | copy-start | bytes 393220
  20.2 155.7 %reduce-scatter.4.cloned.1.call-start = ((), (), s32[]{:S(2)}) async-start(), calls=%async_computation.3 | async-start | bytes 2949120
  98.8 3.5 %copy-start.12 = (f32[1,10]{1,0:T(1,128)S(1)}, f32[1,10]{1,0:T(1,128)}, u32[]{:S(2)}) copy-start(f32[1,10]{1,0:T(1,128)} %get-tuple-element.23) | copy-start | bytes 124
  98.8 3.6 %copy-start.11 = (f32[32,10]{0,1:T(8,128)S(1)}, f32[32,10]{0,1:T(8,128)}, u32[]{:S(2)}) copy-start(f32[32,10]{0,1:T(8,128)} %copy.80) | copy-start | bytes 3844
  106.8 8.0 %copy-start.10 = (f32[2,256,10]{1,2,0:T(8,128)S(1)}, f32[2,256,10]{1,2,0:T(8,128)}, u32[]{:S(2)}) copy-start(f32[2,256,10]{1,2,0:T(8,128)} %copy.81) | copy-start | bytes 61444
  106.8 8.0 %copy-start.15 = (f32[10]{0:T(128)S(1)}, f32[10]{0:T(128)}, u32[]{:S(2)}) copy-start(f32[10]{0:T(128)} %param.18) | copy-start | bytes 124
  107.8 7.0 %copy-start.2 = (bf16[2,256,10,64]{1,0,3,2:T(2,128)(2,1)S(1)}, bf16[2,256,10,64]{1,0,3,2:T(2,128)(2,1)}, u32[]{:S(2)}) copy-start(bf16[2,256,10,64]{1,0,3,2:T(2,128)(2,1)} %reshape.143) | copy-start | bytes 1966084
  107.8 7.0 %copy-start.4 = (f32[1,10,64,128]{3,2,1,0:T(8,128)S(1)}, f32[1,10,64,128]{3,2,1,0:T(8,128)}, u32[]{:S(2)}) copy-start(f32[1,10,64,128]{3,2,1,0:T(8,128)} %get-tuple-element.16) | copy-start | bytes 983044
  107.8 7.1 %copy-start.5 = (f32[2,256,10,64]{1,3,2,0:T(8,128)S(1)}, f32[2,256,10,64]{1,3,2,0:T(8,128)}, u32[]{:S(2)}) copy-start(f32[2,256,10,64]{1,3,2,0:T(8,128)} %fusion.10) | copy-start | bytes 3932164
  116.8 1.3 copy-start.3
  116.9 1.1 copy-start.1
  117.0 14.2 %copy-start.16 = (f32[640]{0:T(1024)S(1)}, f32[640]{0:T(1024)}, u32[]{:S(2)}) copy-start(f32[640]{0:T(1024)} %param.19) | copy-start | bytes 7684
  141.0 1.9 copy-start.14
  141.0 1.9 copy-start.13
  198.9 24.5 %all-to-all-start = ((bf16[320,32,16]{0,2,1:T(8,128)(2,1)}), bf16[320,32,16]{0,2,1:T(8,128)(2,1)}, u32[]{:S(2)}, u32[]{:S(2)}) async-start(bf16[320,32,16]{0,2,1:T(8,128)(2,1)} %bitcast.53), calls=%async_computation | async-start | bytes 786432 | tf_op jit(solution)/shard_map/all_to_all | solution.py:128
Sparse Core Ops, SparseCore 0:
  20.3 87.4 all-gather.2
  141.1 34.7 reduce-scatter.3

commit v2 on v1

--- a/solution.py
+++ b/solution.py
@@ -62,8 +62,25 @@
     seq_count = lax.axis_size("seq")
     me = lax.axis_index("seq")
     log_total = jnp.sum(cum_all[:, :, -1], axis=1)
-    all_states = lax.all_gather(running.astype(jnp.bfloat16), "seq", tiled=False)
-    all_logs = lax.all_gather(log_total, "seq", tiled=False)
+    high = lax.reduce_precision(log_total, exponent_bits=8, mantissa_bits=7)
+    rest = log_total - high
+    middle = lax.reduce_precision(rest, exponent_bits=8, mantissa_bits=7)
+    low = rest - middle
+    spare = jnp.zeros((16, state_size), jnp.float32)
+    spare = spare.at[0:3, 0:heads_here].set(jnp.stack([high, middle, low]))
+    slab = jnp.concatenate(
+        [running.reshape(heads_here * head_size, state_size), spare], axis=0
+    ).astype(jnp.bfloat16)
+    gathered = lax.all_gather(slab, "seq", tiled=False)
+    all_states = gathered[:, : heads_here * head_size].reshape(
+        seq_count, heads_here, head_size, state_size
+    )
+    all_logs = jnp.sum(
+        gathered[:, heads_here * head_size : heads_here * head_size + 3, :heads_here].astype(
+            jnp.float32
+        ),
+        axis=1,
+    )
     index = jnp.arange(seq_count)
     between = (index[:, None] < index[None, :]) & (index[None, :] < me)
     spans = jnp.sum(jnp.where(between[:, :, None], all_logs[None, :, :], 0.0), axis=1)

time: 233 us -> 234 us (level)
  waiting for transfers between devices: 46.2 us -> 120 us
  blocking collectives: 98.5 us -> 25.6 us
  matrix products: 19.9 us -> 17.3 us
  other arithmetic: 8.21 us -> 10.7 us
    all_gather x1, waiting for transfers between devices: 0.99 us -> 77.1 us  [body(): gathered = lax.all_gather(slab, 'seq', tiled=False)]
    unnamed x1 -> x0, blocking collectives: 73 us -> none
    dot_general x1, matrix products: 7 us -> 4.37 us  [body(): jnp.einsum('jh,jhpn->hpn', gains, all_states.astype(jnp.float32), precisi...]
    unnamed x47 -> x38, local copies, waits for them, and re-layouts: 18.5 us -> 17.6 us
  transfers between devices with their start and end apart: 3 -> 3, of which waited for: 3 -> 3; matrix products, arithmetic and copies ran while one was open for 7% -> 6% of each run, Pallas kernels for 0% -> 0%
where the time goes in v2:
time: 234 us; the launch traced here: 233 us
  waiting for transfers between devices  120 us (51%)
  local copies, waits for them, and re-layouts  34.5 us (15%)
  blocking collectives  25.6 us (11%)
  matrix products  17.3 us (7%)
  between operations  14.4 us (6%)
  other arithmetic  10.7 us (5%)
  starting transfers between devices  10.4 us (4%)
    all_gather x1, waiting for transfers between devices, body(): gathered = lax.all_gather(slab, 'seq', tiled=False)  77.1 us
    unnamed x3, waiting for transfers between devices  30.6 us
    unnamed x38, local copies, waits for them, and re-layouts  17.6 us
    psum x1, blocking collectives, body(): lax.psum((jnp.sum(out_wide, axis=0), jnp.sum(out_wide * out_wide, axis=0)...  12.9 us
    psum x1, blocking collectives, body(): squares = lax.psum(jnp.sum(gated * gated, axis=-1), 'head')  12.6 us
    all_to_all x1, waiting for transfers between devices, body(): lax.all_to_all(buffer.reshape(local_feat, seq_count, slot_cap), 'seq', sp...  12.4 us
    all_to_all x1, starting transfers between devices, body(): lax.all_to_all(buffer.reshape(local_feat, seq_count, slot_cap), 'seq', sp...  10.1 us
    dot_general x1, matrix products, body(): jnp.einsum('kd,tk->dt', w_out, hidden, preferred_element_type=jnp.float32)  5.37 us
  transfers between devices with their start and end apart: 3, of which 3 were waited for; matrix products, arithmetic and copies ran while one was open for 6% of the time, Pallas kernels for 0%

profile of v2, /device:TPU:32, one launch (start us, length us, event | category | flops | bytes accessed | tf_op | source)
XLA Modules:
  0.0 232.9 jit_solution(15210052519273104533)
XLA Ops:
  11.6 2.2 copy.94
  13.8 2.7 %reshape.278 = bf16[2,256,10,64]{1,0,3,2:T(2,128)(2,1)} reshape(bf16[512,640]{0,1:T(8,128)(2,1)} %copy.94) | data formatting | bytes 1310720 | tf_op jit(solution)/shard_map/reshape | solution.py:38
  16.5 2.2 fusion.21
  20.0 1.3 fusion.34
  22.3 1.3 copy.91
  26.3 2.1 copy.104
  28.8 4.0 %fusion.10 = f32[2,256,10,64]{1,3,2,0:T(8,128)} fusion(f32[10,2,256]{2,0,1:T(8,128)} %copy.93, f32[10,2,256]{2,0,1:T(8,128)} %copy.91, f32[2,256,256]{2,1,0:T(8,128)S(1)} %fusion.52, pred[256,256]{1,0:T(8,128)(4,1)S(1)} %iota_compare_fusion.2, bf16[2,256,10,64]{1,0,3,2:T(2,128)(2,1)} %reshape.278), kind=kOutput, calls=%fused_computation.17 | convolution fusion | flops 175636480 | bytes 2596864 | tf_op jit(solution)/shard_map/hcts,cshp->cthp/dot_general | solution.py:48
  32.7 77.1 %all-gather.2.cloned.1.call-done = bf16[32,656,128]{2,1,0:T(8,128)(2,1)} async-done(((bf16[1,656,128]{2,1,0:T(8,128)(2,1)}), bf16[32,656,128]{2,1,0:T(8,128)(2,1)}) %all-gather.2.cloned.1.call-update) | async-done | bytes 5373968 | tf_op jit(solution)/shard_map/all_gather | solution.py:74
  111.0 2.5 %slice-done = bf16[32,640,128]{2,1,0:T(8,128)(2,1)S(1)} async-done(((bf16[32,656,128]{2,1,0:T(8,128)(2,1)}), bf16[32,640,128]{2,1,0:T(8,128)(2,1)S(1)}, s32[]{:S(2)}) %slice-start) | async-done | bytes 5242904 | tf_op jit(solution)/shard_map/slice | solution.py:75
  113.5 4.4 %fusion = f32[10,1,64,128]{3,1,2,0:T(1,128)S(1)} fusion(bf16[32,10,64,128]{3,2,1,0:T(8,128)(2,1)S(1)} %bitcast.70, f32[32,10,1,1]{0,1,2,3:T(8,128)S(1)} %select_bitcast_fusion), kind=kOutput, calls=%fused_computation.2 | convolution fusion | flops 31457280 | bytes 5571840 | tf_op jit(solution)/shard_map/jh,jhpn->hpn/dot_general | solution.py:88
  121.6 12.6 %psum.21 = f32[512]{0:T(512)S(1)} all-reduce(f32[512]{0:T(512)S(1)} %multiply_reduce_fusion), channel_id=1, replica_groups=mesh['seq'=32,'head'=8] {'head'}, use_global_device_ids=true, to_apply=%region_6.7 | all-reduce | flops 512 | bytes 4096 | tf_op jit(solution)/shard_map/psum | solution.py:107
  134.2 5.4 %fusion.2 = bf16[2560,512]{0,1:T(8,128)(2,1)} fusion(bf16[640,2560]{1,0:T(8,128)(2,1)S(1)} %copy-done, f32[640]{0:T(1024)S(1)} %copy-done.14, f32[512]{0:T(512)S(1)} %add_rsqrt_fusion.1, f32[512,640]{0,1:T(8,128)} %bitcast.72, bf16[512,640]{0,1:T(8,128)(2,1)} %copy.104), kind=kOutput, calls=%fused_computation.6 | convolution fusion | flops 1681981440 | bytes 7868928 | tf_op jit(solution)/shard_map/kd,tk->dt/dot_general | solution.py:111
  139.6 4.4 %copy.111 = bf16[2560,512]{1,0:T(8,128)(2,1)} copy(bf16[2560,512]{0,1:T(8,128)(2,1)} %fusion.2) | data formatting | bytes 5242880
  144.0 1.9 copy.86
  146.2 30.6 %reduce-scatter.4.cloned.1.call-done = bf16[320,512]{1,0:T(8,128)(2,1)} async-done(((bf16[2560,512]{1,0:T(8,128)(2,1)}), bf16[320,512]{1,0:T(8,128)(2,1)}) %reduce-scatter.4.cloned.1.call-update) | async-done | bytes 327696
  176.7 1.9 copy.112
  178.6 2.0 convert_reduce_fusion
  180.6 12.9 %all-reduce.3 = (f32[512]{0:T(512)S(1)}, f32[512]{0:T(512)S(1)}) all-reduce(f32[512]{0:T(512)S(1)} %get-tuple-element.25, f32[512]{0:T(512)S(1)} %get-tuple-element.24), channel_id=1, replica_groups=mesh['seq'=32,'head'=8] {'head'}, use_global_device_ids=true, to_apply=%region_12.13 | all-reduce | flops 1024 | bytes 8192 | tf_op jit(solution)/shard_map/psum | solution.py:134
  193.5 2.0 fusion.24
  195.5 4.2 %scatter_custom_fusion = bf16[320,512]{0,1:T(8,128)(2,1)} fusion(s32[256]{0:T(256)S(1)} %compare_select_fusion.1, bf16[320,512]{0,1:T(8,128)(2,1)} %fusion.24, s32[1024]{0:T(1024)S(1)} %pad_clamp_fusion, bf16[]{:T(256)} %constant.67.clone.1), kind=kCustom, calls=%fused_computation.58 | custom fusion | bytes 328192 | tf_op jit(solution)/shard_map/scatter | solution.py:143
  199.7 10.1 %all-to-all-start = ((bf16[320,32,16]{0,2,1:T(8,128)(2,1)}), bf16[320,32,16]{0,2,1:T(8,128)(2,1)}, u32[]{:S(2)}, u32[]{:S(2)}) async-start(bf16[320,32,16]{0,2,1:T(8,128)(2,1)} %bitcast.74), calls=%async_computation | async-start | bytes 786432 | tf_op jit(solution)/shard_map/all_to_all | solution.py:145
  209.9 1.9 copy.105
  211.8 12.4 %all-to-all-done = bf16[320,32,16]{0,2,1:T(8,128)(2,1)} async-done(((bf16[320,32,16]{0,2,1:T(8,128)(2,1)}), bf16[320,32,16]{0,2,1:T(8,128)(2,1)}, u32[]{:S(2)}, u32[]{:S(2)}) %all-to-all-start) | async-done | bytes 327712 | tf_op jit(solution)/shard_map/all_to_all | solution.py:145
  224.1 1.9 copy.106
  (84 shorter events, 14.6 us)
Async XLA Ops:
  7.2 127.1 %copy-start = (bf16[640,2560]{1,0:T(8,128)(2,1)S(1)}, bf16[640,2560]{1,0:T(8,128)(2,1)}, u32[]{:S(2)}) copy-start(bf16[640,2560]{1,0:T(8,128)(2,1)} %param.22) | copy-start | bytes 9830404
  7.2 102.7 %all-gather.2.cloned.1.call-start = ((), (), s32[]{:S(2)}) async-start(), calls=%async_computation.2 | async-start | bytes 5541888 | tf_op jit(solution)/shard_map/all_gather | solution.py:74
  9.7 1.9 copy-start.8
  10.9 0.6 copy-start.9
  11.6 4.9 %copy-start.6 = (bf16[512,128]{1,0:T(8,128)(2,1)S(1)}, bf16[512,128]{1,0:T(8,128)(2,1)}, u32[]{:S(2)}) copy-start(bf16[512,128]{1,0:T(8,128)(2,1)} %param.18) | copy-start | bytes 393220
  20.0 8.5 %copy-start.7 = (bf16[512,128]{1,0:T(8,128)(2,1)S(1)}, bf16[512,128]{1,0:T(8,128)(2,1)}, u32[]{:S(2)}) copy-start(bf16[512,128]{1,0:T(8,128)(2,1)} %param.19) | copy-start | bytes 393220
  22.1 154.7 %reduce-scatter.4.cloned.1.call-start = ((), (), s32[]{:S(2)}) async-start(), calls=%async_computation.3 | async-start | bytes 2949120
  111.0 2.5 %slice-start = ((bf16[32,656,128]{2,1,0:T(8,128)(2,1)}), bf16[32,640,128]{2,1,0:T(8,128)(2,1)S(1)}, s32[]{:S(2)}) async-start(bf16[32,656,128]{2,1,0:T(8,128)(2,1)} %all-gather.2.cloned.1.call-done), calls=%async_computation.4 | async-start | bytes 10485760 | tf_op jit(solution)/shard_map/slice | solution.py:75
  113.5 4.4 %copy-start.2 = (bf16[2,256,10,64]{1,0,3,2:T(2,128)(2,1)S(1)}, bf16[2,256,10,64]{1,0,3,2:T(2,128)(2,1)}, u32[]{:S(2)}) copy-start(bf16[2,256,10,64]{1,0,3,2:T(2,128)(2,1)} %reshape.278) | copy-start | bytes 1966084
  113.5 4.4 %copy-start.4 = (f32[1,10,64,128]{3,2,1,0:T(8,128)S(1)}, f32[1,10,64,128]{3,2,1,0:T(8,128)}, u32[]{:S(2)}) copy-start(f32[1,10,64,128]{3,2,1,0:T(8,128)} %get-tuple-element.30) | copy-start | bytes 983044
  113.5 4.4 %copy-start.5 = (f32[2,256,10,64]{1,3,2,0:T(8,128)S(1)}, f32[2,256,10,64]{1,3,2,0:T(8,128)}, u32[]{:S(2)}) copy-start(f32[2,256,10,64]{1,3,2,0:T(8,128)} %fusion.10) | copy-start | bytes 3932164
  113.5 4.4 %copy-start.10 = (f32[2,256,10]{1,2,0:T(8,128)S(1)}, f32[2,256,10]{1,2,0:T(8,128)}, u32[]{:S(2)}) copy-start(f32[2,256,10]{1,2,0:T(8,128)} %copy.101) | copy-start | bytes 61444
  113.5 4.4 %copy-start.13 = (f32[10]{0:T(128)S(1)}, f32[10]{0:T(128)}, u32[]{:S(2)}) copy-start(f32[10]{0:T(128)} %param.20) | copy-start | bytes 124
  119.9 1.3 copy-start.3
  120.0 1.1 copy-start.1
  120.0 14.2 %copy-start.14 = (f32[640]{0:T(1024)S(1)}, f32[640]{0:T(1024)}, u32[]{:S(2)}) copy-start(f32[640]{0:T(1024)} %param.21) | copy-start | bytes 7684
  144.0 1.9 copy-start.12
  144.0 1.9 copy-start.11
  199.7 24.4 %all-to-all-start = ((bf16[320,32,16]{0,2,1:T(8,128)(2,1)}), bf16[320,32,16]{0,2,1:T(8,128)(2,1)}, u32[]{:S(2)}, u32[]{:S(2)}) async-start(bf16[320,32,16]{0,2,1:T(8,128)(2,1)} %bitcast.74), calls=%async_computation | async-start | bytes 786432 | tf_op jit(solution)/shard_map/all_to_all | solution.py:145
Sparse Core Ops, SparseCore 0:
  22.2 87.5 all-gather.1
  144.1 32.5 reduce-scatter.3

commit v3 on v0

--- a/solution.py
+++ b/solution.py
@@ -59,13 +59,33 @@
         reaches.append(reach)
         running = block_decay[:, number][:, None, None] * running + block_states[number]
         reach = reach * block_decay[:, number]
-    empty_state = jnp.zeros((heads_here, head_size, state_size), jnp.float32)
+    seq_count = lax.axis_size("seq")
+    log_total = jnp.sum(cum_all[:, :, -1], axis=1)
+    rows = heads_here * head_size
 
-    def relay_step(turn, pair):
-        arrived = from_behind(pair[1].astype(jnp.bfloat16), "seq", 1).astype(jnp.float32)
-        return (arrived, reach[:, None, None] * arrived + running)
+    def pack(logs, state):
+        high = lax.reduce_precision(logs, exponent_bits=8, mantissa_bits=7)
+        rest = logs - high
+        middle = lax.reduce_precision(rest, exponent_bits=8, mantissa_bits=7)
+        spare = jnp.zeros((16, state_size), jnp.float32)
+        spare = spare.at[0:3, 0:heads_here].set(jnp.stack([high, middle, rest - middle]))
+        return jnp.concatenate([state.reshape(rows, state_size), spare], axis=0).astype(
+            jnp.bfloat16
+        )
 
-    incoming, _ = lax.fori_loop(0, lax.axis_size("seq") - 1, relay_step, (empty_state, running))
+    def unpack(slab):
+        wide = slab.astype(jnp.float32)
+        logs = jnp.sum(wide[rows : rows + 3, :heads_here], axis=0)
+        return logs, wide[:rows].reshape(heads_here, head_size, state_size)
+
+    logs, state = unpack(from_behind(pack(log_total, running), "seq", 1))
+    distance = 1
+    while distance < seq_count:
+        earlier_logs, earlier_state = unpack(from_behind(pack(logs, state), "seq", distance))
+        state = jnp.exp(logs)[:, None, None] * earlier_state + state
+        logs = logs + earlier_logs
+        distance *= 2
+    incoming = state
     start_states = jnp.stack(starts) + jnp.stack(reaches)[:, :, None, None] * incoming[None]
     carried = jnp.einsum(
         "ctn,chpn->cthp",
@@ -91,7 +111,6 @@
     ).astype(jnp.float32)
     block_out = (resid.astype(jnp.float32) + proj).astype(jnp.bfloat16)
     features = resid.shape[0] * lax.axis_size("head")
-    seq_count = lax.axis_size("seq")
     masked_here = masked_pos.shape[0]
     slot_cap = 2 * masked_here // seq_count
     local_pos = masked_pos % rows_here

time: 547 us -> 218 us (0.40)
  waiting for transfers between devices: 324 us -> 72.7 us
  other arithmetic: 64.7 us -> 18.7 us
  starting transfers between devices: 71 us -> 34 us
  local copies, waits for them, and re-layouts: 30.2 us -> 37.7 us
    ppermute x31 -> x6, waiting for transfers between devices: 243 us -> 26 us  [from_behind(): lax.ppermute(value, axis, [(source, source + steps) for source in range(l...]
    add x32 -> x1, other arithmetic: 55.3 us -> 0.2 us  [body(): state = jnp.exp(logs)[:, None, None] * earlier_state + state]
    ppermute x31 -> x6, starting transfers between devices: 60.8 us -> 23.9 us  [from_behind(): lax.ppermute(value, axis, [(source, source + steps) for source in range(l...]
    unnamed x2, waiting for transfers between devices: 68.4 us -> 34.4 us
    another operation x4 -> x24, other arithmetic: 1.27 us -> 7.97 us
    unnamed x24 -> x74, local copies, waits for them, and re-layouts: 17.5 us -> 21 us
  transfers between devices with their start and end apart: 33 -> 8, of which waited for: 33 -> 7; matrix products, arithmetic and copies ran while one was open for 1% -> 8% of each run, Pallas kernels for 0% -> 0%
where the time goes in v3:
time: 218 us; the launch traced here: 217 us
  waiting for transfers between devices  72.7 us (33%)
  local copies, waits for them, and re-layouts  37.7 us (17%)
  starting transfers between devices  34 us (16%)
  blocking collectives  25.6 us (12%)
  other arithmetic  18.7 us (9%)
  between operations  14.7 us (7%)
  matrix products  13.7 us (6%)
    unnamed x2, waiting for transfers between devices  34.4 us
    ppermute x6, waiting for transfers between devices, from_behind(): lax.ppermute(value, axis, [(source, source + steps) for source in range(l...  26 us
    ppermute x6, starting transfers between devices, from_behind(): lax.ppermute(value, axis, [(source, source + steps) for source in range(l...  23.9 us
    unnamed x74, local copies, waits for them, and re-layouts  21 us
    psum x1, blocking collectives, body(): lax.psum((jnp.sum(out_wide, axis=0), jnp.sum(out_wide * out_wide, axis=0)...  13 us
    psum x1, blocking collectives, body(): squares = lax.psum(jnp.sum(gated * gated, axis=-1), 'head')  12.6 us
    all_to_all x1, waiting for transfers between devices, body(): lax.all_to_all(buffer.reshape(local_feat, seq_count, slot_cap), 'seq', sp...  12.4 us
    all_to_all x1, starting transfers between devices, body(): lax.all_to_all(buffer.reshape(local_feat, seq_count, slot_cap), 'seq', sp...  10.1 us
  transfers between devices with their start and end apart: 8, of which 7 were waited for; matrix products, arithmetic and copies ran while one was open for 8% of the time, Pallas kernels for 0%

profile of v3, /device:TPU:32, one launch (start us, length us, event | category | flops | bytes accessed | tf_op | source)
XLA Modules:
  0.0 217.1 jit_solution(15405289258268676743)
XLA Ops:
  11.1 2.2 %copy.54 = bf16[512,640]{0,1:T(8,128)(2,1)} copy(bf16[512,640]{1,0:T(8,128)(2,1)} %param.24) | data formatting | bytes 1310720 | tf_op args[0]
  13.3 2.7 %reshape.657 = bf16[2,256,10,64]{1,0,3,2:T(2,128)(2,1)} reshape(bf16[512,640]{0,1:T(8,128)(2,1)} %copy.54) | data formatting | bytes 1310720 | tf_op jit(solution)/shard_map/reshape | solution.py:38
  16.5 2.2 %fusion.19 = f32[2,10,64,128]{3,2,1,0:T(8,128)S(1)} fusion(f32[2,256,128]{2,1,0:T(8,128)S(1)} %convert_element_type.78, f32[10,2,256]{2,0,1:T(8,128)S(1)} %copy.58, bf16[2,256,10,64]{1,0,3,2:T(2,128)(2,1)} %reshape.657), kind=kOutput, calls=%fused_computation.29 | convolution fusion | flops 85196800 | bytes 1593344 | tf_op jit(solution)/shard_map/hcsn,cshp->chpn/dot_general | solution.py:51
  21.3 3.5 %collective-permute-start = (bf16[656,128]{1,0:T(8,128)(2,1)S(1)}, bf16[656,128]{1,0:T(8,128)(2,1)S(1)}, u32[]{:S(2)}, u32[]{:S(2)}) collective-permute-start(bf16[656,128]{1,0:T(8,128)(2,1)S(1)} %pad_maximum_fusion), channel_id=1, source_target_pairs={{0,8},{8,16},{16,24},{24,32},{32,40},{40,48},{48,56},{56,64},{64,7... | collective-permute-start | bytes 503816 | tf_op jit(solution)/shard_map/ppermute | solution.py:15
  24.8 6.5 %collective-permute-done = bf16[656,128]{1,0:T(8,128)(2,1)S(1)} collective-permute-done((bf16[656,128]{1,0:T(8,128)(2,1)S(1)}, bf16[656,128]{1,0:T(8,128)(2,1)S(1)}, u32[]{:S(2)}, u32[]{:S(2)}) %collective-permute-start) | collective-permute-done | bytes 167968 | tf_op jit(solution)/shard_map/ppermute | solution.py:15
  34.1 7.4 %collective-permute-done.1 = bf16[656,128]{1,0:T(8,128)(2,1)S(1)} collective-permute-done((bf16[656,128]{1,0:T(8,128)(2,1)S(1)}, bf16[656,128]{1,0:T(8,128)(2,1)S(1)}, u32[]{:S(2)}, u32[]{:S(2)}) %collective-permute-start.1) | collective-permute-done | bytes 167968 | tf_op jit(solution)/shard_map/ppermute | solution.py:15
  47.1 7.9 %collective-permute-done.2 = bf16[656,128]{1,0:T(8,128)(2,1)} collective-permute-done((bf16[656,128]{1,0:T(8,128)(2,1)}, bf16[656,128]{1,0:T(8,128)(2,1)}, u32[]{:S(2)}, u32[]{:S(2)}) %collective-permute-start.2) | collective-permute-done | bytes 167968 | tf_op jit(solution)/shard_map/ppermute | solution.py:15
  56.0 2.0 fusion.102
  58.1 3.8 %collective-permute-start.3 = (bf16[656,128]{1,0:T(8,128)(2,1)S(1)}, bf16[656,128]{1,0:T(8,128)(2,1)S(1)}, u32[]{:S(2)}, u32[]{:S(2)}) collective-permute-start(bf16[656,128]{1,0:T(8,128)(2,1)S(1)} %pad_maximum_fusion.3), channel_id=1, source_target_pairs={{0,32},{8,40},{16,48},{24,56},{32,64},{40,72},{48,80},{56,88},{64,... | collective-permute-start | bytes 503816 | tf_op jit(solution)/shard_map/ppermute | solution.py:15
  69.3 10.1 %collective-permute-start.4 = (bf16[656,128]{1,0:T(8,128)(2,1)}, bf16[656,128]{1,0:T(8,128)(2,1)}, u32[]{:S(2)}, u32[]{:S(2)}) collective-permute-start(bf16[656,128]{1,0:T(8,128)(2,1)} %pad_maximum_fusion.4), channel_id=1, source_target_pairs={{0,64},{8,72},{16,80},{24,88},{32,96},{40,104},{48,112},{56,120},{... | collective-permute-start | bytes 503816 | tf_op jit(solution)/shard_map/ppermute | solution.py:15
  79.4 4.0 %fusion.8 = f32[2,256,10,64]{1,3,2,0:T(8,128)} fusion(f32[10,2,256]{2,0,1:T(8,128)} %copy.53, f32[10,2,256]{2,0,1:T(8,128)S(1)} %copy.51, f32[2,256,256]{2,1,0:T(8,128)} %fusion.104, pred[256,256]{1,0:T(8,128)(4,1)} %iota_compare_fusion.1, bf16[2,256,10,64]{1,0,3,2:T(2,128)(2,1)} %reshape.657), kind=kOutput, calls=%fused_computation.15 | convolution fusion | flops 175636480 | bytes 2596864 | tf_op jit(solution)/shard_map/hcts,cshp->cthp/dot_general | solution.py:48
  83.5 2.2 %copy.63 = bf16[512,640]{0,1:T(8,128)(2,1)} copy(bf16[512,640]{1,0:T(8,128)(2,1)} %param.25) | data formatting | bytes 1310720 | tf_op args[1]
  91.4 2.6 %collective-permute-start.5 = (bf16[656,128]{1,0:T(8,128)(2,1)S(1)}, bf16[656,128]{1,0:T(8,128)(2,1)S(1)}, u32[]{:S(2)}, u32[]{:S(2)}) collective-permute-start(bf16[656,128]{1,0:T(8,128)(2,1)S(1)} %pad_maximum_fusion.5), channel_id=1, source_target_pairs={{0,128},{8,136},{16,144},{24,152},{32,160},{40,168},{48,176},{56,1... | collective-permute-start | bytes 503816 | tf_op jit(solution)/shard_map/ppermute | solution.py:15
  95.1 3.0 %collective-permute-done.5 = bf16[656,128]{1,0:T(8,128)(2,1)S(1)} collective-permute-done((bf16[656,128]{1,0:T(8,128)(2,1)S(1)}, bf16[656,128]{1,0:T(8,128)(2,1)S(1)}, u32[]{:S(2)}, u32[]{:S(2)}) %collective-permute-start.5) | collective-permute-done | bytes 167968 | tf_op jit(solution)/shard_map/ppermute | solution.py:15
  102.0 12.6 %psum.21 = f32[512]{0:T(512)S(1)} all-reduce(f32[512]{0:T(512)S(1)} %multiply_reduce_fusion), channel_id=1, replica_groups=mesh['seq'=32,'head'=8] {'head'}, use_global_device_ids=true, to_apply=%region_9.10 | all-reduce | flops 512 | bytes 4096 | tf_op jit(solution)/shard_map/psum | solution.py:101
  114.6 5.4 %fusion = bf16[2560,512]{0,1:T(8,128)(2,1)} fusion(bf16[640,2560]{1,0:T(8,128)(2,1)S(1)} %copy-done, f32[640]{0:T(1024)S(1)} %copy-done.32, f32[512]{0:T(512)S(1)} %add_rsqrt_fusion.1, f32[512,640]{0,1:T(8,128)} %bitcast.96, bf16[512,640]{0,1:T(8,128)(2,1)} %copy.63), kind=kOutput, calls=%fused_computation.4 | convolution fusion | flops 1681981440 | bytes 7868928 | tf_op jit(solution)/shard_map/kd,tk->dt/dot_general | solution.py:105
  120.0 4.4 %copy.67 = bf16[2560,512]{1,0:T(8,128)(2,1)} copy(bf16[2560,512]{0,1:T(8,128)(2,1)} %fusion) | data formatting | bytes 5242880
  126.6 34.4 %reduce-scatter.4.cloned.1.call-done = bf16[320,512]{1,0:T(8,128)(2,1)} async-done(((bf16[2560,512]{1,0:T(8,128)(2,1)}), bf16[320,512]{1,0:T(8,128)(2,1)}) %reduce-scatter.4.cloned.1.call-update) | async-done | bytes 327696
  162.8 2.0 convert_reduce_fusion
  164.8 13.0 %all-reduce.8 = (f32[512]{0:T(512)S(1)}, f32[512]{0:T(512)S(1)}) all-reduce(f32[512]{0:T(512)S(1)} %get-tuple-element.81, f32[512]{0:T(512)S(1)} %get-tuple-element.80), channel_id=1, replica_groups=mesh['seq'=32,'head'=8] {'head'}, use_global_device_ids=true, to_apply=%region_15.16 | all-reduce | flops 1024 | bytes 8192 | tf_op jit(solution)/shard_map/psum | solution.py:128
  177.8 2.0 fusion.22
  179.8 4.2 %scatter_custom_fusion = bf16[320,512]{0,1:T(8,128)(2,1)} fusion(s32[256]{0:T(256)S(1)} %compare_select_fusion.1, bf16[320,512]{0,1:T(8,128)(2,1)} %fusion.22, s32[1024]{0:T(1024)S(1)} %pad_clamp_fusion, bf16[]{:T(256)} %constant.150.clone.1), kind=kCustom, calls=%fused_computation.60 | custom fusion | bytes 328192 | tf_op jit(solution)/shard_map/scatter | solution.py:137
  184.0 10.1 %all-to-all-start = ((bf16[320,32,16]{0,2,1:T(8,128)(2,1)}), bf16[320,32,16]{0,2,1:T(8,128)(2,1)}, u32[]{:S(2)}, u32[]{:S(2)}) async-start(bf16[320,32,16]{0,2,1:T(8,128)(2,1)} %bitcast.98), calls=%async_computation | async-start | bytes 786432 | tf_op jit(solution)/shard_map/all_to_all | solution.py:139
  196.0 12.4 %all-to-all-done = bf16[320,32,16]{0,2,1:T(8,128)(2,1)} async-done(((bf16[320,32,16]{0,2,1:T(8,128)(2,1)}), bf16[320,32,16]{0,2,1:T(8,128)(2,1)}, u32[]{:S(2)}, u32[]{:S(2)}) %all-to-all-start) | async-done | bytes 327712 | tf_op jit(solution)/shard_map/all_to_all | solution.py:139
  (172 shorter events, 41.8 us)
Async XLA Ops:
  7.2 107.5 %copy-start = (bf16[640,2560]{1,0:T(8,128)(2,1)S(1)}, bf16[640,2560]{1,0:T(8,128)(2,1)}, u32[]{:S(2)}) copy-start(bf16[640,2560]{1,0:T(8,128)(2,1)} %param.32) | copy-start | bytes 9830404
  7.2 153.8 %reduce-scatter.4.cloned.1.call-start = ((), (), s32[]{:S(2)}) async-start(), calls=%async_computation.2 | async-start | bytes 2949120
  11.0 4.9 %copy-start.17 = (bf16[512,128]{1,0:T(8,128)(2,1)S(1)}, bf16[512,128]{1,0:T(8,128)(2,1)}, u32[]{:S(2)}) copy-start(bf16[512,128]{1,0:T(8,128)(2,1)} %param.28) | copy-start | bytes 393220
  21.3 10.0 %collective-permute-start = (bf16[656,128]{1,0:T(8,128)(2,1)S(1)}, bf16[656,128]{1,0:T(8,128)(2,1)S(1)}, u32[]{:S(2)}, u32[]{:S(2)}) collective-permute-start(bf16[656,128]{1,0:T(8,128)(2,1)S(1)} %pad_maximum_fusion), channel_id=1, source_target_pairs={{0,8},{8,16},{16,24},{24,32},{32,40},{40,48},{48,56},{56,64},{64,7... | collective-permute-start | bytes 503816 | tf_op jit(solution)/shard_map/ppermute | solution.py:15
  32.2 9.4 %collective-permute-start.1 = (bf16[656,128]{1,0:T(8,128)(2,1)S(1)}, bf16[656,128]{1,0:T(8,128)(2,1)S(1)}, u32[]{:S(2)}, u32[]{:S(2)}) collective-permute-start(bf16[656,128]{1,0:T(8,128)(2,1)S(1)} %pad_maximum_fusion.1), channel_id=1, source_target_pairs={{0,8},{8,16},{16,24},{24,32},{32,40},{40,48},{48,56},{56,64},{64,7... | collective-permute-start | bytes 503816 | tf_op jit(solution)/shard_map/ppermute | solution.py:15
  45.0 10.0 %collective-permute-start.2 = (bf16[656,128]{1,0:T(8,128)(2,1)}, bf16[656,128]{1,0:T(8,128)(2,1)}, u32[]{:S(2)}, u32[]{:S(2)}) collective-permute-start(bf16[656,128]{1,0:T(8,128)(2,1)} %pad_maximum_fusion.2), channel_id=1, source_target_pairs={{0,16},{8,24},{16,32},{24,40},{32,48},{40,56},{48,64},{56,72},{64,... | collective-permute-start | bytes 503816 | tf_op jit(solution)/shard_map/ppermute | solution.py:15
  47.1 14.8 %copy-start.18 = (bf16[512,128]{1,0:T(8,128)(2,1)S(1)}, bf16[512,128]{1,0:T(8,128)(2,1)}, u32[]{:S(2)}) copy-start(bf16[512,128]{1,0:T(8,128)(2,1)} %param.28) | copy-start | bytes 393220
  47.1 14.8 %copy-start.19 = (bf16[512,128]{1,0:T(8,128)(2,1)S(1)}, bf16[512,128]{1,0:T(8,128)(2,1)}, u32[]{:S(2)}) copy-start(bf16[512,128]{1,0:T(8,128)(2,1)} %param.29) | copy-start | bytes 393220
  58.1 7.3 %collective-permute-start.3 = (bf16[656,128]{1,0:T(8,128)(2,1)S(1)}, bf16[656,128]{1,0:T(8,128)(2,1)S(1)}, u32[]{:S(2)}, u32[]{:S(2)}) collective-permute-start(bf16[656,128]{1,0:T(8,128)(2,1)S(1)} %pad_maximum_fusion.3), channel_id=1, source_target_pairs={{0,32},{8,40},{16,48},{24,56},{32,64},{40,72},{48,80},{56,88},{64,... | collective-permute-start | bytes 503816 | tf_op jit(solution)/shard_map/ppermute | solution.py:15
  67.2 16.3 %copy-start.27 = (f32[10]{0:T(128)}, f32[10]{0:T(128)S(1)}, u32[]{:S(2)}) copy-start(f32[10]{0:T(128)S(1)} %exp.60) | copy-start | bytes 124
  69.3 20.7 %collective-permute-start.4 = (bf16[656,128]{1,0:T(8,128)(2,1)}, bf16[656,128]{1,0:T(8,128)(2,1)}, u32[]{:S(2)}, u32[]{:S(2)}) collective-permute-start(bf16[656,128]{1,0:T(8,128)(2,1)} %pad_maximum_fusion.4), channel_id=1, source_target_pairs={{0,64},{8,72},{16,80},{24,88},{32,96},{40,104},{48,112},{56,120},{... | collective-permute-start | bytes 503816 | tf_op jit(solution)/shard_map/ppermute | solution.py:15
  85.7 4.1 %copy-start.23 = (f32[10]{0:T(128)S(1)}, f32[10]{0:T(128)}, u32[]{:S(2)}) copy-start(f32[10]{0:T(128)} %get-tuple-element.85) | copy-start | bytes 124
  86.4 3.5 %copy-start.11 = (bf16[656,128]{1,0:T(8,128)(2,1)S(1)}, bf16[656,128]{1,0:T(8,128)(2,1)}, u32[]{:S(2)}) copy-start(bf16[656,128]{1,0:T(8,128)(2,1)} %copy-done.10) | copy-start | bytes 503812
  90.0 5.0 %copy-start.26 = (f32[10]{0:T(128)S(1)}, f32[10]{0:T(128)}, u32[]{:S(2)}) copy-start(f32[10]{0:T(128)} %copy-done.25) | copy-start | bytes 124
  91.0 7.1 %copy-start.14 = (f32[640,128]{1,0:T(8,128)S(1)}, f32[640,128]{1,0:T(8,128)}, u32[]{:S(2)}) copy-start(f32[640,128]{1,0:T(8,128)} %slice.204) | copy-start | bytes 983044
  91.0 7.1 %copy-start.15 = (f32[640,128]{1,0:T(8,128)S(1)}, f32[640,128]{1,0:T(8,128)}, u32[]{:S(2)}) copy-start(f32[640,128]{1,0:T(8,128)} %slice.206) | copy-start | bytes 983044
  91.0 7.1 %copy-start.16 = (f32[640,128]{1,0:T(8,128)S(1)}, f32[640,128]{1,0:T(8,128)}, u32[]{:S(2)}) copy-start(f32[640,128]{1,0:T(8,128)} %slice.208) | copy-start | bytes 983044
  91.0 7.1 %copy-start.22 = (f32[10]{0:T(128)S(1)}, f32[10]{0:T(128)}, u32[]{:S(2)}) copy-start(f32[10]{0:T(128)} %copy-done.21) | copy-start | bytes 124
  91.0 7.1 %copy-start.28 = (f32[10]{0:T(128)S(1)}, f32[10]{0:T(128)}, u32[]{:S(2)}) copy-start(f32[10]{0:T(128)} %copy-done.27) | copy-start | bytes 124
  91.4 6.7 %collective-permute-start.5 = (bf16[656,128]{1,0:T(8,128)(2,1)S(1)}, bf16[656,128]{1,0:T(8,128)(2,1)S(1)}, u32[]{:S(2)}, u32[]{:S(2)}) collective-permute-start(bf16[656,128]{1,0:T(8,128)(2,1)S(1)} %pad_maximum_fusion.5), channel_id=1, source_target_pairs={{0,128},{8,136},{16,144},{24,152},{32,160},{40,168},{48,176},{56,1... | collective-permute-start | bytes 503816 | tf_op jit(solution)/shard_map/ppermute | solution.py:15
  95.0 3.4 %copy-start.7 = (bf16[2,256,10,64]{1,0,3,2:T(2,128)(2,1)S(1)}, bf16[2,256,10,64]{1,0,3,2:T(2,128)(2,1)}, u32[]{:S(2)}) copy-start(bf16[2,256,10,64]{1,0,3,2:T(2,128)(2,1)} %reshape.657) | copy-start | bytes 1966084
  95.0 3.4 %copy-start.12 = (f32[1,10,64,128]{3,2,1,0:T(8,128)S(1)}, f32[1,10,64,128]{3,2,1,0:T(8,128)}, u32[]{:S(2)}) copy-start(f32[1,10,64,128]{3,2,1,0:T(8,128)} %get-tuple-element.96) | copy-start | bytes 983044
  100.4 14.2 %copy-start.32 = (f32[640]{0:T(1024)S(1)}, f32[640]{0:T(1024)}, u32[]{:S(2)}) copy-start(f32[640]{0:T(1024)} %param.31) | copy-start | bytes 7684
  184.0 24.4 %all-to-all-start = ((bf16[320,32,16]{0,2,1:T(8,128)(2,1)}), bf16[320,32,16]{0,2,1:T(8,128)(2,1)}, u32[]{:S(2)}, u32[]{:S(2)}) async-start(bf16[320,32,16]{0,2,1:T(8,128)(2,1)} %bitcast.98), calls=%async_computation | async-start | bytes 786432 | tf_op jit(solution)/shard_map/all_to_all | solution.py:139
  (17 other events, 25.7 us)
Sparse Core Ops, SparseCore 0:
  124.5 36.3 reduce-scatter.3

commit v4 on v3

--- a/solution.py
+++ b/solution.py
@@ -100,7 +100,7 @@
     gated = mixed * jax.nn.silu(z_gate.astype(jnp.float32))
     squares = lax.psum(jnp.sum(gated * gated, axis=-1), "head")
     mean_sq = squares / (channels * lax.axis_size("head"))
-    hidden = (gated * lax.rsqrt(mean_sq + EPS)[:, None] * norm_weight[None, :]).astype(jnp.bfloat16)
+    hidden = (gated * norm_weight[None, :]).astype(jnp.bfloat16)
     proj = lax.psum_scatter(
         jnp.einsum("kd,tk->dt", w_out, hidden, preferred_element_type=jnp.float32).astype(
             jnp.bfloat16
@@ -109,6 +109,7 @@
         scatter_dimension=0,
         tiled=True,
     ).astype(jnp.float32)
+    proj = proj * lax.rsqrt(mean_sq + EPS)[None, :]
     block_out = (resid.astype(jnp.float32) + proj).astype(jnp.bfloat16)
     features = resid.shape[0] * lax.axis_size("head")
     masked_here = masked_pos.shape[0]

time: 218 us -> 206 us (0.945)
  waiting for transfers between devices: 72.7 us -> 60.5 us
    unnamed x2, waiting for transfers between devices: 34.4 us -> 22.3 us
  transfers between devices with their start and end apart: 8 -> 8, of which waited for: 7 -> 7; matrix products, arithmetic and copies ran while one was open for 8% -> 10% of each run, Pallas kernels for 0% -> 0%
where the time goes in v4:
time: 206 us; the launch traced here: 205 us
  waiting for transfers between devices  60.5 us (29%)
  local copies, waits for them, and re-layouts  37.7 us (18%)
  starting transfers between devices  34.2 us (17%)
  blocking collectives  25.3 us (12%)
  other arithmetic  20.4 us (10%)
  between operations  14.7 us (7%)
  matrix products  12.3 us (6%)
    ppermute x6, waiting for transfers between devices, from_behind(): lax.ppermute(value, axis, [(source, source + steps) for source in range(l...  25.8 us
    ppermute x6, starting transfers between devices, from_behind(): lax.ppermute(value, axis, [(source, source + steps) for source in range(l...  24.1 us
    unnamed x2, waiting for transfers between devices  22.3 us
    unnamed x74, local copies, waits for them, and re-layouts  21 us
    psum x1, blocking collectives, body(): lax.psum((jnp.sum(out_wide, axis=0), jnp.sum(out_wide * out_wide, axis=0)...  12.9 us
    psum x1, blocking collectives, body(): squares = lax.psum(jnp.sum(gated * gated, axis=-1), 'head')  12.4 us
    all_to_all x1, waiting for transfers between devices, body(): lax.all_to_all(buffer.reshape(local_feat, seq_count, slot_cap), 'seq', sp...  12.4 us
    all_to_all x1, starting transfers between devices, body(): lax.all_to_all(buffer.reshape(local_feat, seq_count, slot_cap), 'seq', sp...  10.1 us
  transfers between devices with their start and end apart: 8, of which 7 were waited for; matrix products, arithmetic and copies ran while one was open for 10% of the time, Pallas kernels for 0%

profile of v4, /device:TPU:32, one launch (start us, length us, event | category | flops | bytes accessed | tf_op | source)
XLA Modules:
  0.0 205.1 jit_solution(11342105755686168864)
XLA Ops:
  10.5 2.2 %copy.54 = bf16[512,640]{0,1:T(8,128)(2,1)} copy(bf16[512,640]{1,0:T(8,128)(2,1)} %param.24) | data formatting | bytes 1310720 | tf_op args[0]
  12.7 2.7 %reshape.657 = bf16[2,256,10,64]{1,0,3,2:T(2,128)(2,1)} reshape(bf16[512,640]{0,1:T(8,128)(2,1)} %copy.54) | data formatting | bytes 1310720 | tf_op jit(solution)/shard_map/reshape | solution.py:38
  16.5 2.2 %fusion.19 = f32[2,10,64,128]{3,2,1,0:T(8,128)S(1)} fusion(f32[2,256,128]{2,1,0:T(8,128)S(1)} %convert_element_type.78, f32[10,2,256]{2,0,1:T(8,128)S(1)} %copy.58, bf16[2,256,10,64]{1,0,3,2:T(2,128)(2,1)} %reshape.657), kind=kOutput, calls=%fused_computation.29 | convolution fusion | flops 85196800 | bytes 1593344 | tf_op jit(solution)/shard_map/hcsn,cshp->chpn/dot_general | solution.py:51
  21.4 3.5 %collective-permute-start = (bf16[656,128]{1,0:T(8,128)(2,1)S(1)}, bf16[656,128]{1,0:T(8,128)(2,1)S(1)}, u32[]{:S(2)}, u32[]{:S(2)}) collective-permute-start(bf16[656,128]{1,0:T(8,128)(2,1)S(1)} %pad_maximum_fusion), channel_id=1, source_target_pairs={{0,8},{8,16},{16,24},{24,32},{32,40},{40,48},{48,56},{56,64},{64,7... | collective-permute-start | bytes 503816 | tf_op jit(solution)/shard_map/ppermute | solution.py:15
  24.9 6.5 %collective-permute-done = bf16[656,128]{1,0:T(8,128)(2,1)S(1)} collective-permute-done((bf16[656,128]{1,0:T(8,128)(2,1)S(1)}, bf16[656,128]{1,0:T(8,128)(2,1)S(1)}, u32[]{:S(2)}, u32[]{:S(2)}) %collective-permute-start) | collective-permute-done | bytes 167968 | tf_op jit(solution)/shard_map/ppermute | solution.py:15
  34.2 7.4 %collective-permute-done.1 = bf16[656,128]{1,0:T(8,128)(2,1)S(1)} collective-permute-done((bf16[656,128]{1,0:T(8,128)(2,1)S(1)}, bf16[656,128]{1,0:T(8,128)(2,1)S(1)}, u32[]{:S(2)}, u32[]{:S(2)}) %collective-permute-start.1) | collective-permute-done | bytes 167968 | tf_op jit(solution)/shard_map/ppermute | solution.py:15
  47.1 7.9 %collective-permute-done.2 = bf16[656,128]{1,0:T(8,128)(2,1)} collective-permute-done((bf16[656,128]{1,0:T(8,128)(2,1)}, bf16[656,128]{1,0:T(8,128)(2,1)}, u32[]{:S(2)}, u32[]{:S(2)}) %collective-permute-start.2) | collective-permute-done | bytes 167968 | tf_op jit(solution)/shard_map/ppermute | solution.py:15
  56.0 2.0 fusion.101
  58.1 3.8 %collective-permute-start.3 = (bf16[656,128]{1,0:T(8,128)(2,1)S(1)}, bf16[656,128]{1,0:T(8,128)(2,1)S(1)}, u32[]{:S(2)}, u32[]{:S(2)}) collective-permute-start(bf16[656,128]{1,0:T(8,128)(2,1)S(1)} %pad_maximum_fusion.3), channel_id=1, source_target_pairs={{0,32},{8,40},{16,48},{24,56},{32,64},{40,72},{48,80},{56,88},{64,... | collective-permute-start | bytes 503816 | tf_op jit(solution)/shard_map/ppermute | solution.py:15
  69.4 10.1 %collective-permute-start.4 = (bf16[656,128]{1,0:T(8,128)(2,1)}, bf16[656,128]{1,0:T(8,128)(2,1)}, u32[]{:S(2)}, u32[]{:S(2)}) collective-permute-start(bf16[656,128]{1,0:T(8,128)(2,1)} %pad_maximum_fusion.4), channel_id=1, source_target_pairs={{0,64},{8,72},{16,80},{24,88},{32,96},{40,104},{48,112},{56,120},{... | collective-permute-start | bytes 503816 | tf_op jit(solution)/shard_map/ppermute | solution.py:15
  79.5 4.1 %fusion.8 = f32[2,256,10,64]{1,3,2,0:T(8,128)} fusion(f32[10,2,256]{2,0,1:T(8,128)S(1)} %copy.53, f32[10,2,256]{2,0,1:T(8,128)} %copy.51, f32[2,256,256]{2,1,0:T(8,128)} %fusion.103, pred[256,256]{1,0:T(8,128)(4,1)} %iota_compare_fusion.1, bf16[2,256,10,64]{1,0,3,2:T(2,128)(2,1)} %reshape.657), kind=kOutput, calls=%fused_computation.15 | convolution fusion | flops 175636480 | bytes 2596864 | tf_op jit(solution)/shard_map/hcts,cshp->cthp/dot_general | solution.py:48
  83.6 2.2 %copy.63 = bf16[512,640]{0,1:T(8,128)(2,1)} copy(bf16[512,640]{1,0:T(8,128)(2,1)} %param.25) | data formatting | bytes 1310720 | tf_op args[1]
  91.5 2.8 %collective-permute-start.5 = (bf16[656,128]{1,0:T(8,128)(2,1)S(1)}, bf16[656,128]{1,0:T(8,128)(2,1)S(1)}, u32[]{:S(2)}, u32[]{:S(2)}) collective-permute-start(bf16[656,128]{1,0:T(8,128)(2,1)S(1)} %pad_maximum_fusion.5), channel_id=1, source_target_pairs={{0,128},{8,136},{16,144},{24,152},{32,160},{40,168},{48,176},{56,1... | collective-permute-start | bytes 503816 | tf_op jit(solution)/shard_map/ppermute | solution.py:15
  95.3 2.8 %collective-permute-done.5 = bf16[656,128]{1,0:T(8,128)(2,1)S(1)} collective-permute-done((bf16[656,128]{1,0:T(8,128)(2,1)S(1)}, bf16[656,128]{1,0:T(8,128)(2,1)S(1)}, u32[]{:S(2)}, u32[]{:S(2)}) %collective-permute-start.5) | collective-permute-done | bytes 167968 | tf_op jit(solution)/shard_map/ppermute | solution.py:15
  101.6 3.9 %fusion = bf16[2560,512]{0,1:T(8,128)(2,1)} fusion(bf16[640,2560]{1,0:T(8,128)(2,1)S(1)} %copy-done, f32[640]{0:T(1024)S(1)} %copy-done.32, f32[512,640]{0,1:T(8,128)S(1)} %bitcast.95, bf16[512,640]{0,1:T(8,128)(2,1)S(1)} %copy-done.8), kind=kOutput, calls=%fused_computation.4 | convolution fusion | flops 1681653760 | bytes 7866880 | tf_op jit(solution)/shard_map/kd,tk->dt/dot_general | solution.py:105
  105.6 4.4 %copy.67 = bf16[2560,512]{1,0:T(8,128)(2,1)} copy(bf16[2560,512]{0,1:T(8,128)(2,1)} %fusion) | data formatting | bytes 5242880
  114.1 12.4 %psum.21 = f32[512]{0:T(512)S(1)} all-reduce(f32[512]{0:T(512)S(1)} %multiply_reduce_fusion), channel_id=1, replica_groups=mesh['seq'=32,'head'=8] {'head'}, use_global_device_ids=true, to_apply=%region_10.11 | all-reduce | flops 512 | bytes 4096 | tf_op jit(solution)/shard_map/psum | solution.py:101
  126.5 22.3 %reduce-scatter.4.cloned.1.call-done = bf16[320,512]{1,0:T(8,128)(2,1)} async-done(((bf16[2560,512]{1,0:T(8,128)(2,1)}), bf16[320,512]{1,0:T(8,128)(2,1)}) %reduce-scatter.4.cloned.1.call-update) | async-done | bytes 327696
  150.7 2.1 %convert_reduce_fusion = (f32[512]{0:T(512)S(1)}, f32[512]{0:T(512)S(1)}, bf16[320,512]{0,1:T(8,128)(2,1)}) fusion(f32[512]{0:T(512)S(1)} %add_rsqrt_fusion.1, bf16[320,512]{0,1:T(8,128)(2,1)} %copy.68, bf16[320,512]{0,1:T(8,128)(2,1)} %copy.46), kind=kLoop, calls=%fused_computation.32 | loop fusion | flops 1473536 | bytes 989184 | tf_op jit(solution)/shard_map/reduce_sum | solution.py:129
  152.8 12.9 %all-reduce.8 = (f32[512]{0:T(512)S(1)}, f32[512]{0:T(512)S(1)}) all-reduce(f32[512]{0:T(512)S(1)} %get-tuple-element.81, f32[512]{0:T(512)S(1)} %get-tuple-element.80), channel_id=1, replica_groups=mesh['seq'=32,'head'=8] {'head'}, use_global_device_ids=true, to_apply=%region_15.16 | all-reduce | flops 1024 | bytes 8192 | tf_op jit(solution)/shard_map/psum | solution.py:129
  165.8 2.0 fusion.22
  167.7 4.2 %scatter_custom_fusion = bf16[320,512]{0,1:T(8,128)(2,1)} fusion(s32[256]{0:T(256)S(1)} %compare_select_fusion.1, bf16[320,512]{0,1:T(8,128)(2,1)} %fusion.22, s32[1024]{0:T(1024)S(1)} %pad_clamp_fusion, bf16[]{:T(256)} %constant.150.clone.1), kind=kCustom, calls=%fused_computation.59 | custom fusion | bytes 328192 | tf_op jit(solution)/shard_map/scatter | solution.py:138
  172.0 10.1 %all-to-all-start = ((bf16[320,32,16]{0,2,1:T(8,128)(2,1)}), bf16[320,32,16]{0,2,1:T(8,128)(2,1)}, u32[]{:S(2)}, u32[]{:S(2)}) async-start(bf16[320,32,16]{0,2,1:T(8,128)(2,1)} %bitcast.98), calls=%async_computation | async-start | bytes 786432 | tf_op jit(solution)/shard_map/all_to_all | solution.py:140
  183.9 12.4 %all-to-all-done = bf16[320,32,16]{0,2,1:T(8,128)(2,1)} async-done(((bf16[320,32,16]{0,2,1:T(8,128)(2,1)}), bf16[320,32,16]{0,2,1:T(8,128)(2,1)}, u32[]{:S(2)}, u32[]{:S(2)}) %all-to-all-start) | async-done | bytes 327712 | tf_op jit(solution)/shard_map/all_to_all | solution.py:140
  (172 shorter events, 43.3 us)
Async XLA Ops:
  7.2 94.5 %copy-start = (bf16[640,2560]{1,0:T(8,128)(2,1)S(1)}, bf16[640,2560]{1,0:T(8,128)(2,1)}, u32[]{:S(2)}) copy-start(bf16[640,2560]{1,0:T(8,128)(2,1)} %param.32) | copy-start | bytes 9830404
  7.2 141.6 %reduce-scatter.4.cloned.1.call-start = ((), (), s32[]{:S(2)}) async-start(), calls=%async_computation.2 | async-start | bytes 2949120
  10.5 5.4 %copy-start.17 = (bf16[512,128]{1,0:T(8,128)(2,1)S(1)}, bf16[512,128]{1,0:T(8,128)(2,1)}, u32[]{:S(2)}) copy-start(bf16[512,128]{1,0:T(8,128)(2,1)} %param.28) | copy-start | bytes 393220
  21.4 10.0 %collective-permute-start = (bf16[656,128]{1,0:T(8,128)(2,1)S(1)}, bf16[656,128]{1,0:T(8,128)(2,1)S(1)}, u32[]{:S(2)}, u32[]{:S(2)}) collective-permute-start(bf16[656,128]{1,0:T(8,128)(2,1)S(1)} %pad_maximum_fusion), channel_id=1, source_target_pairs={{0,8},{8,16},{16,24},{24,32},{32,40},{40,48},{48,56},{56,64},{64,7... | collective-permute-start | bytes 503816 | tf_op jit(solution)/shard_map/ppermute | solution.py:15
  32.2 9.4 %collective-permute-start.1 = (bf16[656,128]{1,0:T(8,128)(2,1)S(1)}, bf16[656,128]{1,0:T(8,128)(2,1)S(1)}, u32[]{:S(2)}, u32[]{:S(2)}) collective-permute-start(bf16[656,128]{1,0:T(8,128)(2,1)S(1)} %pad_maximum_fusion.1), channel_id=1, source_target_pairs={{0,8},{8,16},{16,24},{24,32},{32,40},{40,48},{48,56},{56,64},{64,7... | collective-permute-start | bytes 503816 | tf_op jit(solution)/shard_map/ppermute | solution.py:15
  45.0 10.0 %collective-permute-start.2 = (bf16[656,128]{1,0:T(8,128)(2,1)}, bf16[656,128]{1,0:T(8,128)(2,1)}, u32[]{:S(2)}, u32[]{:S(2)}) collective-permute-start(bf16[656,128]{1,0:T(8,128)(2,1)} %pad_maximum_fusion.2), channel_id=1, source_target_pairs={{0,16},{8,24},{16,32},{24,40},{32,48},{40,56},{48,64},{56,72},{64,... | collective-permute-start | bytes 503816 | tf_op jit(solution)/shard_map/ppermute | solution.py:15
  47.1 14.8 %copy-start.18 = (bf16[512,128]{1,0:T(8,128)(2,1)S(1)}, bf16[512,128]{1,0:T(8,128)(2,1)}, u32[]{:S(2)}) copy-start(bf16[512,128]{1,0:T(8,128)(2,1)} %param.28) | copy-start | bytes 393220
  47.1 14.8 %copy-start.19 = (bf16[512,128]{1,0:T(8,128)(2,1)S(1)}, bf16[512,128]{1,0:T(8,128)(2,1)}, u32[]{:S(2)}) copy-start(bf16[512,128]{1,0:T(8,128)(2,1)} %param.29) | copy-start | bytes 393220
  58.1 7.3 %collective-permute-start.3 = (bf16[656,128]{1,0:T(8,128)(2,1)S(1)}, bf16[656,128]{1,0:T(8,128)(2,1)S(1)}, u32[]{:S(2)}, u32[]{:S(2)}) collective-permute-start(bf16[656,128]{1,0:T(8,128)(2,1)S(1)} %pad_maximum_fusion.3), channel_id=1, source_target_pairs={{0,32},{8,40},{16,48},{24,56},{32,64},{40,72},{48,80},{56,88},{64,... | collective-permute-start | bytes 503816 | tf_op jit(solution)/shard_map/ppermute | solution.py:15
  69.4 20.7 %collective-permute-start.4 = (bf16[656,128]{1,0:T(8,128)(2,1)}, bf16[656,128]{1,0:T(8,128)(2,1)}, u32[]{:S(2)}, u32[]{:S(2)}) collective-permute-start(bf16[656,128]{1,0:T(8,128)(2,1)} %pad_maximum_fusion.4), channel_id=1, source_target_pairs={{0,64},{8,72},{16,80},{24,88},{32,96},{40,104},{48,112},{56,120},{... | collective-permute-start | bytes 503816 | tf_op jit(solution)/shard_map/ppermute | solution.py:15
  85.8 4.1 %copy-start.23 = (f32[10]{0:T(128)S(1)}, f32[10]{0:T(128)}, u32[]{:S(2)}) copy-start(f32[10]{0:T(128)} %get-tuple-element.85) | copy-start | bytes 124
  86.5 3.5 %copy-start.11 = (bf16[656,128]{1,0:T(8,128)(2,1)S(1)}, bf16[656,128]{1,0:T(8,128)(2,1)}, u32[]{:S(2)}) copy-start(bf16[656,128]{1,0:T(8,128)(2,1)} %copy-done.10) | copy-start | bytes 503812
  86.5 4.7 %copy-start.26 = (f32[1,10]{1,0:T(1,128)S(1)}, f32[1,10]{1,0:T(1,128)}, u32[]{:S(2)}) copy-start(f32[1,10]{1,0:T(1,128)} %copy-done.25) | copy-start | bytes 124
  90.1 5.2 %copy-start.28 = (f32[10]{0:T(128)S(1)}, f32[10]{0:T(128)}, u32[]{:S(2)}) copy-start(f32[10]{0:T(128)} %copy-done.27) | copy-start | bytes 124
  91.1 7.1 %copy-start.14 = (f32[640,128]{1,0:T(8,128)S(1)}, f32[640,128]{1,0:T(8,128)}, u32[]{:S(2)}) copy-start(f32[640,128]{1,0:T(8,128)} %slice.204) | copy-start | bytes 983044
  91.1 7.1 %copy-start.15 = (f32[640,128]{1,0:T(8,128)S(1)}, f32[640,128]{1,0:T(8,128)}, u32[]{:S(2)}) copy-start(f32[640,128]{1,0:T(8,128)} %slice.206) | copy-start | bytes 983044
  91.1 7.1 %copy-start.16 = (f32[640,128]{1,0:T(8,128)S(1)}, f32[640,128]{1,0:T(8,128)}, u32[]{:S(2)}) copy-start(f32[640,128]{1,0:T(8,128)} %slice.208) | copy-start | bytes 983044
  91.1 7.1 %copy-start.22 = (f32[10]{0:T(128)S(1)}, f32[10]{0:T(128)}, u32[]{:S(2)}) copy-start(f32[10]{0:T(128)} %copy-done.21) | copy-start | bytes 124
  91.5 6.7 %collective-permute-start.5 = (bf16[656,128]{1,0:T(8,128)(2,1)S(1)}, bf16[656,128]{1,0:T(8,128)(2,1)S(1)}, u32[]{:S(2)}, u32[]{:S(2)}) collective-permute-start(bf16[656,128]{1,0:T(8,128)(2,1)S(1)} %pad_maximum_fusion.5), channel_id=1, source_target_pairs={{0,128},{8,136},{16,144},{24,152},{32,160},{40,168},{48,176},{56,1... | collective-permute-start | bytes 503816 | tf_op jit(solution)/shard_map/ppermute | solution.py:15
  95.3 3.2 %copy-start.7 = (bf16[2,256,10,64]{1,0,3,2:T(2,128)(2,1)S(1)}, bf16[2,256,10,64]{1,0,3,2:T(2,128)(2,1)}, u32[]{:S(2)}) copy-start(bf16[2,256,10,64]{1,0,3,2:T(2,128)(2,1)} %reshape.657) | copy-start | bytes 1966084
  95.3 3.2 %copy-start.12 = (f32[1,10,64,128]{3,2,1,0:T(8,128)S(1)}, f32[1,10,64,128]{3,2,1,0:T(8,128)}, u32[]{:S(2)}) copy-start(f32[1,10,64,128]{3,2,1,0:T(8,128)} %get-tuple-element.96) | copy-start | bytes 983044
  95.3 3.2 %copy-start.13 = (f32[2,256,10,64]{1,3,2,0:T(8,128)S(1)}, f32[2,256,10,64]{1,3,2,0:T(8,128)}, u32[]{:S(2)}) copy-start(f32[2,256,10,64]{1,3,2,0:T(8,128)} %fusion.8) | copy-start | bytes 3932164
  95.3 3.2 %copy-start.20 = (bf16[512,128]{1,0:T(8,128)(2,1)S(1)}, bf16[512,128]{1,0:T(8,128)(2,1)}, u32[]{:S(2)}) copy-start(bf16[512,128]{1,0:T(8,128)(2,1)} %param.29) | copy-start | bytes 393220
  172.0 24.4 %all-to-all-start = ((bf16[320,32,16]{0,2,1:T(8,128)(2,1)}), bf16[320,32,16]{0,2,1:T(8,128)(2,1)}, u32[]{:S(2)}, u32[]{:S(2)}) async-start(bf16[320,32,16]{0,2,1:T(8,128)(2,1)} %bitcast.98), calls=%async_computation | async-start | bytes 786432 | tf_op jit(solution)/shard_map/all_to_all | solution.py:140
  (17 other events, 20.7 us)
Sparse Core Ops, SparseCore 0:
  110.1 38.6 reduce-scatter.3

commit v5 on v4

--- a/solution.py
+++ b/solution.py
@@ -101,14 +101,18 @@
     squares = lax.psum(jnp.sum(gated * gated, axis=-1), "head")
     mean_sq = squares / (channels * lax.axis_size("head"))
     hidden = (gated * norm_weight[None, :]).astype(jnp.bfloat16)
-    proj = lax.psum_scatter(
-        jnp.einsum("kd,tk->dt", w_out, hidden, preferred_element_type=jnp.float32).astype(
-            jnp.bfloat16
-        ),
+    partials = jnp.einsum("kd,tk->dt", w_out, hidden, preferred_element_type=jnp.float32).astype(
+        jnp.bfloat16
+    )
+    groups = lax.axis_size("head")
+    arrived = lax.all_to_all(
+        partials.reshape(groups, partials.shape[0] // groups, rows_here),
         "head",
-        scatter_dimension=0,
-        tiled=True,
-    ).astype(jnp.float32)
+        0,
+        0,
+        tiled=False,
+    )
+    proj = jnp.sum(arrived.astype(jnp.float32), axis=0)
     proj = proj * lax.rsqrt(mean_sq + EPS)[None, :]
     block_out = (resid.astype(jnp.float32) + proj).astype(jnp.bfloat16)
     features = resid.shape[0] * lax.axis_size("head")

time: 206 us -> 202 us (0.981)
  waiting for transfers between devices: 60.5 us -> 39.3 us
  blocking collectives: 25.3 us -> 46 us
  between operations: 14.7 us -> 1.37 us
  other arithmetic: 20.4 us -> 25.3 us
  starting transfers between devices: 34.2 us -> 38.6 us
    unnamed x2 -> x0, waiting for transfers between devices: 22.3 us -> none
    psum x1, blocking collectives: 12.4 us -> 33.4 us  [body(): squares = lax.psum(jnp.sum(gated * gated, axis=-1), 'head')]
    unnamed x74 -> x96, local copies, waits for them, and re-layouts: 21 us -> 14.1 us
    all_to_all x0 -> x1, starting transfers between devices: none -> 4.71 us  [body(): lax.all_to_all(partials.reshape(groups, partials.shape[0] // groups, rows...]
    convert_element_type x0 -> x1, local copies, waits for them, and re-layouts: none -> 4.41 us  [body(): jnp.einsum('kd,tk->dt', w_out, hidden, preferred_element_type=jnp.float32)]
    reduce_sum x0 -> x1, other arithmetic: none -> 3.02 us  [body(): proj = jnp.sum(arrived.astype(jnp.float32), axis=0)]
    reduce_sum x0 -> x1, local copies, waits for them, and re-layouts: none -> 2.24 us  [body(): proj = jnp.sum(arrived.astype(jnp.float32), axis=0)]
  transfers between devices with their start and end apart: 8 -> 8, of which waited for: 7 -> 6; matrix products, arithmetic and copies ran while one was open for 10% -> 10% of each run, Pallas kernels for 0% -> 0%
where the time goes in v5:
time: 202 us; the launch traced here: 201 us
  blocking collectives  46 us (23%)
  waiting for transfers between devices  39.3 us (19%)
  starting transfers between devices  38.6 us (19%)
  local copies, waits for them, and re-layouts  38 us (19%)
  other arithmetic  25.3 us (13%)
  matrix products  12.3 us (6%)
    psum x1, blocking collectives, body(): squares = lax.psum(jnp.sum(gated * gated, axis=-1), 'head')  33.4 us
    ppermute x6, waiting for transfers between devices, from_behind(): lax.ppermute(value, axis, [(source, source + steps) for source in range(l...  26.6 us
    ppermute x6, starting transfers between devices, from_behind(): lax.ppermute(value, axis, [(source, source + steps) for source in range(l...  24 us
    unnamed x96, local copies, waits for them, and re-layouts  14.1 us
    all_to_all x1, waiting for transfers between devices, body(): lax.all_to_all(buffer.reshape(local_feat, seq_count, slot_cap), 'seq', sp...  12.7 us
    psum x1, blocking collectives, body(): lax.psum((jnp.sum(out_wide, axis=0), jnp.sum(out_wide * out_wide, axis=0)...  12.6 us
    all_to_all x1, starting transfers between devices, body(): lax.all_to_all(buffer.reshape(local_feat, seq_count, slot_cap), 'seq', sp...  9.91 us
    another operation x17, other arithmetic  7.94 us
  transfers between devices with their start and end apart: 8, of which 6 were waited for; matrix products, arithmetic and copies ran while one was open for 10% of the time, Pallas kernels for 0%

profile of v5, /device:TPU:32, one launch (start us, length us, event | category | flops | bytes accessed | tf_op | source)
XLA Modules:
  0.0 201.0 jit_solution(16041550649173824401)
XLA Ops:
  8.0 2.2 %copy.55 = bf16[512,640]{0,1:T(8,128)(2,1)} copy(bf16[512,640]{1,0:T(8,128)(2,1)} %param.24) | data formatting | bytes 1310720 | tf_op args[0]
  10.2 2.7 %reshape.660 = bf16[2,256,10,64]{1,0,3,2:T(2,128)(2,1)} reshape(bf16[512,640]{0,1:T(8,128)(2,1)} %copy.55) | data formatting | bytes 1310720 | tf_op jit(solution)/shard_map/reshape | solution.py:38
  12.9 2.2 %fusion.19 = f32[2,10,64,128]{3,2,1,0:T(8,128)S(1)} fusion(f32[2,256,128]{2,1,0:T(8,128)S(1)} %convert_element_type.78, f32[10,2,256]{2,0,1:T(8,128)} %copy.59, bf16[2,256,10,64]{1,0,3,2:T(2,128)(2,1)} %reshape.660), kind=kOutput, calls=%fused_computation.30 | convolution fusion | flops 85196800 | bytes 1593344 | tf_op jit(solution)/shard_map/hcsn,cshp->chpn/dot_general | solution.py:51
  16.2 3.5 %collective-permute-start = (bf16[656,128]{1,0:T(8,128)(2,1)S(1)}, bf16[656,128]{1,0:T(8,128)(2,1)S(1)}, u32[]{:S(2)}, u32[]{:S(2)}) collective-permute-start(bf16[656,128]{1,0:T(8,128)(2,1)S(1)} %pad_maximum_fusion), channel_id=1, source_target_pairs={{0,8},{8,16},{16,24},{24,32},{32,40},{40,48},{48,56},{56,64},{64,7... | collective-permute-start | bytes 503816 | tf_op jit(solution)/shard_map/ppermute | solution.py:15
  19.7 6.5 %collective-permute-done = bf16[656,128]{1,0:T(8,128)(2,1)S(1)} collective-permute-done((bf16[656,128]{1,0:T(8,128)(2,1)S(1)}, bf16[656,128]{1,0:T(8,128)(2,1)S(1)}, u32[]{:S(2)}, u32[]{:S(2)}) %collective-permute-start) | collective-permute-done | bytes 167968 | tf_op jit(solution)/shard_map/ppermute | solution.py:15
  29.0 7.4 %collective-permute-done.1 = bf16[656,128]{1,0:T(8,128)(2,1)S(1)} collective-permute-done((bf16[656,128]{1,0:T(8,128)(2,1)S(1)}, bf16[656,128]{1,0:T(8,128)(2,1)S(1)}, u32[]{:S(2)}, u32[]{:S(2)}) %collective-permute-start.1) | collective-permute-done | bytes 167968 | tf_op jit(solution)/shard_map/ppermute | solution.py:15
  41.9 7.9 %collective-permute-done.2 = bf16[656,128]{1,0:T(8,128)(2,1)} collective-permute-done((bf16[656,128]{1,0:T(8,128)(2,1)}, bf16[656,128]{1,0:T(8,128)(2,1)}, u32[]{:S(2)}, u32[]{:S(2)}) %collective-permute-start.2) | collective-permute-done | bytes 167968 | tf_op jit(solution)/shard_map/ppermute | solution.py:15
  52.9 3.8 %collective-permute-start.3 = (bf16[656,128]{1,0:T(8,128)(2,1)S(1)}, bf16[656,128]{1,0:T(8,128)(2,1)S(1)}, u32[]{:S(2)}, u32[]{:S(2)}) collective-permute-start(bf16[656,128]{1,0:T(8,128)(2,1)S(1)} %pad_maximum_fusion.3), channel_id=1, source_target_pairs={{0,32},{8,40},{16,48},{24,56},{32,64},{40,72},{48,80},{56,88},{64,... | collective-permute-start | bytes 503816 | tf_op jit(solution)/shard_map/ppermute | solution.py:15
  65.4 10.2 %collective-permute-start.4 = (bf16[656,128]{1,0:T(8,128)(2,1)}, bf16[656,128]{1,0:T(8,128)(2,1)}, u32[]{:S(2)}, u32[]{:S(2)}) collective-permute-start(bf16[656,128]{1,0:T(8,128)(2,1)} %pad_maximum_fusion.4), channel_id=1, source_target_pairs={{0,64},{8,72},{16,80},{24,88},{32,96},{40,104},{48,112},{56,120},{... | collective-permute-start | bytes 503816 | tf_op jit(solution)/shard_map/ppermute | solution.py:15
  75.6 4.0 %fusion.8 = f32[2,256,10,64]{1,3,2,0:T(8,128)} fusion(f32[10,2,256]{2,0,1:T(8,128)} %copy.54, f32[10,2,256]{2,0,1:T(8,128)S(1)} %copy.52, f32[2,256,256]{2,1,0:T(8,128)} %fusion.103, pred[256,256]{1,0:T(8,128)(4,1)S(1)} %iota_compare_fusion.1, bf16[2,256,10,64]{1,0,3,2:T(2,128)(2,1)} %reshape.660), kind=kOutput, calls=%fused_computation.16 | convolution fusion | flops 175636480 | bytes 2596864 | tf_op jit(solution)/shard_map/hcts,cshp->cthp/dot_general | solution.py:48
  79.7 2.2 %copy.64 = bf16[512,640]{0,1:T(8,128)(2,1)} copy(bf16[512,640]{1,0:T(8,128)(2,1)} %param.25) | data formatting | bytes 1310720 | tf_op args[1]
  87.6 2.6 %collective-permute-start.5 = (bf16[656,128]{1,0:T(8,128)(2,1)S(1)}, bf16[656,128]{1,0:T(8,128)(2,1)S(1)}, u32[]{:S(2)}, u32[]{:S(2)}) collective-permute-start(bf16[656,128]{1,0:T(8,128)(2,1)S(1)} %pad_maximum_fusion.5), channel_id=1, source_target_pairs={{0,128},{8,136},{16,144},{24,152},{32,160},{40,168},{48,176},{56,1... | collective-permute-start | bytes 503816 | tf_op jit(solution)/shard_map/ppermute | solution.py:15
  91.3 3.0 %collective-permute-done.5 = bf16[656,128]{1,0:T(8,128)(2,1)S(1)} collective-permute-done((bf16[656,128]{1,0:T(8,128)(2,1)S(1)}, bf16[656,128]{1,0:T(8,128)(2,1)S(1)}, u32[]{:S(2)}, u32[]{:S(2)}) %collective-permute-start.5) | collective-permute-done | bytes 167968 | tf_op jit(solution)/shard_map/ppermute | solution.py:15
  97.7 3.9 %fusion = bf16[2560,512]{0,1:T(8,128)(2,1)} fusion(bf16[640,2560]{1,0:T(8,128)(2,1)S(1)} %copy-done, f32[640]{0:T(1024)S(1)} %copy-done.44, f32[512,640]{0,1:T(8,128)S(1)} %bitcast.97, bf16[512,640]{0,1:T(8,128)(2,1)S(1)} %copy-done.8), kind=kOutput, calls=%fused_computation.5 | convolution fusion | flops 1681653760 | bytes 7866880 | tf_op jit(solution)/shard_map/kd,tk->dt/dot_general | solution.py:104
  101.7 4.4 %copy.65 = bf16[2560,512]{1,0:T(8,128)(2,1)} copy(bf16[2560,512]{0,1:T(8,128)(2,1)} %fusion) | data formatting | bytes 5242880 | tf_op jit(solution)/shard_map/convert_element_type | solution.py:104
  106.1 4.7 %all-to-all-start = ((bf16[8,320,512]{2,1,0:T(8,128)(2,1)}), bf16[8,320,512]{2,1,0:T(8,128)(2,1)}, u32[]{:S(2)}, u32[]{:S(2)}) async-start(bf16[8,320,512]{2,1,0:T(8,128)(2,1)} %bitcast.96), calls=%async_computation | async-start | bytes 5242880 | tf_op jit(solution)/shard_map/all_to_all | solution.py:108
  114.9 33.4 %psum.21 = f32[512]{0:T(512)S(1)} all-reduce(f32[512]{0:T(512)S(1)} %multiply_reduce_fusion), channel_id=1, replica_groups=mesh['seq'=32,'head'=8] {'head'}, use_global_device_ids=true, to_apply=%region_10.11 | all-reduce | flops 512 | bytes 4096 | tf_op jit(solution)/shard_map/psum | solution.py:101
  148.3 3.0 %convert_reduce_fusion = f32[320,512]{1,0:T(8,128)} fusion(bf16[8,320,512]{2,1,0:T(8,128)(2,1)} %all-to-all-done), kind=kLoop, calls=%fused_computation.2 | loop fusion | flops 2457600 | bytes 3276800 | tf_op jit(solution)/shard_map/reduce_sum | solution.py:115
  151.3 2.2 %copy.66 = f32[320,512]{0,1:T(8,128)} copy(f32[320,512]{1,0:T(8,128)} %convert_reduce_fusion) | data formatting | bytes 1310720 | tf_op jit(solution)/shard_map/reduce_sum | solution.py:115
  153.6 2.2 %convert_reduce_fusion.1 = (f32[512]{0:T(512)S(1)}, f32[512]{0:T(512)S(1)}, bf16[320,512]{0,1:T(8,128)(2,1)}) fusion(f32[320,512]{0,1:T(8,128)} %copy.66, f32[512]{0:T(512)S(1)} %add_rsqrt_fusion.1, bf16[320,512]{0,1:T(8,128)(2,1)} %copy.47), kind=kLoop, calls=%fused_computation.33 | loop fusion | flops 1309696 | bytes 1316864 | tf_op jit(solution)/shard_map/reduce_sum | solution.py:133
  155.8 12.6 %all-reduce.8 = (f32[512]{0:T(512)S(1)}, f32[512]{0:T(512)S(1)}) all-reduce(f32[512]{0:T(512)S(1)} %get-tuple-element.81, f32[512]{0:T(512)S(1)} %get-tuple-element.80), channel_id=1, replica_groups=mesh['seq'=32,'head'=8] {'head'}, use_global_device_ids=true, to_apply=%region_15.16 | all-reduce | flops 1024 | bytes 8192 | tf_op jit(solution)/shard_map/psum | solution.py:133
  170.4 4.2 %scatter_custom_fusion = bf16[320,512]{0,1:T(8,128)(2,1)} fusion(s32[256]{0:T(256)S(1)} %compare_select_fusion.1, bf16[320,512]{0,1:T(8,128)(2,1)} %fusion.22, s32[1024]{0:T(1024)S(1)} %pad_clamp_fusion, bf16[]{:T(256)} %constant.150.clone.1), kind=kCustom, calls=%fused_computation.60 | custom fusion | bytes 328192 | tf_op jit(solution)/shard_map/scatter | solution.py:142
  174.6 9.9 %all-to-all-start.1 = ((bf16[320,32,16]{0,2,1:T(8,128)(2,1)}), bf16[320,32,16]{0,2,1:T(8,128)(2,1)}, u32[]{:S(2)}, u32[]{:S(2)}) async-start(bf16[320,32,16]{0,2,1:T(8,128)(2,1)} %bitcast.100), calls=%async_computation.1 | async-start | bytes 786432 | tf_op jit(solution)/shard_map/all_to_all | solution.py:144
  186.4 12.7 %all-to-all-done.1 = bf16[320,32,16]{0,2,1:T(8,128)(2,1)} async-done(((bf16[320,32,16]{0,2,1:T(8,128)(2,1)}), bf16[320,32,16]{0,2,1:T(8,128)(2,1)}, u32[]{:S(2)}, u32[]{:S(2)}) %all-to-all-start.1) | async-done | bytes 327712 | tf_op jit(solution)/shard_map/all_to_all | solution.py:144
  (196 shorter events, 47.9 us)
Async XLA Ops:
  0.6 97.1 %copy-start = (bf16[640,2560]{1,0:T(8,128)(2,1)S(1)}, bf16[640,2560]{1,0:T(8,128)(2,1)}, u32[]{:S(2)}) copy-start(bf16[640,2560]{1,0:T(8,128)(2,1)} %param.32) | copy-start | bytes 9830404
  1.6 5.5 %copy-start.22 = (f32[10,2,256]{2,1,0:T(2,128)}, f32[10,2,256]{2,1,0:T(2,128)S(1)}, u32[]{:S(2)}) copy-start(f32[10,2,256]{2,1,0:T(2,128)S(1)} %mul.253) | copy-start | bytes 61444
  16.2 10.0 %collective-permute-start = (bf16[656,128]{1,0:T(8,128)(2,1)S(1)}, bf16[656,128]{1,0:T(8,128)(2,1)S(1)}, u32[]{:S(2)}, u32[]{:S(2)}) collective-permute-start(bf16[656,128]{1,0:T(8,128)(2,1)S(1)} %pad_maximum_fusion), channel_id=1, source_target_pairs={{0,8},{8,16},{16,24},{24,32},{32,40},{40,48},{48,56},{56,64},{64,7... | collective-permute-start | bytes 503816 | tf_op jit(solution)/shard_map/ppermute | solution.py:15
  27.1 9.4 %collective-permute-start.1 = (bf16[656,128]{1,0:T(8,128)(2,1)S(1)}, bf16[656,128]{1,0:T(8,128)(2,1)S(1)}, u32[]{:S(2)}, u32[]{:S(2)}) collective-permute-start(bf16[656,128]{1,0:T(8,128)(2,1)S(1)} %pad_maximum_fusion.1), channel_id=1, source_target_pairs={{0,8},{8,16},{16,24},{24,32},{32,40},{40,48},{48,56},{56,64},{64,7... | collective-permute-start | bytes 503816 | tf_op jit(solution)/shard_map/ppermute | solution.py:15
  37.2 15.6 %copy-start.27 = (f32[10]{0:T(128)}, f32[10]{0:T(128)S(1)}, u32[]{:S(2)}) copy-start(f32[10]{0:T(128)S(1)} %get-tuple-element.112) | copy-start | bytes 124
  39.8 10.0 %collective-permute-start.2 = (bf16[656,128]{1,0:T(8,128)(2,1)}, bf16[656,128]{1,0:T(8,128)(2,1)}, u32[]{:S(2)}, u32[]{:S(2)}) collective-permute-start(bf16[656,128]{1,0:T(8,128)(2,1)} %pad_maximum_fusion.2), channel_id=1, source_target_pairs={{0,16},{8,24},{16,32},{24,40},{32,48},{40,56},{48,64},{56,72},{64,... | collective-permute-start | bytes 503816 | tf_op jit(solution)/shard_map/ppermute | solution.py:15
  41.9 14.8 %copy-start.17 = (bf16[512,128]{1,0:T(8,128)(2,1)S(1)}, bf16[512,128]{1,0:T(8,128)(2,1)}, u32[]{:S(2)}) copy-start(bf16[512,128]{1,0:T(8,128)(2,1)} %param.28) | copy-start | bytes 393220
  41.9 14.8 %copy-start.18 = (bf16[512,128]{1,0:T(8,128)(2,1)S(1)}, bf16[512,128]{1,0:T(8,128)(2,1)}, u32[]{:S(2)}) copy-start(bf16[512,128]{1,0:T(8,128)(2,1)} %param.29) | copy-start | bytes 393220
  50.8 7.0 %copy-start.21 = (f32[10,2,256]{2,1,0:T(2,128)S(1)}, f32[10,2,256]{2,1,0:T(2,128)}, u32[]{:S(2)}) copy-start(f32[10,2,256]{2,1,0:T(2,128)} %copy-done.20) | copy-start | bytes 61444
  50.8 7.0 %copy-start.23 = (f32[10,2,256]{2,1,0:T(2,128)S(1)}, f32[10,2,256]{2,1,0:T(2,128)}, u32[]{:S(2)}) copy-start(f32[10,2,256]{2,1,0:T(2,128)} %copy-done.22) | copy-start | bytes 61444
  52.9 7.3 %collective-permute-start.3 = (bf16[656,128]{1,0:T(8,128)(2,1)S(1)}, bf16[656,128]{1,0:T(8,128)(2,1)S(1)}, u32[]{:S(2)}, u32[]{:S(2)}) collective-permute-start(bf16[656,128]{1,0:T(8,128)(2,1)S(1)} %pad_maximum_fusion.3), channel_id=1, source_target_pairs={{0,32},{8,40},{16,48},{24,56},{32,64},{40,72},{48,80},{56,88},{64,... | collective-permute-start | bytes 503816 | tf_op jit(solution)/shard_map/ppermute | solution.py:15
  65.4 14.3 %copy-start.24 = (f32[2,256,10]{1,0,2:T(2,128)S(1)}, f32[2,256,10]{1,0,2:T(2,128)}, u32[]{:S(2)}) copy-start(f32[2,256,10]{1,0,2:T(2,128)} %get-tuple-element.101) | copy-start | bytes 61444
  65.4 20.8 %collective-permute-start.4 = (bf16[656,128]{1,0:T(8,128)(2,1)}, bf16[656,128]{1,0:T(8,128)(2,1)}, u32[]{:S(2)}, u32[]{:S(2)}) collective-permute-start(bf16[656,128]{1,0:T(8,128)(2,1)} %pad_maximum_fusion.4), channel_id=1, source_target_pairs={{0,64},{8,72},{16,80},{24,88},{32,96},{40,104},{48,112},{56,120},{... | collective-permute-start | bytes 503816 | tf_op jit(solution)/shard_map/ppermute | solution.py:15
  87.2 7.1 %copy-start.14 = (f32[640,128]{1,0:T(8,128)S(1)}, f32[640,128]{1,0:T(8,128)}, u32[]{:S(2)}) copy-start(f32[640,128]{1,0:T(8,128)} %slice.204) | copy-start | bytes 983044
  87.2 7.1 %copy-start.15 = (f32[640,128]{1,0:T(8,128)S(1)}, f32[640,128]{1,0:T(8,128)}, u32[]{:S(2)}) copy-start(f32[640,128]{1,0:T(8,128)} %slice.206) | copy-start | bytes 983044
  87.2 7.1 %copy-start.16 = (f32[640,128]{1,0:T(8,128)S(1)}, f32[640,128]{1,0:T(8,128)}, u32[]{:S(2)}) copy-start(f32[640,128]{1,0:T(8,128)} %slice.208) | copy-start | bytes 983044
  87.2 7.1 %copy-start.28 = (f32[10]{0:T(128)S(1)}, f32[10]{0:T(128)}, u32[]{:S(2)}) copy-start(f32[10]{0:T(128)} %copy-done.27) | copy-start | bytes 124
  87.2 7.1 %copy-start.30 = (f32[10]{0:T(128)S(1)}, f32[10]{0:T(128)}, u32[]{:S(2)}) copy-start(f32[10]{0:T(128)} %copy-done.29) | copy-start | bytes 124
  87.2 7.1 %copy-start.40 = (f32[10]{0:T(128)S(1)}, f32[10]{0:T(128)}, u32[]{:S(2)}) copy-start(f32[10]{0:T(128)} %copy-done.39) | copy-start | bytes 124
  87.6 6.7 %collective-permute-start.5 = (bf16[656,128]{1,0:T(8,128)(2,1)S(1)}, bf16[656,128]{1,0:T(8,128)(2,1)S(1)}, u32[]{:S(2)}, u32[]{:S(2)}) collective-permute-start(bf16[656,128]{1,0:T(8,128)(2,1)S(1)} %pad_maximum_fusion.5), channel_id=1, source_target_pairs={{0,128},{8,136},{16,144},{24,152},{32,160},{40,168},{48,176},{56,1... | collective-permute-start | bytes 503816 | tf_op jit(solution)/shard_map/ppermute | solution.py:15
  106.1 6.6 %copy-start.42 = (s32[256]{0:T(256)S(1)}, s32[256]{0:T(256)}, u32[]{:S(2)}) copy-start(s32[256]{0:T(256)} %param.34) | copy-start | bytes 3076
  106.1 6.7 %copy-start.41 = (s32[256]{0:T(256)S(1)}, s32[256]{0:T(256)}, u32[]{:S(2)}) copy-start(s32[256]{0:T(256)} %param.35) | copy-start | bytes 3076
  106.1 42.2 %all-to-all-start = ((bf16[8,320,512]{2,1,0:T(8,128)(2,1)}), bf16[8,320,512]{2,1,0:T(8,128)(2,1)}, u32[]{:S(2)}, u32[]{:S(2)}) async-start(bf16[8,320,512]{2,1,0:T(8,128)(2,1)} %bitcast.96), calls=%async_computation | async-start | bytes 5242880 | tf_op jit(solution)/shard_map/all_to_all | solution.py:108
  174.6 24.5 %all-to-all-start.1 = ((bf16[320,32,16]{0,2,1:T(8,128)(2,1)}), bf16[320,32,16]{0,2,1:T(8,128)(2,1)}, u32[]{:S(2)}, u32[]{:S(2)}) async-start(bf16[320,32,16]{0,2,1:T(8,128)(2,1)} %bitcast.100), calls=%async_computation.1 | async-start | bytes 786432 | tf_op jit(solution)/shard_map/all_to_all | solution.py:144
  (29 other events, 56.7 us)

commit v6 on v5

--- a/solution.py
+++ b/solution.py
@@ -98,21 +98,27 @@
     mixed = inner + carried + d_skip[None, None, :, None] * x_all.astype(jnp.float32)
     mixed = mixed.reshape(rows_here, channels)
     gated = mixed * jax.nn.silu(z_gate.astype(jnp.float32))
-    squares = lax.psum(jnp.sum(gated * gated, axis=-1), "head")
-    mean_sq = squares / (channels * lax.axis_size("head"))
+    local_squares = jnp.sum(gated * gated, axis=-1)
     hidden = (gated * norm_weight[None, :]).astype(jnp.bfloat16)
     partials = jnp.einsum("kd,tk->dt", w_out, hidden, preferred_element_type=jnp.float32).astype(
         jnp.bfloat16
     )
     groups = lax.axis_size("head")
-    arrived = lax.all_to_all(
-        partials.reshape(groups, partials.shape[0] // groups, rows_here),
-        "head",
-        0,
-        0,
-        tiled=False,
+    high = lax.reduce_precision(local_squares, exponent_bits=8, mantissa_bits=7)
+    rest = local_squares - high
+    middle = lax.reduce_precision(rest, exponent_bits=8, mantissa_bits=7)
+    extra = jnp.zeros((16, rows_here), jnp.float32).at[0:3].set(
+        jnp.stack([high, middle, rest - middle])
     )
-    proj = jnp.sum(arrived.astype(jnp.float32), axis=0)
+    extra = jnp.broadcast_to(extra.astype(jnp.bfloat16)[None], (groups, 16, rows_here))
+    sent = jnp.concatenate(
+        [partials.reshape(groups, partials.shape[0] // groups, rows_here), extra], axis=1
+    )
+    arrived = lax.all_to_all(sent, "head", 0, 0, tiled=False)
+    block_rows = partials.shape[0] // groups
+    proj = jnp.sum(arrived[:, :block_rows].astype(jnp.float32), axis=0)
+    squares = jnp.sum(arrived[:, block_rows : block_rows + 3].astype(jnp.float32), axis=(0, 1))
+    mean_sq = squares / (channels * groups)
     proj = proj * lax.rsqrt(mean_sq + EPS)[None, :]
     block_out = (resid.astype(jnp.float32) + proj).astype(jnp.bfloat16)
     features = resid.shape[0] * lax.axis_size("head")

time: 202 us -> 201 us (level)
  blocking collectives: 46 us -> 12.7 us
  waiting for transfers between devices: 39.3 us -> 70.5 us
    psum x1 -> x0, blocking collectives: 33.4 us -> none  [body(): squares = lax.psum(jnp.sum(gated * gated, axis=-1), 'head')]
    all_to_all x1, waiting for transfers between devices: 0.01 us -> 32 us  [body(): arrived = lax.all_to_all(sent, 'head', 0, 0, tiled=False)]
    concatenate x0 -> x1, other arithmetic: none -> 3.57 us  [body(): jnp.concatenate([partials.reshape(groups, partials.shape[0] // groups, ro...]
    reduce_sum x2 -> x3, other arithmetic: 4.95 us -> 4.32 us  [the longest x1 3 us: body(): proj = jnp.sum(arrived[:, :block_rows].astype(jnp.float32), axis=0)]
    another operation x17 -> x19, other arithmetic: 7.94 us -> 7.4 us
    unnamed x96 -> x70, local copies, waits for them, and re-layouts: 14.1 us -> 14.6 us
  transfers between devices with their start and end apart: 8 -> 8, of which waited for: 6 -> 7; matrix products, arithmetic and copies ran while one was open for 10% -> 9% of each run, Pallas kernels for 0% -> 0%
where the time goes in v6:
time: 201 us; the launch traced here: 200 us
  waiting for transfers between devices  70.5 us (35%)
  starting transfers between devices  38.5 us (19%)
  local copies, waits for them, and re-layouts  38 us (19%)
  other arithmetic  26.4 us (13%)
  blocking collectives  12.7 us (6%)
  matrix products  12.3 us (6%)
    all_to_all x1, waiting for transfers between devices, body(): arrived = lax.all_to_all(sent, 'head', 0, 0, tiled=False)  32 us
    ppermute x6, waiting for transfers between devices, from_behind(): lax.ppermute(value, axis, [(source, source + steps) for source in range(l...  25.8 us
    ppermute x6, starting transfers between devices, from_behind(): lax.ppermute(value, axis, [(source, source + steps) for source in range(l...  24.1 us
    unnamed x70, local copies, waits for them, and re-layouts  14.6 us
    psum x1, blocking collectives, body(): lax.psum((jnp.sum(out_wide, axis=0), jnp.sum(out_wide * out_wide, axis=0)...  12.7 us
    all_to_all x1, waiting for transfers between devices, body(): lax.all_to_all(buffer.reshape(local_feat, seq_count, slot_cap), 'seq', sp...  12.6 us
    all_to_all x1, starting transfers between devices, body(): lax.all_to_all(buffer.reshape(local_feat, seq_count, slot_cap), 'seq', sp...  9.92 us
    another operation x18, other arithmetic  7.38 us
  transfers between devices with their start and end apart: 8, of which 7 were waited for; matrix products, arithmetic and copies ran while one was open for 9% of the time, Pallas kernels for 0%

profile of v6, /device:TPU:32, one launch (start us, length us, event | category | flops | bytes accessed | tf_op | source)
XLA Modules:
  0.0 199.7 jit_solution(14245780853581480360)
XLA Ops:
  4.0 2.2 %copy.55 = bf16[512,640]{0,1:T(8,128)(2,1)} copy(bf16[512,640]{1,0:T(8,128)(2,1)} %param.26) | data formatting | bytes 1310720 | tf_op args[0]
  6.2 2.7 %reshape.713 = bf16[2,256,10,64]{1,0,3,2:T(2,128)(2,1)} reshape(bf16[512,640]{0,1:T(8,128)(2,1)} %copy.55) | data formatting | bytes 1310720 | tf_op jit(solution)/shard_map/reshape | solution.py:38
  10.0 2.2 %fusion.19 = f32[2,10,64,128]{3,2,1,0:T(8,128)S(1)} fusion(f32[2,256,128]{2,1,0:T(8,128)S(1)} %convert_element_type.82, f32[10,2,256]{2,0,1:T(8,128)S(1)} %copy.59, bf16[2,256,10,64]{1,0,3,2:T(2,128)(2,1)} %reshape.713), kind=kOutput, calls=%fused_computation.31 | convolution fusion | flops 85196800 | bytes 1593344 | tf_op jit(solution)/shard_map/hcsn,cshp->chpn/dot_general | solution.py:51
  14.9 3.5 %collective-permute-start = (bf16[656,128]{1,0:T(8,128)(2,1)S(1)}, bf16[656,128]{1,0:T(8,128)(2,1)S(1)}, u32[]{:S(2)}, u32[]{:S(2)}) collective-permute-start(bf16[656,128]{1,0:T(8,128)(2,1)S(1)} %pad_maximum_fusion.1), channel_id=1, source_target_pairs={{0,8},{8,16},{16,24},{24,32},{32,40},{40,48},{48,56},{56,64},{64,7... | collective-permute-start | bytes 503816 | tf_op jit(solution)/shard_map/ppermute | solution.py:15
  18.4 6.5 %collective-permute-done = bf16[656,128]{1,0:T(8,128)(2,1)S(1)} collective-permute-done((bf16[656,128]{1,0:T(8,128)(2,1)S(1)}, bf16[656,128]{1,0:T(8,128)(2,1)S(1)}, u32[]{:S(2)}, u32[]{:S(2)}) %collective-permute-start) | collective-permute-done | bytes 167968 | tf_op jit(solution)/shard_map/ppermute | solution.py:15
  27.7 7.4 %collective-permute-done.1 = bf16[656,128]{1,0:T(8,128)(2,1)S(1)} collective-permute-done((bf16[656,128]{1,0:T(8,128)(2,1)S(1)}, bf16[656,128]{1,0:T(8,128)(2,1)S(1)}, u32[]{:S(2)}, u32[]{:S(2)}) %collective-permute-start.1) | collective-permute-done | bytes 167968 | tf_op jit(solution)/shard_map/ppermute | solution.py:15
  40.7 7.9 %collective-permute-done.2 = bf16[656,128]{1,0:T(8,128)(2,1)} collective-permute-done((bf16[656,128]{1,0:T(8,128)(2,1)}, bf16[656,128]{1,0:T(8,128)(2,1)}, u32[]{:S(2)}, u32[]{:S(2)}) %collective-permute-start.2) | collective-permute-done | bytes 167968 | tf_op jit(solution)/shard_map/ppermute | solution.py:15
  51.6 3.8 %collective-permute-start.3 = (bf16[656,128]{1,0:T(8,128)(2,1)S(1)}, bf16[656,128]{1,0:T(8,128)(2,1)S(1)}, u32[]{:S(2)}, u32[]{:S(2)}) collective-permute-start(bf16[656,128]{1,0:T(8,128)(2,1)S(1)} %pad_maximum_fusion.4), channel_id=1, source_target_pairs={{0,32},{8,40},{16,48},{24,56},{32,64},{40,72},{48,80},{56,88},{64,... | collective-permute-start | bytes 503816 | tf_op jit(solution)/shard_map/ppermute | solution.py:15
  62.9 10.1 %collective-permute-start.4 = (bf16[656,128]{1,0:T(8,128)(2,1)}, bf16[656,128]{1,0:T(8,128)(2,1)}, u32[]{:S(2)}, u32[]{:S(2)}) collective-permute-start(bf16[656,128]{1,0:T(8,128)(2,1)} %pad_maximum_fusion.5), channel_id=1, source_target_pairs={{0,64},{8,72},{16,80},{24,88},{32,96},{40,104},{48,112},{56,120},{... | collective-permute-start | bytes 503816 | tf_op jit(solution)/shard_map/ppermute | solution.py:15
  73.0 4.1 %fusion.8 = f32[2,256,10,64]{1,3,2,0:T(8,128)} fusion(f32[10,2,256]{2,0,1:T(8,128)S(1)} %copy.54, f32[10,2,256]{2,0,1:T(8,128)} %copy.52, f32[2,256,256]{2,1,0:T(8,128)} %fusion.109, pred[256,256]{1,0:T(8,128)(4,1)} %iota_compare_fusion.1, bf16[2,256,10,64]{1,0,3,2:T(2,128)(2,1)} %reshape.713), kind=kOutput, calls=%fused_computation.17 | convolution fusion | flops 175636480 | bytes 2596864 | tf_op jit(solution)/shard_map/hcts,cshp->cthp/dot_general | solution.py:48
  85.0 2.8 %collective-permute-start.5 = (bf16[656,128]{1,0:T(8,128)(2,1)S(1)}, bf16[656,128]{1,0:T(8,128)(2,1)S(1)}, u32[]{:S(2)}, u32[]{:S(2)}) collective-permute-start(bf16[656,128]{1,0:T(8,128)(2,1)S(1)} %pad_maximum_fusion.6), channel_id=1, source_target_pairs={{0,128},{8,136},{16,144},{24,152},{32,160},{40,168},{48,176},{56,1... | collective-permute-start | bytes 503816 | tf_op jit(solution)/shard_map/ppermute | solution.py:15
  88.9 2.8 %collective-permute-done.5 = bf16[656,128]{1,0:T(8,128)(2,1)S(1)} collective-permute-done((bf16[656,128]{1,0:T(8,128)(2,1)S(1)}, bf16[656,128]{1,0:T(8,128)(2,1)S(1)}, u32[]{:S(2)}, u32[]{:S(2)}) %collective-permute-start.5) | collective-permute-done | bytes 167968 | tf_op jit(solution)/shard_map/ppermute | solution.py:15
  95.5 3.9 %fusion = bf16[2560,512]{0,1:T(8,128)(2,1)} fusion(bf16[640,2560]{1,0:T(8,128)(2,1)S(1)} %copy-done, f32[640]{0:T(1024)S(1)} %copy-done.31, f32[512,640]{0,1:T(8,128)S(1)} %bitcast.98, bf16[512,640]{0,1:T(8,128)(2,1)S(1)} %copy-done.7), kind=kOutput, calls=%fused_computation.5 | convolution fusion | flops 1681653760 | bytes 7866880 | tf_op jit(solution)/shard_map/kd,tk->dt/dot_general | solution.py:103
  99.4 4.4 %copy.65 = bf16[2560,512]{1,0:T(8,128)(2,1)} copy(bf16[2560,512]{0,1:T(8,128)(2,1)} %fusion) | data formatting | bytes 5242880 | tf_op jit(solution)/shard_map/convert_element_type | solution.py:103
  103.8 3.6 %pad_maximum_fusion = bf16[8,336,512]{2,1,0:T(8,128)(2,1)} fusion(bf16[8,16,512]{2,1,0:T(8,128)(2,1)S(1)} %broadcast_in_dim.31, bf16[8,320,512]{2,1,0:T(8,128)(2,1)} %bitcast.96), kind=kLoop, calls=%fused_computation.6 | loop fusion | flops 5505024 | bytes 5505024 | tf_op jit(solution)/shard_map/concatenate | solution.py:114
  107.4 4.5 %all-to-all-start = ((bf16[8,336,512]{2,1,0:T(8,128)(2,1)}), bf16[8,336,512]{2,1,0:T(8,128)(2,1)}, u32[]{:S(2)}, u32[]{:S(2)}) async-start(bf16[8,336,512]{2,1,0:T(8,128)(2,1)} %pad_maximum_fusion), calls=%async_computation | async-start | bytes 5505024 | tf_op jit(solution)/shard_map/all_to_all | solution.py:117
  114.1 32.0 %all-to-all-done = bf16[8,336,512]{2,1,0:T(8,128)(2,1)} async-done(((bf16[8,336,512]{2,1,0:T(8,128)(2,1)}), bf16[8,336,512]{2,1,0:T(8,128)(2,1)}, u32[]{:S(2)}, u32[]{:S(2)}) %all-to-all-start) | async-done | bytes 2752544 | tf_op jit(solution)/shard_map/all_to_all | solution.py:117
  146.2 3.0 %convert_reduce_fusion = f32[320,512]{1,0:T(8,128)} fusion(bf16[8,336,512]{2,1,0:T(8,128)(2,1)} %all-to-all-done), kind=kLoop, calls=%fused_computation.2 | loop fusion | flops 2457600 | bytes 3276800 | tf_op jit(solution)/shard_map/reduce_sum | solution.py:119
  149.2 2.2 %copy.66 = f32[320,512]{0,1:T(8,128)} copy(f32[320,512]{1,0:T(8,128)} %convert_reduce_fusion) | data formatting | bytes 1310720 | tf_op jit(solution)/shard_map/reduce_sum | solution.py:119
  152.3 2.2 %convert_reduce_fusion.1 = (f32[512]{0:T(512)S(1)}, f32[512]{0:T(512)S(1)}, bf16[320,512]{0,1:T(8,128)(2,1)}) fusion(f32[320,512]{0,1:T(8,128)} %copy.66, f32[512]{0:T(512)S(1)} %add_rsqrt_fusion.1, bf16[320,512]{0,1:T(8,128)(2,1)} %copy.47), kind=kLoop, calls=%fused_computation.34 | loop fusion | flops 1309696 | bytes 1316864 | tf_op jit(solution)/shard_map/reduce_sum | solution.py:139
  154.5 12.7 %all-reduce.9 = (f32[512]{0:T(512)S(1)}, f32[512]{0:T(512)S(1)}) all-reduce(f32[512]{0:T(512)S(1)} %get-tuple-element.93, f32[512]{0:T(512)S(1)} %get-tuple-element.92), channel_id=1, replica_groups=mesh['seq'=32,'head'=8] {'head'}, use_global_device_ids=true, to_apply=%region_15.16 | all-reduce | flops 1024 | bytes 8192 | tf_op jit(solution)/shard_map/psum | solution.py:139
  169.2 4.2 %scatter_custom_fusion = bf16[320,512]{0,1:T(8,128)(2,1)} fusion(s32[256]{0:T(256)S(1)} %compare_select_fusion.1, bf16[320,512]{0,1:T(8,128)(2,1)} %fusion.22, s32[1024]{0:T(1024)S(1)} %pad_clamp_fusion, bf16[]{:T(256)} %constant.177.clone.1), kind=kCustom, calls=%fused_computation.61 | custom fusion | bytes 328192 | tf_op jit(solution)/shard_map/scatter | solution.py:148
  173.4 9.9 %all-to-all-start.1 = ((bf16[320,32,16]{0,2,1:T(8,128)(2,1)}), bf16[320,32,16]{0,2,1:T(8,128)(2,1)}, u32[]{:S(2)}, u32[]{:S(2)}) async-start(bf16[320,32,16]{0,2,1:T(8,128)(2,1)} %bitcast.100), calls=%async_computation.1 | async-start | bytes 786432 | tf_op jit(solution)/shard_map/all_to_all | solution.py:150
  185.2 12.6 %all-to-all-done.1 = bf16[320,32,16]{0,2,1:T(8,128)(2,1)} async-done(((bf16[320,32,16]{0,2,1:T(8,128)(2,1)}), bf16[320,32,16]{0,2,1:T(8,128)(2,1)}, u32[]{:S(2)}, u32[]{:S(2)}) %all-to-all-start.1) | async-done | bytes 327712 | tf_op jit(solution)/shard_map/all_to_all | solution.py:150
  (174 shorter events, 46.9 us)
Async XLA Ops:
  0.6 94.8 %copy-start = (bf16[640,2560]{1,0:T(8,128)(2,1)S(1)}, bf16[640,2560]{1,0:T(8,128)(2,1)}, u32[]{:S(2)}) copy-start(bf16[640,2560]{1,0:T(8,128)(2,1)} %param.34) | copy-start | bytes 9830404
  4.0 5.3 %copy-start.16 = (bf16[512,128]{1,0:T(8,128)(2,1)S(1)}, bf16[512,128]{1,0:T(8,128)(2,1)}, u32[]{:S(2)}) copy-start(bf16[512,128]{1,0:T(8,128)(2,1)} %param.30) | copy-start | bytes 393220
  14.9 10.0 %collective-permute-start = (bf16[656,128]{1,0:T(8,128)(2,1)S(1)}, bf16[656,128]{1,0:T(8,128)(2,1)S(1)}, u32[]{:S(2)}, u32[]{:S(2)}) collective-permute-start(bf16[656,128]{1,0:T(8,128)(2,1)S(1)} %pad_maximum_fusion.1), channel_id=1, source_target_pairs={{0,8},{8,16},{16,24},{24,32},{32,40},{40,48},{48,56},{56,64},{64,7... | collective-permute-start | bytes 503816 | tf_op jit(solution)/shard_map/ppermute | solution.py:15
  25.7 9.4 %collective-permute-start.1 = (bf16[656,128]{1,0:T(8,128)(2,1)S(1)}, bf16[656,128]{1,0:T(8,128)(2,1)S(1)}, u32[]{:S(2)}, u32[]{:S(2)}) collective-permute-start(bf16[656,128]{1,0:T(8,128)(2,1)S(1)} %pad_maximum_fusion.2), channel_id=1, source_target_pairs={{0,8},{8,16},{16,24},{24,32},{32,40},{40,48},{48,56},{56,64},{64,7... | collective-permute-start | bytes 503816 | tf_op jit(solution)/shard_map/ppermute | solution.py:15
  38.6 10.0 %collective-permute-start.2 = (bf16[656,128]{1,0:T(8,128)(2,1)}, bf16[656,128]{1,0:T(8,128)(2,1)}, u32[]{:S(2)}, u32[]{:S(2)}) collective-permute-start(bf16[656,128]{1,0:T(8,128)(2,1)} %pad_maximum_fusion.3), channel_id=1, source_target_pairs={{0,16},{8,24},{16,32},{24,40},{32,48},{40,56},{48,64},{56,72},{64,... | collective-permute-start | bytes 503816 | tf_op jit(solution)/shard_map/ppermute | solution.py:15
  40.7 14.8 %copy-start.17 = (bf16[512,128]{1,0:T(8,128)(2,1)S(1)}, bf16[512,128]{1,0:T(8,128)(2,1)}, u32[]{:S(2)}) copy-start(bf16[512,128]{1,0:T(8,128)(2,1)} %param.30) | copy-start | bytes 393220
  40.7 14.8 %copy-start.18 = (bf16[512,128]{1,0:T(8,128)(2,1)S(1)}, bf16[512,128]{1,0:T(8,128)(2,1)}, u32[]{:S(2)}) copy-start(bf16[512,128]{1,0:T(8,128)(2,1)} %param.31) | copy-start | bytes 393220
  51.6 7.3 %collective-permute-start.3 = (bf16[656,128]{1,0:T(8,128)(2,1)S(1)}, bf16[656,128]{1,0:T(8,128)(2,1)S(1)}, u32[]{:S(2)}, u32[]{:S(2)}) collective-permute-start(bf16[656,128]{1,0:T(8,128)(2,1)S(1)} %pad_maximum_fusion.4), channel_id=1, source_target_pairs={{0,32},{8,40},{16,48},{24,56},{32,64},{40,72},{48,80},{56,88},{64,... | collective-permute-start | bytes 503816 | tf_op jit(solution)/shard_map/ppermute | solution.py:15
  62.9 20.7 %collective-permute-start.4 = (bf16[656,128]{1,0:T(8,128)(2,1)}, bf16[656,128]{1,0:T(8,128)(2,1)}, u32[]{:S(2)}, u32[]{:S(2)}) collective-permute-start(bf16[656,128]{1,0:T(8,128)(2,1)} %pad_maximum_fusion.5), channel_id=1, source_target_pairs={{0,64},{8,72},{16,80},{24,88},{32,96},{40,104},{48,112},{56,120},{... | collective-permute-start | bytes 503816 | tf_op jit(solution)/shard_map/ppermute | solution.py:15
  79.3 4.2 %copy-start.22 = (f32[10]{0:T(128)S(1)}, f32[10]{0:T(128)}, u32[]{:S(2)}) copy-start(f32[10]{0:T(128)} %get-tuple-element.97) | copy-start | bytes 124
  80.0 3.5 %copy-start.10 = (bf16[656,128]{1,0:T(8,128)(2,1)S(1)}, bf16[656,128]{1,0:T(8,128)(2,1)}, u32[]{:S(2)}) copy-start(bf16[656,128]{1,0:T(8,128)(2,1)} %copy-done.9) | copy-start | bytes 503812
  80.0 4.7 %copy-start.25 = (f32[1,10]{1,0:T(1,128)S(1)}, f32[1,10]{1,0:T(1,128)}, u32[]{:S(2)}) copy-start(f32[1,10]{1,0:T(1,128)} %copy-done.24) | copy-start | bytes 124
  83.6 5.2 %copy-start.27 = (f32[10]{0:T(128)S(1)}, f32[10]{0:T(128)}, u32[]{:S(2)}) copy-start(f32[10]{0:T(128)} %copy-done.26) | copy-start | bytes 124
  84.6 7.1 %copy-start.13 = (f32[640,128]{1,0:T(8,128)S(1)}, f32[640,128]{1,0:T(8,128)}, u32[]{:S(2)}) copy-start(f32[640,128]{1,0:T(8,128)} %slice.228) | copy-start | bytes 983044
  84.6 7.1 %copy-start.14 = (f32[640,128]{1,0:T(8,128)S(1)}, f32[640,128]{1,0:T(8,128)}, u32[]{:S(2)}) copy-start(f32[640,128]{1,0:T(8,128)} %slice.230) | copy-start | bytes 983044
  84.6 7.1 %copy-start.15 = (f32[640,128]{1,0:T(8,128)S(1)}, f32[640,128]{1,0:T(8,128)}, u32[]{:S(2)}) copy-start(f32[640,128]{1,0:T(8,128)} %slice.232) | copy-start | bytes 983044
  84.6 7.1 %copy-start.21 = (f32[10]{0:T(128)S(1)}, f32[10]{0:T(128)}, u32[]{:S(2)}) copy-start(f32[10]{0:T(128)} %copy-done.20) | copy-start | bytes 124
  85.0 6.7 %collective-permute-start.5 = (bf16[656,128]{1,0:T(8,128)(2,1)S(1)}, bf16[656,128]{1,0:T(8,128)(2,1)S(1)}, u32[]{:S(2)}, u32[]{:S(2)}) collective-permute-start(bf16[656,128]{1,0:T(8,128)(2,1)S(1)} %pad_maximum_fusion.6), channel_id=1, source_target_pairs={{0,128},{8,136},{16,144},{24,152},{32,160},{40,168},{48,176},{56,1... | collective-permute-start | bytes 503816 | tf_op jit(solution)/shard_map/ppermute | solution.py:15
  88.8 3.2 %copy-start.6 = (bf16[2,256,10,64]{1,0,3,2:T(2,128)(2,1)S(1)}, bf16[2,256,10,64]{1,0,3,2:T(2,128)(2,1)}, u32[]{:S(2)}) copy-start(bf16[2,256,10,64]{1,0,3,2:T(2,128)(2,1)} %reshape.713) | copy-start | bytes 1966084
  88.8 3.2 %copy-start.11 = (f32[1,10,64,128]{3,2,1,0:T(8,128)S(1)}, f32[1,10,64,128]{3,2,1,0:T(8,128)}, u32[]{:S(2)}) copy-start(f32[1,10,64,128]{3,2,1,0:T(8,128)} %get-tuple-element.108) | copy-start | bytes 983044
  107.4 6.4 %copy-start.29 = (s32[256]{0:T(256)S(1)}, s32[256]{0:T(256)}, u32[]{:S(2)}) copy-start(s32[256]{0:T(256)} %param.36) | copy-start | bytes 3076
  107.4 6.5 %copy-start.28 = (s32[256]{0:T(256)S(1)}, s32[256]{0:T(256)}, u32[]{:S(2)}) copy-start(s32[256]{0:T(256)} %param.37) | copy-start | bytes 3076
  107.4 38.7 %all-to-all-start = ((bf16[8,336,512]{2,1,0:T(8,128)(2,1)}), bf16[8,336,512]{2,1,0:T(8,128)(2,1)}, u32[]{:S(2)}, u32[]{:S(2)}) async-start(bf16[8,336,512]{2,1,0:T(8,128)(2,1)} %pad_maximum_fusion), calls=%async_computation | async-start | bytes 5505024 | tf_op jit(solution)/shard_map/all_to_all | solution.py:117
  173.4 24.4 %all-to-all-start.1 = ((bf16[320,32,16]{0,2,1:T(8,128)(2,1)}), bf16[320,32,16]{0,2,1:T(8,128)(2,1)}, u32[]{:S(2)}, u32[]{:S(2)}) async-start(bf16[320,32,16]{0,2,1:T(8,128)(2,1)} %bitcast.100), calls=%async_computation.1 | async-start | bytes 786432 | tf_op jit(solution)/shard_map/all_to_all | solution.py:150
  (16 other events, 22.1 us)

commit v7 on v6

--- a/solution.py
+++ b/solution.py
@@ -78,13 +78,20 @@
         logs = jnp.sum(wide[rows : rows + 3, :heads_here], axis=0)
         return logs, wide[:rows].reshape(heads_here, head_size, state_size)
 
-    logs, state = unpack(from_behind(pack(log_total, running), "seq", 1))
+    logs = jnp.zeros_like(log_total)
+    state = jnp.zeros_like(running)
+    window_logs, window_state = log_total, running
     distance = 1
     while distance < seq_count:
-        earlier_logs, earlier_state = unpack(from_behind(pack(logs, state), "seq", distance))
+        earlier_logs, earlier_state = unpack(
+            from_behind(pack(window_logs, window_state), "seq", distance)
+        )
         state = jnp.exp(logs)[:, None, None] * earlier_state + state
         logs = logs + earlier_logs
         distance *= 2
+        if distance < seq_count:
+            window_state = jnp.exp(log_total)[:, None, None] * state + running
+            window_logs = logs + log_total
     incoming = state
     start_states = jnp.stack(starts) + jnp.stack(reaches)[:, :, None, None] * incoming[None]
     carried = jnp.einsum(

time: 201 us -> 194 us (0.965)
  waiting for transfers between devices: 70.5 us -> 62.2 us
  other arithmetic: 26.4 us -> 29.5 us
    ppermute x6 -> x5, waiting for transfers between devices: 25.8 us -> 17.4 us  [from_behind(): lax.ppermute(value, axis, [(source, source + steps) for source in range(l...]
    ppermute x6 -> x5, starting transfers between devices: 24.1 us -> 27.4 us  [from_behind(): lax.ppermute(value, axis, [(source, source + steps) for source in range(l...]
    another operation x18, other arithmetic: 7.38 us -> 10.2 us
    all_to_all x1, starting transfers between devices: 9.92 us -> 7.66 us  [body(): lax.all_to_all(buffer.reshape(local_feat, seq_count, slot_cap), 'seq', sp...]
    slice x7 -> x5, local copies, waits for them, and re-layouts: 5.13 us -> 3.01 us  [unpack(): return (logs, wide[:rows].reshape(heads_here, head_size, state_size))]
    unnamed x70 -> x72, local copies, waits for them, and re-layouts: 14.6 us -> 15.4 us
  transfers between devices with their start and end apart: 8 -> 7, of which waited for: 7 -> 6; matrix products, arithmetic and copies ran while one was open for 9% -> 7% of each run, Pallas kernels for 0% -> 0%
where the time goes in v7:
time: 194 us; the launch traced here: 193 us
  waiting for transfers between devices  62.2 us (32%)
  starting transfers between devices  39.8 us (21%)
  local copies, waits for them, and re-layouts  36.8 us (19%)
  other arithmetic  29.5 us (15%)
  blocking collectives  12.7 us (7%)
  matrix products  11 us (6%)
    all_to_all x1, waiting for transfers between devices, body(): arrived = lax.all_to_all(sent, 'head', 0, 0, tiled=False)  31.9 us
    ppermute x5, starting transfers between devices, from_behind(): lax.ppermute(value, axis, [(source, source + steps) for source in range(l...  27.4 us
    ppermute x5, waiting for transfers between devices, from_behind(): lax.ppermute(value, axis, [(source, source + steps) for source in range(l...  17.4 us
    unnamed x72, local copies, waits for them, and re-layouts  15.4 us
    all_to_all x1, waiting for transfers between devices, body(): lax.all_to_all(buffer.reshape(local_feat, seq_count, slot_cap), 'seq', sp...  13 us
    psum x1, blocking collectives, body(): lax.psum((jnp.sum(out_wide, axis=0), jnp.sum(out_wide * out_wide, axis=0)...  12.7 us
    another operation x18, other arithmetic  10.2 us
    all_to_all x1, starting transfers between devices, body(): lax.all_to_all(buffer.reshape(local_feat, seq_count, slot_cap), 'seq', sp...  7.66 us
  transfers between devices with their start and end apart: 7, of which 6 were waited for; matrix products, arithmetic and copies ran while one was open for 7% of the time, Pallas kernels for 0%

profile of v7, /device:TPU:32, one launch (start us, length us, event | category | flops | bytes accessed | tf_op | source)
XLA Modules:
  0.0 193.2 jit_solution(3175947583673282056)
XLA Ops:
  4.0 2.2 %copy.55 = bf16[512,640]{0,1:T(8,128)(2,1)} copy(bf16[512,640]{1,0:T(8,128)(2,1)} %param.24) | data formatting | bytes 1310720 | tf_op args[0]
  6.2 2.7 %reshape.670 = bf16[2,256,10,64]{1,0,3,2:T(2,128)(2,1)} reshape(bf16[512,640]{0,1:T(8,128)(2,1)} %copy.55) | data formatting | bytes 1310720 | tf_op jit(solution)/shard_map/reshape | solution.py:38
  16.2 3.5 %collective-permute-start = (bf16[656,128]{1,0:T(8,128)(2,1)}, bf16[656,128]{1,0:T(8,128)(2,1)S(1)}, u32[]{:S(2)}, u32[]{:S(2)}) collective-permute-start(bf16[656,128]{1,0:T(8,128)(2,1)} %pad_maximum_fusion.1), channel_id=1, source_target_pairs={{0,8},{8,16},{16,24},{24,32},{32,40},{40,48},{48,56},{56,64},{64,7... | collective-permute-start | bytes 503816 | tf_op jit(solution)/shard_map/ppermute | solution.py:15
  19.9 6.6 %collective-permute-done = bf16[656,128]{1,0:T(8,128)(2,1)S(1)} collective-permute-done((bf16[656,128]{1,0:T(8,128)(2,1)}, bf16[656,128]{1,0:T(8,128)(2,1)S(1)}, u32[]{:S(2)}, u32[]{:S(2)}) %collective-permute-start) | collective-permute-done | bytes 167968 | tf_op jit(solution)/shard_map/ppermute | solution.py:15
  28.4 3.0 %collective-permute-start.1 = (bf16[656,128]{1,0:T(8,128)(2,1)S(1)}, bf16[656,128]{1,0:T(8,128)(2,1)S(1)}, u32[]{:S(2)}, u32[]{:S(2)}) collective-permute-start(bf16[656,128]{1,0:T(8,128)(2,1)S(1)} %pad_maximum_fusion.2), channel_id=1, source_target_pairs={{0,16},{8,24},{16,32},{24,40},{32,48},{40,56},{48,64},{56,72},{64,... | collective-permute-start | bytes 503816 | tf_op jit(solution)/shard_map/ppermute | solution.py:15
  31.4 6.7 %collective-permute-done.1 = bf16[656,128]{1,0:T(8,128)(2,1)S(1)} collective-permute-done((bf16[656,128]{1,0:T(8,128)(2,1)S(1)}, bf16[656,128]{1,0:T(8,128)(2,1)S(1)}, u32[]{:S(2)}, u32[]{:S(2)}) %collective-permute-start.1) | collective-permute-done | bytes 167968 | tf_op jit(solution)/shard_map/ppermute | solution.py:15
  41.8 3.8 %collective-permute-start.2 = (bf16[656,128]{1,0:T(8,128)(2,1)}, bf16[656,128]{1,0:T(8,128)(2,1)}, u32[]{:S(2)}, u32[]{:S(2)}) collective-permute-start(bf16[656,128]{1,0:T(8,128)(2,1)} %pad_maximum_fusion.3), channel_id=1, source_target_pairs={{0,32},{8,40},{16,48},{24,56},{32,64},{40,72},{48,80},{56,88},{64,... | collective-permute-start | bytes 503816 | tf_op jit(solution)/shard_map/ppermute | solution.py:15
  45.7 3.6 %collective-permute-done.2 = bf16[656,128]{1,0:T(8,128)(2,1)} collective-permute-done((bf16[656,128]{1,0:T(8,128)(2,1)}, bf16[656,128]{1,0:T(8,128)(2,1)}, u32[]{:S(2)}, u32[]{:S(2)}) %collective-permute-start.2) | collective-permute-done | bytes 167968 | tf_op jit(solution)/shard_map/ppermute | solution.py:15
  50.3 2.2 %add_convert_fusion.2 = (bf16[640,128]{1,0:T(8,128)(2,1)S(1)}, f32[640,128]{1,0:T(8,128)}) fusion(f32[640,128]{1,0:T(8,128)} %get-tuple-element.96, f32[640]{0:T(1024)S(1)} %mul.287, f32[656,128]{1,0:T(8,128)} %copy-done.1, f32[656,128]{1,0:T(8,128)} %copy-done.2, f32[640]{0:T(1024)S(1)} %mul.291, f32[656,128]{1,0:T(8,128)S(1)} %convert_element_type.82, ...), kind=kLoop, calls=%fused_computation.54 | loop fusion | flops 573440 | bytes 1809920 | tf_op jit(solution)/shard_map/convert.14
  52.5 8.3 %collective-permute-start.3 = (bf16[656,128]{1,0:T(8,128)(2,1)S(1)}, bf16[656,128]{1,0:T(8,128)(2,1)S(1)}, u32[]{:S(2)}, u32[]{:S(2)}) collective-permute-start(bf16[656,128]{1,0:T(8,128)(2,1)S(1)} %pad_maximum_fusion.4), channel_id=1, source_target_pairs={{0,64},{8,72},{16,80},{24,88},{32,96},{40,104},{48,112},{56,120},{... | collective-permute-start | bytes 503816 | tf_op jit(solution)/shard_map/ppermute | solution.py:15
  69.8 8.8 %collective-permute-start.4 = (bf16[656,128]{1,0:T(8,128)(2,1)}, bf16[656,128]{1,0:T(8,128)(2,1)}, u32[]{:S(2)}, u32[]{:S(2)}) collective-permute-start(bf16[656,128]{1,0:T(8,128)(2,1)} %pad_maximum_fusion.5), channel_id=1, source_target_pairs={{0,128},{8,136},{16,144},{24,152},{32,160},{40,168},{48,176},{56,1... | collective-permute-start | bytes 503816 | tf_op jit(solution)/shard_map/ppermute | solution.py:15
  78.6 2.8 %fusion.8 = f32[2,256,10,64]{1,3,2,0:T(8,128)} fusion(f32[10,2,256]{2,0,1:T(8,128)S(1)} %copy.54, f32[10,2,256]{2,0,1:T(8,128)S(1)} %copy-done.18, f32[2,256,256]{2,1,0:T(8,128)S(1)} %copy-done.12, pred[256,256]{1,0:T(8,128)(4,1)S(1)} %copy-done.17, bf16[2,256,10,64]{1,0,3,2:T(2,128)(2,1)S(1)} %copy-done.3), kind=kOutput, calls=%fused_computation.17 | convolution fusion | flops 175636480 | bytes 2596864 | tf_op jit(solution)/shard_map/hcts,cshp->cthp/dot_general | solution.py:48
  90.8 3.9 %fusion = bf16[2560,512]{0,1:T(8,128)(2,1)} fusion(bf16[640,2560]{1,0:T(8,128)(2,1)S(1)} %copy-done, f32[640]{0:T(1024)S(1)} %copy-done.32, f32[512,640]{0,1:T(8,128)S(1)} %bitcast.105, bf16[512,640]{0,1:T(8,128)(2,1)S(1)} %copy-done.5), kind=kOutput, calls=%fused_computation.5 | convolution fusion | flops 1681653760 | bytes 7866880 | tf_op jit(solution)/shard_map/kd,tk->dt/dot_general | solution.py:110
  94.7 4.4 %copy.65 = bf16[2560,512]{1,0:T(8,128)(2,1)} copy(bf16[2560,512]{0,1:T(8,128)(2,1)} %fusion) | data formatting | bytes 5242880 | tf_op jit(solution)/shard_map/convert_element_type | solution.py:110
  99.2 3.6 %pad_maximum_fusion = bf16[8,336,512]{2,1,0:T(8,128)(2,1)} fusion(bf16[8,16,512]{2,1,0:T(8,128)(2,1)S(1)} %broadcast_in_dim.31, bf16[8,320,512]{2,1,0:T(8,128)(2,1)} %bitcast.103), kind=kLoop, calls=%fused_computation.6 | loop fusion | flops 5505024 | bytes 5505024 | tf_op jit(solution)/shard_map/concatenate | solution.py:121
  102.8 4.7 %all-to-all-start = ((bf16[8,336,512]{2,1,0:T(8,128)(2,1)}), bf16[8,336,512]{2,1,0:T(8,128)(2,1)}, u32[]{:S(2)}, u32[]{:S(2)}) async-start(bf16[8,336,512]{2,1,0:T(8,128)(2,1)} %pad_maximum_fusion), calls=%async_computation | async-start | bytes 5505024 | tf_op jit(solution)/shard_map/all_to_all | solution.py:124
  109.7 31.9 %all-to-all-done = bf16[8,336,512]{2,1,0:T(8,128)(2,1)} async-done(((bf16[8,336,512]{2,1,0:T(8,128)(2,1)}), bf16[8,336,512]{2,1,0:T(8,128)(2,1)}, u32[]{:S(2)}, u32[]{:S(2)}) %all-to-all-start) | async-done | bytes 2752544 | tf_op jit(solution)/shard_map/all_to_all | solution.py:124
  141.5 3.0 %convert_reduce_fusion = f32[320,512]{1,0:T(8,128)} fusion(bf16[8,336,512]{2,1,0:T(8,128)(2,1)} %all-to-all-done), kind=kLoop, calls=%fused_computation.2 | loop fusion | flops 2457600 | bytes 3276800 | tf_op jit(solution)/shard_map/reduce_sum | solution.py:126
  144.5 2.3 %copy.66 = f32[320,512]{0,1:T(8,128)} copy(f32[320,512]{1,0:T(8,128)} %convert_reduce_fusion) | data formatting | bytes 1310720 | tf_op jit(solution)/shard_map/reduce_sum | solution.py:126
  147.7 2.2 %convert_reduce_fusion.1 = (f32[512]{0:T(512)S(1)}, f32[512]{0:T(512)S(1)}, bf16[320,512]{0,1:T(8,128)(2,1)}) fusion(f32[320,512]{0,1:T(8,128)} %copy.66, f32[512]{0:T(512)S(1)} %add_rsqrt_fusion.1, bf16[320,512]{0,1:T(8,128)(2,1)} %copy.47), kind=kLoop, calls=%fused_computation.34 | loop fusion | flops 1309696 | bytes 1316864 | tf_op jit(solution)/shard_map/reduce_sum | solution.py:146
  149.9 12.7 %all-reduce.8 = (f32[512]{0:T(512)S(1)}, f32[512]{0:T(512)S(1)}) all-reduce(f32[512]{0:T(512)S(1)} %get-tuple-element.81, f32[512]{0:T(512)S(1)} %get-tuple-element.80), channel_id=1, replica_groups=mesh['seq'=32,'head'=8] {'head'}, use_global_device_ids=true, to_apply=%region_14.15 | all-reduce | flops 1024 | bytes 8192 | tf_op jit(solution)/shard_map/psum | solution.py:146
  164.5 4.2 %scatter_custom_fusion = bf16[320,512]{0,1:T(8,128)(2,1)} fusion(s32[256]{0:T(256)S(1)} %compare_select_fusion.1, bf16[320,512]{0,1:T(8,128)(2,1)} %fusion.22, s32[1024]{0:T(1024)S(1)} %pad_clamp_fusion, bf16[]{:T(256)} %constant.159.clone.1), kind=kCustom, calls=%fused_computation.62 | custom fusion | bytes 328192 | tf_op jit(solution)/shard_map/scatter | solution.py:155
  168.8 7.7 %all-to-all-start.1 = ((bf16[320,32,16]{0,2,1:T(8,128)(2,1)}), bf16[320,32,16]{0,2,1:T(8,128)(2,1)}, u32[]{:S(2)}, u32[]{:S(2)}) async-start(bf16[320,32,16]{0,2,1:T(8,128)(2,1)} %bitcast.107), calls=%async_computation.1 | async-start | bytes 786432 | tf_op jit(solution)/shard_map/all_to_all | solution.py:157
  178.3 13.0 %all-to-all-done.1 = bf16[320,32,16]{0,2,1:T(8,128)(2,1)} async-done(((bf16[320,32,16]{0,2,1:T(8,128)(2,1)}), bf16[320,32,16]{0,2,1:T(8,128)(2,1)}, u32[]{:S(2)}, u32[]{:S(2)}) %all-to-all-start.1) | async-done | bytes 327712 | tf_op jit(solution)/shard_map/all_to_all | solution.py:157
  (167 shorter events, 44.3 us)
Async XLA Ops:
  0.6 90.2 %copy-start = (bf16[640,2560]{1,0:T(8,128)(2,1)S(1)}, bf16[640,2560]{1,0:T(8,128)(2,1)}, u32[]{:S(2)}) copy-start(bf16[640,2560]{1,0:T(8,128)(2,1)} %param.32) | copy-start | bytes 9830404
  4.0 5.3 %copy-start.13 = (bf16[512,128]{1,0:T(8,128)(2,1)S(1)}, bf16[512,128]{1,0:T(8,128)(2,1)}, u32[]{:S(2)}) copy-start(bf16[512,128]{1,0:T(8,128)(2,1)} %param.28) | copy-start | bytes 393220
  16.2 10.2 %collective-permute-start = (bf16[656,128]{1,0:T(8,128)(2,1)}, bf16[656,128]{1,0:T(8,128)(2,1)S(1)}, u32[]{:S(2)}, u32[]{:S(2)}) collective-permute-start(bf16[656,128]{1,0:T(8,128)(2,1)} %pad_maximum_fusion.1), channel_id=1, source_target_pairs={{0,8},{8,16},{16,24},{24,32},{32,40},{40,48},{48,56},{56,64},{64,7... | collective-permute-start | bytes 503816 | tf_op jit(solution)/shard_map/ppermute | solution.py:15
  28.4 9.7 %collective-permute-start.1 = (bf16[656,128]{1,0:T(8,128)(2,1)S(1)}, bf16[656,128]{1,0:T(8,128)(2,1)S(1)}, u32[]{:S(2)}, u32[]{:S(2)}) collective-permute-start(bf16[656,128]{1,0:T(8,128)(2,1)S(1)} %pad_maximum_fusion.2), channel_id=1, source_target_pairs={{0,16},{8,24},{16,32},{24,40},{32,48},{40,56},{48,64},{56,72},{64,... | collective-permute-start | bytes 503816 | tf_op jit(solution)/shard_map/ppermute | solution.py:15
  38.9 13.6 %copy-start.19 = (f32[1,10]{1,0:T(1,128)}, f32[1,10]{1,0:T(1,128)S(1)}, u32[]{:S(2)}) copy-start(f32[1,10]{1,0:T(1,128)S(1)} %get-tuple-element.92) | copy-start | bytes 124
  38.9 6.7 %copy-start.21 = (f32[10]{0:T(128)}, f32[10]{0:T(128)S(1)}, u32[]{:S(2)}) copy-start(f32[10]{0:T(128)S(1)} %get-tuple-element.118) | copy-start | bytes 124
  41.8 7.6 %collective-permute-start.2 = (bf16[656,128]{1,0:T(8,128)(2,1)}, bf16[656,128]{1,0:T(8,128)(2,1)}, u32[]{:S(2)}, u32[]{:S(2)}) collective-permute-start(bf16[656,128]{1,0:T(8,128)(2,1)} %pad_maximum_fusion.3), channel_id=1, source_target_pairs={{0,32},{8,40},{16,48},{24,56},{32,64},{40,72},{48,80},{56,88},{64,... | collective-permute-start | bytes 503816 | tf_op jit(solution)/shard_map/ppermute | solution.py:15
  45.7 15.1 %copy-start.14 = (bf16[512,128]{1,0:T(8,128)(2,1)S(1)}, bf16[512,128]{1,0:T(8,128)(2,1)}, u32[]{:S(2)}) copy-start(bf16[512,128]{1,0:T(8,128)(2,1)} %param.28) | copy-start | bytes 393220
  45.7 15.1 %copy-start.15 = (bf16[512,128]{1,0:T(8,128)(2,1)S(1)}, bf16[512,128]{1,0:T(8,128)(2,1)}, u32[]{:S(2)}) copy-start(bf16[512,128]{1,0:T(8,128)(2,1)} %param.29) | copy-start | bytes 393220
  52.5 12.6 %copy-start.20 = (f32[1,10]{1,0:T(1,128)S(1)}, f32[1,10]{1,0:T(1,128)}, u32[]{:S(2)}) copy-start(f32[1,10]{1,0:T(1,128)} %copy-done.19) | copy-start | bytes 124
  52.5 11.1 %collective-permute-start.3 = (bf16[656,128]{1,0:T(8,128)(2,1)S(1)}, bf16[656,128]{1,0:T(8,128)(2,1)S(1)}, u32[]{:S(2)}, u32[]{:S(2)}) collective-permute-start(bf16[656,128]{1,0:T(8,128)(2,1)S(1)} %pad_maximum_fusion.4), channel_id=1, source_target_pairs={{0,64},{8,72},{16,80},{24,88},{32,96},{40,104},{48,112},{56,120},{... | collective-permute-start | bytes 503816 | tf_op jit(solution)/shard_map/ppermute | solution.py:15
  62.5 16.2 %copy-start.18 = (f32[10,2,256]{2,0,1:T(8,128)S(1)}, f32[10,2,256]{2,0,1:T(8,128)}, u32[]{:S(2)}) copy-start(f32[10,2,256]{2,0,1:T(8,128)} %copy.52) | copy-start | bytes 61444
  66.9 11.7 %copy-start.3 = (bf16[2,256,10,64]{1,0,3,2:T(2,128)(2,1)S(1)}, bf16[2,256,10,64]{1,0,3,2:T(2,128)(2,1)}, u32[]{:S(2)}) copy-start(bf16[2,256,10,64]{1,0,3,2:T(2,128)(2,1)} %reshape.670) | copy-start | bytes 1966084
  66.9 11.7 %copy-start.12 = (f32[2,256,256]{2,1,0:T(8,128)S(1)}, f32[2,256,256]{2,1,0:T(8,128)}, u32[]{:S(2)}) copy-start(f32[2,256,256]{2,1,0:T(8,128)} %fusion.99) | copy-start | bytes 1572868
  66.9 11.7 %copy-start.17 = (pred[256,256]{1,0:T(8,128)(4,1)S(1)}, pred[256,256]{1,0:T(8,128)(4,1)}, u32[]{:S(2)}) copy-start(pred[256,256]{1,0:T(8,128)(4,1)} %iota_compare_fusion.1) | copy-start | bytes 196612
  69.8 15.9 %collective-permute-start.4 = (bf16[656,128]{1,0:T(8,128)(2,1)}, bf16[656,128]{1,0:T(8,128)(2,1)}, u32[]{:S(2)}, u32[]{:S(2)}) collective-permute-start(bf16[656,128]{1,0:T(8,128)(2,1)} %pad_maximum_fusion.5), channel_id=1, source_target_pairs={{0,128},{8,136},{16,144},{24,152},{32,160},{40,168},{48,176},{56,1... | collective-permute-start | bytes 503816 | tf_op jit(solution)/shard_map/ppermute | solution.py:15
  83.7 3.1 %copy-start.22 = (f32[10]{0:T(128)S(1)}, f32[10]{0:T(128)}, u32[]{:S(2)}) copy-start(f32[10]{0:T(128)} %copy-done.21) | copy-start | bytes 124
  83.7 3.1 %copy-start.24 = (f32[10]{0:T(128)S(1)}, f32[10]{0:T(128)}, u32[]{:S(2)}) copy-start(f32[10]{0:T(128)} %copy-done.23) | copy-start | bytes 124
  83.7 3.1 %copy-start.26 = (f32[10]{0:T(128)S(1)}, f32[10]{0:T(128)}, u32[]{:S(2)}) copy-start(f32[10]{0:T(128)} %copy-done.25) | copy-start | bytes 124
  83.7 3.1 %copy-start.27 = (f32[10]{0:T(128)S(1)}, f32[10]{0:T(128)}, u32[]{:S(2)}) copy-start(f32[10]{0:T(128)} %get-tuple-element.109) | copy-start | bytes 124
  102.8 6.6 %copy-start.30 = (s32[256]{0:T(256)S(1)}, s32[256]{0:T(256)}, u32[]{:S(2)}) copy-start(s32[256]{0:T(256)} %param.34) | copy-start | bytes 3076
  102.8 6.7 %copy-start.29 = (s32[256]{0:T(256)S(1)}, s32[256]{0:T(256)}, u32[]{:S(2)}) copy-start(s32[256]{0:T(256)} %param.35) | copy-start | bytes 3076
  102.8 38.8 %all-to-all-start = ((bf16[8,336,512]{2,1,0:T(8,128)(2,1)}), bf16[8,336,512]{2,1,0:T(8,128)(2,1)}, u32[]{:S(2)}, u32[]{:S(2)}) async-start(bf16[8,336,512]{2,1,0:T(8,128)(2,1)} %pad_maximum_fusion), calls=%async_computation | async-start | bytes 5505024 | tf_op jit(solution)/shard_map/all_to_all | solution.py:124
  168.8 22.6 %all-to-all-start.1 = ((bf16[320,32,16]{0,2,1:T(8,128)(2,1)}), bf16[320,32,16]{0,2,1:T(8,128)(2,1)}, u32[]{:S(2)}, u32[]{:S(2)}) async-start(bf16[320,32,16]{0,2,1:T(8,128)(2,1)} %bitcast.107), calls=%async_computation.1 | async-start | bytes 786432 | tf_op jit(solution)/shard_map/all_to_all | solution.py:157
  (16 other events, 19.5 us)

commit v8 on v7

--- a/solution.py
+++ b/solution.py
@@ -149,11 +149,12 @@
     normed = ((out_wide - mean_col[None, :]) * lax.rsqrt(variance + EPS)[None, :]).astype(
         jnp.bfloat16
     )
-    buffer = (
-        jnp.zeros((local_feat, seq_count * slot_cap), jnp.bfloat16)
-        .at[:, placed]
-        .set(normed[:, local_pos])
-    )
+    pos_hot = (local_pos[:, None] == jnp.arange(rows_here)[None, :]).astype(jnp.bfloat16)
+    slot_hot = (placed[:, None] == jnp.arange(seq_count * slot_cap)[None, :]).astype(jnp.bfloat16)
+    select = jnp.einsum("jp,js->ps", pos_hot, slot_hot, preferred_element_type=jnp.float32)
+    buffer = jnp.dot(
+        normed, select.astype(jnp.bfloat16), preferred_element_type=jnp.float32
+    ).astype(jnp.bfloat16)
     received = lax.all_to_all(
         buffer.reshape(local_feat, seq_count, slot_cap),
         "seq",

time: 194 us -> 188 us (0.969)
  blocking collectives: 12.7 us -> 35.2 us
  waiting for transfers between devices: 62.2 us -> 51.3 us
  local copies, waits for them, and re-layouts: 36.8 us -> 28.2 us
  starting transfers between devices: 39.8 us -> 31.9 us
  other arithmetic: 29.5 us -> 25.6 us
  matrix products: 11 us -> 13.4 us
    all_to_all x0 -> x1, blocking collectives: none -> 22.5 us  [body(): lax.all_to_all(buffer.reshape(local_feat, seq_count, slot_cap), 'seq', sp...]
    all_to_all x1 -> x0, waiting for transfers between devices: 13 us -> none  [body(): lax.all_to_all(buffer.reshape(local_feat, seq_count, slot_cap), 'seq', sp...]
    all_to_all x1 -> x0, starting transfers between devices: 7.66 us -> none  [body(): lax.all_to_all(buffer.reshape(local_feat, seq_count, slot_cap), 'seq', sp...]
    scatter x1 -> x0, local copies, waits for them, and re-layouts: 4.23 us -> none  [body(): buffer = jnp.zeros((local_feat, seq_count * slot_cap), jnp.bfloat16).at[:...]
    unnamed x72, local copies, waits for them, and re-layouts: 15.4 us -> 11.5 us
    dot_general x0 -> x1, matrix products: none -> 2.4 us  [body(): jnp.dot(normed, select.astype(jnp.bfloat16), preferred_element_type=jnp.f...]
    reduce_sum x1 -> x0, local copies, waits for them, and re-layouts: 2.26 us -> none  [body(): proj = jnp.sum(arrived[:, :block_rows].astype(jnp.float32), axis=0)]
    all_to_all x1, waiting for transfers between devices: 31.9 us -> 34 us  [body(): arrived = lax.all_to_all(sent, 'head', 0, 0, tiled=False)]
  transfers between devices with their start and end apart: 7 -> 6, of which waited for: 6 -> 5; matrix products, arithmetic and copies ran while one was open for 7% -> 5% of each run, Pallas kernels for 0% -> 0%
where the time goes in v8:
time: 188 us; the launch traced here: 187 us
  waiting for transfers between devices  51.3 us (27%)
  blocking collectives  35.2 us (19%)
  starting transfers between devices  31.9 us (17%)
  local copies, waits for them, and re-layouts  28.2 us (15%)
  other arithmetic  25.6 us (14%)
  matrix products  13.4 us (7%)
    all_to_all x1, waiting for transfers between devices, body(): arrived = lax.all_to_all(sent, 'head', 0, 0, tiled=False)  34 us
    ppermute x5, starting transfers between devices, from_behind(): lax.ppermute(value, axis, [(source, source + steps) for source in range(l...  27.4 us
    all_to_all x1, blocking collectives, body(): lax.all_to_all(buffer.reshape(local_feat, seq_count, slot_cap), 'seq', sp...  22.5 us
    ppermute x5, waiting for transfers between devices, from_behind(): lax.ppermute(value, axis, [(source, source + steps) for source in range(l...  17.4 us
    psum x1, blocking collectives, body(): lax.psum((jnp.sum(out_wide, axis=0), jnp.sum(out_wide * out_wide, axis=0)...  12.7 us
    unnamed x72, local copies, waits for them, and re-layouts  11.5 us
    another operation x18, other arithmetic  10.2 us
    all_to_all x1, starting transfers between devices, body(): arrived = lax.all_to_all(sent, 'head', 0, 0, tiled=False)  4.55 us
  transfers between devices with their start and end apart: 6, of which 5 were waited for; matrix products, arithmetic and copies ran while one was open for 5% of the time, Pallas kernels for 0%

profile of v8, /device:TPU:32, one launch (start us, length us, event | category | flops | bytes accessed | tf_op | source)
XLA Modules:
  0.0 186.9 jit_solution(5005838721322765436)
XLA Ops:
  4.0 2.2 %copy.50 = bf16[512,640]{0,1:T(8,128)(2,1)} copy(bf16[512,640]{1,0:T(8,128)(2,1)} %param.24) | data formatting | bytes 1310720 | tf_op args[0]
  6.2 2.7 %reshape.672 = bf16[2,256,10,64]{1,0,3,2:T(2,128)(2,1)} reshape(bf16[512,640]{0,1:T(8,128)(2,1)} %copy.50) | data formatting | bytes 1310720 | tf_op jit(solution)/shard_map/reshape | solution.py:38
  10.1 2.2 %fusion.19 = f32[2,10,64,128]{3,2,1,0:T(8,128)S(1)} fusion(f32[2,256,128]{2,1,0:T(8,128)S(1)} %convert_element_type.86, f32[10,2,256]{2,0,1:T(8,128)S(1)} %copy.54, bf16[2,256,10,64]{1,0,3,2:T(2,128)(2,1)} %reshape.672), kind=kOutput, calls=%fused_computation.30 | convolution fusion | flops 85196800 | bytes 1593344 | tf_op jit(solution)/shard_map/hcsn,cshp->chpn/dot_general | solution.py:51
  13.6 2.1 %fusion.103 = (bf16[640,128]{1,0:T(8,128)(2,1)S(1)}, f32[640,128]{1,0:T(8,128)}) fusion(f32[1,10,64,128]{3,2,1,0:T(8,128)} %get-tuple-element.97, f32[1,10,64,128]{3,2,1,0:T(8,128)} %get-tuple-element.95, f32[640]{0:T(1024)S(1)} %mul.283, f32[640]{0:T(1024)S(1)} %mul.280), kind=kLoop, calls=%fused_computation.190 | loop fusion | flops 327680 | bytes 1152000 | tf_op jit(solution)/shard_map/convert.35
  16.3 3.5 %collective-permute-start = (bf16[656,128]{1,0:T(8,128)(2,1)}, bf16[656,128]{1,0:T(8,128)(2,1)S(1)}, u32[]{:S(2)}, u32[]{:S(2)}) collective-permute-start(bf16[656,128]{1,0:T(8,128)(2,1)} %pad_maximum_fusion.1), channel_id=1, source_target_pairs={{0,8},{8,16},{16,24},{24,32},{32,40},{40,48},{48,56},{56,64},{64,7... | collective-permute-start | bytes 503816 | tf_op jit(solution)/shard_map/ppermute | solution.py:15
  19.9 6.6 %collective-permute-done = bf16[656,128]{1,0:T(8,128)(2,1)S(1)} collective-permute-done((bf16[656,128]{1,0:T(8,128)(2,1)}, bf16[656,128]{1,0:T(8,128)(2,1)S(1)}, u32[]{:S(2)}, u32[]{:S(2)}) %collective-permute-start) | collective-permute-done | bytes 167968 | tf_op jit(solution)/shard_map/ppermute | solution.py:15
  28.5 3.0 %collective-permute-start.1 = (bf16[656,128]{1,0:T(8,128)(2,1)S(1)}, bf16[656,128]{1,0:T(8,128)(2,1)S(1)}, u32[]{:S(2)}, u32[]{:S(2)}) collective-permute-start(bf16[656,128]{1,0:T(8,128)(2,1)S(1)} %pad_maximum_fusion.2), channel_id=1, source_target_pairs={{0,16},{8,24},{16,32},{24,40},{32,48},{40,56},{48,64},{56,72},{64,... | collective-permute-start | bytes 503816 | tf_op jit(solution)/shard_map/ppermute | solution.py:15
  31.5 6.7 %collective-permute-done.1 = bf16[656,128]{1,0:T(8,128)(2,1)S(1)} collective-permute-done((bf16[656,128]{1,0:T(8,128)(2,1)S(1)}, bf16[656,128]{1,0:T(8,128)(2,1)S(1)}, u32[]{:S(2)}, u32[]{:S(2)}) %collective-permute-start.1) | collective-permute-done | bytes 167968 | tf_op jit(solution)/shard_map/ppermute | solution.py:15
  41.7 3.8 %collective-permute-start.2 = (bf16[656,128]{1,0:T(8,128)(2,1)}, bf16[656,128]{1,0:T(8,128)(2,1)}, u32[]{:S(2)}, u32[]{:S(2)}) collective-permute-start(bf16[656,128]{1,0:T(8,128)(2,1)} %pad_maximum_fusion.3), channel_id=1, source_target_pairs={{0,32},{8,40},{16,48},{24,56},{32,64},{40,72},{48,80},{56,88},{64,... | collective-permute-start | bytes 503816 | tf_op jit(solution)/shard_map/ppermute | solution.py:15
  45.7 3.6 %collective-permute-done.2 = bf16[656,128]{1,0:T(8,128)(2,1)} collective-permute-done((bf16[656,128]{1,0:T(8,128)(2,1)}, bf16[656,128]{1,0:T(8,128)(2,1)}, u32[]{:S(2)}, u32[]{:S(2)}) %collective-permute-start.2) | collective-permute-done | bytes 167968 | tf_op jit(solution)/shard_map/ppermute | solution.py:15
  50.3 2.2 %add_convert_fusion.2 = (bf16[640,128]{1,0:T(8,128)(2,1)S(1)}, f32[640,128]{1,0:T(8,128)}) fusion(f32[640,128]{1,0:T(8,128)} %get-tuple-element.94, f32[640]{0:T(1024)S(1)} %mul.287, f32[656,128]{1,0:T(8,128)} %copy-done.1, f32[656,128]{1,0:T(8,128)} %copy-done.2, f32[640]{0:T(1024)S(1)} %mul.291, f32[656,128]{1,0:T(8,128)S(1)} %convert_element_type.90, ...), kind=kLoop, calls=%fused_computation.59 | loop fusion | flops 573440 | bytes 1809920 | tf_op jit(solution)/shard_map/convert.14
  52.5 8.3 %collective-permute-start.3 = (bf16[656,128]{1,0:T(8,128)(2,1)S(1)}, bf16[656,128]{1,0:T(8,128)(2,1)S(1)}, u32[]{:S(2)}, u32[]{:S(2)}) collective-permute-start(bf16[656,128]{1,0:T(8,128)(2,1)S(1)} %pad_maximum_fusion.4), channel_id=1, source_target_pairs={{0,64},{8,72},{16,80},{24,88},{32,96},{40,104},{48,112},{56,120},{... | collective-permute-start | bytes 503816 | tf_op jit(solution)/shard_map/ppermute | solution.py:15
  69.8 8.8 %collective-permute-start.4 = (bf16[656,128]{1,0:T(8,128)(2,1)}, bf16[656,128]{1,0:T(8,128)(2,1)}, u32[]{:S(2)}, u32[]{:S(2)}) collective-permute-start(bf16[656,128]{1,0:T(8,128)(2,1)} %pad_maximum_fusion.5), channel_id=1, source_target_pairs={{0,128},{8,136},{16,144},{24,152},{32,160},{40,168},{48,176},{56,1... | collective-permute-start | bytes 503816 | tf_op jit(solution)/shard_map/ppermute | solution.py:15
  78.6 2.8 %fusion.8 = f32[2,256,10,64]{1,3,2,0:T(8,128)} fusion(f32[10,2,256]{2,0,1:T(8,128)S(1)} %copy.49, f32[10,2,256]{2,0,1:T(8,128)S(1)} %copy-done.19, f32[2,256,256]{2,1,0:T(8,128)S(1)} %copy-done.12, pred[256,256]{1,0:T(8,128)(4,1)S(1)} %copy-done.18, bf16[2,256,10,64]{1,0,3,2:T(2,128)(2,1)S(1)} %copy-done.3), kind=kOutput, calls=%fused_computation.15 | convolution fusion | flops 175636480 | bytes 2596864 | tf_op jit(solution)/shard_map/hcts,cshp->cthp/dot_general | solution.py:48
  81.5 2.2 %copy.59 = bf16[512,640]{0,1:T(8,128)(2,1)} copy(bf16[512,640]{1,0:T(8,128)(2,1)} %param.25) | data formatting | bytes 1310720 | tf_op args[1]
  90.8 3.9 %fusion = bf16[2560,512]{0,1:T(8,128)(2,1)} fusion(bf16[640,2560]{1,0:T(8,128)(2,1)S(1)} %copy-done, f32[640]{0:T(1024)S(1)} %copy-done.33, f32[512,640]{0,1:T(8,128)S(1)} %bitcast.105, bf16[512,640]{0,1:T(8,128)(2,1)S(1)} %copy-done.5), kind=kOutput, calls=%fused_computation.3 | convolution fusion | flops 1681653760 | bytes 7866880 | tf_op jit(solution)/shard_map/kd,tk->dt/dot_general | solution.py:110
  94.7 4.4 %copy.60 = bf16[2560,512]{1,0:T(8,128)(2,1)} copy(bf16[2560,512]{0,1:T(8,128)(2,1)} %fusion) | data formatting | bytes 5242880 | tf_op jit(solution)/shard_map/convert_element_type | solution.py:110
  99.1 3.6 %pad_maximum_fusion = bf16[8,336,512]{2,1,0:T(8,128)(2,1)} fusion(bf16[8,16,512]{2,1,0:T(8,128)(2,1)S(1)} %broadcast_in_dim.25, bf16[8,320,512]{2,1,0:T(8,128)(2,1)} %bitcast.103), kind=kLoop, calls=%fused_computation.4 | loop fusion | flops 5505024 | bytes 5505024 | tf_op jit(solution)/shard_map/concatenate | solution.py:121
  102.7 4.5 %all-to-all-start = ((bf16[8,336,512]{2,1,0:T(8,128)(2,1)}), bf16[8,336,512]{2,1,0:T(8,128)(2,1)}, u32[]{:S(2)}, u32[]{:S(2)}) async-start(bf16[8,336,512]{2,1,0:T(8,128)(2,1)} %pad_maximum_fusion), calls=%async_computation | async-start | bytes 5505024 | tf_op jit(solution)/shard_map/all_to_all | solution.py:124
  107.5 34.0 %all-to-all-done = bf16[8,336,512]{2,1,0:T(8,128)(2,1)} async-done(((bf16[8,336,512]{2,1,0:T(8,128)(2,1)}), bf16[8,336,512]{2,1,0:T(8,128)(2,1)}, u32[]{:S(2)}, u32[]{:S(2)}) %all-to-all-start) | async-done | bytes 2752544 | tf_op jit(solution)/shard_map/all_to_all | solution.py:124
  142.3 2.2 %convert_reduce_fusion = f32[320,512]{1,0:T(8,128)S(1)} fusion(bf16[8,336,512]{2,1,0:T(8,128)(2,1)} %all-to-all-done), kind=kLoop, calls=%fused_computation | loop fusion | flops 2457600 | bytes 3276800 | tf_op jit(solution)/shard_map/reduce_sum | solution.py:126
  145.5 12.7 %all-reduce.8 = (f32[512]{0:T(512)S(1)}, f32[512]{0:T(512)S(1)}) all-reduce(f32[512]{0:T(512)S(1)} %get-tuple-element.79, f32[512]{0:T(512)S(1)} %get-tuple-element.78), channel_id=1, replica_groups=mesh['seq'=32,'head'=8] {'head'}, use_global_device_ids=true, to_apply=%region_13.14 | all-reduce | flops 1024 | bytes 8192 | tf_op jit(solution)/shard_map/psum | solution.py:146
  158.2 2.4 %fusion.21 = bf16[320,512]{1,0:T(8,128)(2,1)} fusion(bf16[320,512]{1,0:T(8,128)(2,1)} %get-tuple-element.82, f32[512]{0:T(512)S(1)} %get-tuple-element.103, f32[512]{0:T(512)S(1)} %get-tuple-element.102, s32[256]{0:T(256)S(1)} %get-tuple-element.126, s32[256]{0:T(256)S(1)} %get-tuple-element.125), kind=kOutput, calls=%fused_computation.32 | convolution fusion | flops 303333376 | bytes 661504 | tf_op jit(solution)/shard_map/dot_general | solution.py:155
  162.4 22.5 %all_to_all.10 = bf16[320,32,16]{0,2,1:T(8,128)(2,1)} all-to-all(bf16[320,32,16]{0,2,1:T(8,128)(2,1)} %bitcast.107), channel_id=1, replica_groups=mesh['seq'=32,'head'=8] {'seq'}, dimensions={1} | all-to-all | bytes 655360 | tf_op jit(solution)/shard_map/all_to_all | solution.py:158
  (163 shorter events, 34.9 us)
Async XLA Ops:
  0.6 90.2 %copy-start = (bf16[640,2560]{1,0:T(8,128)(2,1)S(1)}, bf16[640,2560]{1,0:T(8,128)(2,1)}, u32[]{:S(2)}) copy-start(bf16[640,2560]{1,0:T(8,128)(2,1)} %param.32) | copy-start | bytes 9830404
  4.0 5.4 %copy-start.13 = (bf16[512,128]{1,0:T(8,128)(2,1)S(1)}, bf16[512,128]{1,0:T(8,128)(2,1)}, u32[]{:S(2)}) copy-start(bf16[512,128]{1,0:T(8,128)(2,1)} %param.28) | copy-start | bytes 393220
  16.3 10.2 %collective-permute-start = (bf16[656,128]{1,0:T(8,128)(2,1)}, bf16[656,128]{1,0:T(8,128)(2,1)S(1)}, u32[]{:S(2)}, u32[]{:S(2)}) collective-permute-start(bf16[656,128]{1,0:T(8,128)(2,1)} %pad_maximum_fusion.1), channel_id=1, source_target_pairs={{0,8},{8,16},{16,24},{24,32},{32,40},{40,48},{48,56},{56,64},{64,7... | collective-permute-start | bytes 503816 | tf_op jit(solution)/shard_map/ppermute | solution.py:15
  28.5 9.7 %collective-permute-start.1 = (bf16[656,128]{1,0:T(8,128)(2,1)S(1)}, bf16[656,128]{1,0:T(8,128)(2,1)S(1)}, u32[]{:S(2)}, u32[]{:S(2)}) collective-permute-start(bf16[656,128]{1,0:T(8,128)(2,1)S(1)} %pad_maximum_fusion.2), channel_id=1, source_target_pairs={{0,16},{8,24},{16,32},{24,40},{32,48},{40,56},{48,64},{56,72},{64,... | collective-permute-start | bytes 503816 | tf_op jit(solution)/shard_map/ppermute | solution.py:15
  39.0 13.6 %copy-start.20 = (f32[1,10]{1,0:T(1,128)}, f32[1,10]{1,0:T(1,128)S(1)}, u32[]{:S(2)}) copy-start(f32[1,10]{1,0:T(1,128)S(1)} %get-tuple-element.90) | copy-start | bytes 124
  39.0 6.6 %copy-start.22 = (f32[10]{0:T(128)}, f32[10]{0:T(128)S(1)}, u32[]{:S(2)}) copy-start(f32[10]{0:T(128)S(1)} %get-tuple-element.116) | copy-start | bytes 124
  41.7 7.6 %collective-permute-start.2 = (bf16[656,128]{1,0:T(8,128)(2,1)}, bf16[656,128]{1,0:T(8,128)(2,1)}, u32[]{:S(2)}, u32[]{:S(2)}) collective-permute-start(bf16[656,128]{1,0:T(8,128)(2,1)} %pad_maximum_fusion.3), channel_id=1, source_target_pairs={{0,32},{8,40},{16,48},{24,56},{32,64},{40,72},{48,80},{56,88},{64,... | collective-permute-start | bytes 503816 | tf_op jit(solution)/shard_map/ppermute | solution.py:15
  45.7 15.1 %copy-start.14 = (bf16[512,128]{1,0:T(8,128)(2,1)S(1)}, bf16[512,128]{1,0:T(8,128)(2,1)}, u32[]{:S(2)}) copy-start(bf16[512,128]{1,0:T(8,128)(2,1)} %param.28) | copy-start | bytes 393220
  45.7 15.1 %copy-start.15 = (bf16[512,128]{1,0:T(8,128)(2,1)S(1)}, bf16[512,128]{1,0:T(8,128)(2,1)}, u32[]{:S(2)}) copy-start(bf16[512,128]{1,0:T(8,128)(2,1)} %param.29) | copy-start | bytes 393220
  52.5 12.6 %copy-start.21 = (f32[1,10]{1,0:T(1,128)S(1)}, f32[1,10]{1,0:T(1,128)}, u32[]{:S(2)}) copy-start(f32[1,10]{1,0:T(1,128)} %copy-done.20) | copy-start | bytes 124
  52.5 11.1 %collective-permute-start.3 = (bf16[656,128]{1,0:T(8,128)(2,1)S(1)}, bf16[656,128]{1,0:T(8,128)(2,1)S(1)}, u32[]{:S(2)}, u32[]{:S(2)}) collective-permute-start(bf16[656,128]{1,0:T(8,128)(2,1)S(1)} %pad_maximum_fusion.4), channel_id=1, source_target_pairs={{0,64},{8,72},{16,80},{24,88},{32,96},{40,104},{48,112},{56,120},{... | collective-permute-start | bytes 503816 | tf_op jit(solution)/shard_map/ppermute | solution.py:15
  62.5 16.2 %copy-start.19 = (f32[10,2,256]{2,0,1:T(8,128)S(1)}, f32[10,2,256]{2,0,1:T(8,128)}, u32[]{:S(2)}) copy-start(f32[10,2,256]{2,0,1:T(8,128)} %copy.47) | copy-start | bytes 61444
  66.9 11.7 %copy-start.3 = (bf16[2,256,10,64]{1,0,3,2:T(2,128)(2,1)S(1)}, bf16[2,256,10,64]{1,0,3,2:T(2,128)(2,1)}, u32[]{:S(2)}) copy-start(bf16[2,256,10,64]{1,0,3,2:T(2,128)(2,1)} %reshape.672) | copy-start | bytes 1966084
  66.9 11.7 %copy-start.12 = (f32[2,256,256]{2,1,0:T(8,128)S(1)}, f32[2,256,256]{2,1,0:T(8,128)}, u32[]{:S(2)}) copy-start(f32[2,256,256]{2,1,0:T(8,128)} %fusion.105) | copy-start | bytes 1572868
  66.9 11.7 %copy-start.18 = (pred[256,256]{1,0:T(8,128)(4,1)S(1)}, pred[256,256]{1,0:T(8,128)(4,1)}, u32[]{:S(2)}) copy-start(pred[256,256]{1,0:T(8,128)(4,1)} %iota_compare_fusion.7) | copy-start | bytes 196612
  69.8 15.9 %collective-permute-start.4 = (bf16[656,128]{1,0:T(8,128)(2,1)}, bf16[656,128]{1,0:T(8,128)(2,1)}, u32[]{:S(2)}, u32[]{:S(2)}) collective-permute-start(bf16[656,128]{1,0:T(8,128)(2,1)} %pad_maximum_fusion.5), channel_id=1, source_target_pairs={{0,128},{8,136},{16,144},{24,152},{32,160},{40,168},{48,176},{56,1... | collective-permute-start | bytes 503816 | tf_op jit(solution)/shard_map/ppermute | solution.py:15
  83.7 3.1 %copy-start.23 = (f32[10]{0:T(128)S(1)}, f32[10]{0:T(128)}, u32[]{:S(2)}) copy-start(f32[10]{0:T(128)} %copy-done.22) | copy-start | bytes 124
  83.7 3.1 %copy-start.25 = (f32[10]{0:T(128)S(1)}, f32[10]{0:T(128)}, u32[]{:S(2)}) copy-start(f32[10]{0:T(128)} %copy-done.24) | copy-start | bytes 124
  83.7 3.1 %copy-start.27 = (f32[10]{0:T(128)S(1)}, f32[10]{0:T(128)}, u32[]{:S(2)}) copy-start(f32[10]{0:T(128)} %copy-done.26) | copy-start | bytes 124
  83.7 3.1 %copy-start.28 = (f32[10]{0:T(128)S(1)}, f32[10]{0:T(128)}, u32[]{:S(2)}) copy-start(f32[10]{0:T(128)} %get-tuple-element.107) | copy-start | bytes 124
  102.7 4.6 %copy-start.31 = (s32[256]{0:T(256)S(1)}, s32[256]{0:T(256)}, u32[]{:S(2)}) copy-start(s32[256]{0:T(256)} %param.35) | copy-start | bytes 3076
  102.7 4.8 %copy-start.30 = (s32[256]{0:T(256)S(1)}, s32[256]{0:T(256)}, u32[]{:S(2)}) copy-start(s32[256]{0:T(256)} %param.34) | copy-start | bytes 3076
  102.7 38.8 %all-to-all-start = ((bf16[8,336,512]{2,1,0:T(8,128)(2,1)}), bf16[8,336,512]{2,1,0:T(8,128)(2,1)}, u32[]{:S(2)}, u32[]{:S(2)}) async-start(bf16[8,336,512]{2,1,0:T(8,128)(2,1)} %pad_maximum_fusion), calls=%async_computation | async-start | bytes 5505024 | tf_op jit(solution)/shard_map/all_to_all | solution.py:124
  142.3 2.2 %copy-start.17 = (bf16[320,512]{1,0:T(8,128)(2,1)S(1)}, bf16[320,512]{1,0:T(8,128)(2,1)}, u32[]{:S(2)}) copy-start(bf16[320,512]{1,0:T(8,128)(2,1)} %param.33) | copy-start | bytes 983044
  (16 other events, 19.2 us)

commit v9 on v8

--- a/solution.py
+++ b/solution.py
@@ -107,22 +107,25 @@
     gated = mixed * jax.nn.silu(z_gate.astype(jnp.float32))
     local_squares = jnp.sum(gated * gated, axis=-1)
     hidden = (gated * norm_weight[None, :]).astype(jnp.bfloat16)
-    partials = jnp.einsum("kd,tk->dt", w_out, hidden, preferred_element_type=jnp.float32).astype(
-        jnp.bfloat16
+    groups = lax.axis_size("head")
+    block_rows = w_out.shape[1] // groups
+    padded_w = jnp.pad(
+        jnp.transpose(w_out.reshape(w_out.shape[0], groups, block_rows), (1, 2, 0)),
+        ((0, 0), (0, 16), (0, 0)),
     )
-    groups = lax.axis_size("head")
     high = lax.reduce_precision(local_squares, exponent_bits=8, mantissa_bits=7)
     rest = local_squares - high
     middle = lax.reduce_precision(rest, exponent_bits=8, mantissa_bits=7)
-    extra = jnp.zeros((16, rows_here), jnp.float32).at[0:3].set(
+    extra = jnp.zeros((block_rows + 16, rows_here), jnp.float32).at[block_rows : block_rows + 3].set(
         jnp.stack([high, middle, rest - middle])
     )
-    extra = jnp.broadcast_to(extra.astype(jnp.bfloat16)[None], (groups, 16, rows_here))
-    sent = jnp.concatenate(
-        [partials.reshape(groups, partials.shape[0] // groups, rows_here), extra], axis=1
+    sent = (
+        jnp.einsum("gdk,tk->gdt", padded_w, hidden, preferred_element_type=jnp.float32).astype(
+            jnp.bfloat16
+        )
+        + extra.astype(jnp.bfloat16)[None]
     )
     arrived = lax.all_to_all(sent, "head", 0, 0, tiled=False)
-    block_rows = partials.shape[0] // groups
     proj = jnp.sum(arrived[:, :block_rows].astype(jnp.float32), axis=0)
     squares = jnp.sum(arrived[:, block_rows : block_rows + 3].astype(jnp.float32), axis=(0, 1))
     mean_sq = squares / (channels * groups)

time: 188 us -> 156 us (0.83)
  other arithmetic: 25.6 us -> 6 us
  local copies, waits for them, and re-layouts: 28.2 us -> 19.1 us
    another operation x18, other arithmetic: 10.2 us -> 2.55 us
    convert_element_type x1 -> x0, local copies, waits for them, and re-layouts: 4.39 us -> none  [body(): jnp.einsum('kd,tk->dt', w_out, hidden, preferred_element_type=jnp.float32)]
    concatenate x1 -> x0, other arithmetic: 3.56 us -> none  [body(): jnp.concatenate([partials.reshape(groups, partials.shape[0] // groups, ro...]
    reshape x1, local copies, waits for them, and re-layouts: 2.67 us -> 0.15 us  [body(): x_all = x_in.reshape(blocks, BLOCK, heads_here, head_size)]
    unnamed x72 -> x51, local copies, waits for them, and re-layouts: 11.5 us -> 11.2 us
  transfers between devices with their start and end apart: 6 -> 6, of which waited for: 5 -> 5; matrix products, arithmetic and copies ran while one was open for 5% -> 9% of each run, Pallas kernels for 0% -> 0%
where the time goes in v9:
time: 156 us; the launch traced here: 155 us
  waiting for transfers between devices  51.4 us (33%)
  blocking collectives  33.7 us (22%)
  starting transfers between devices  31.8 us (20%)
  local copies, waits for them, and re-layouts  19.1 us (12%)
  matrix products  12 us (8%)
  other arithmetic  6 us (4%)
    all_to_all x1, waiting for transfers between devices, body(): arrived = lax.all_to_all(sent, 'head', 0, 0, tiled=False)  34 us
    ppermute x5, starting transfers between devices, from_behind(): lax.ppermute(value, axis, [(source, source + steps) for source in range(l...  27.4 us
    all_to_all x1, blocking collectives, body(): lax.all_to_all(buffer.reshape(local_feat, seq_count, slot_cap), 'seq', sp...  21 us
    ppermute x5, waiting for transfers between devices, from_behind(): lax.ppermute(value, axis, [(source, source + steps) for source in range(l...  17.5 us
    psum x1, blocking collectives, body(): lax.psum((jnp.sum(out_wide, axis=0), jnp.sum(out_wide * out_wide, axis=0)...  12.7 us
    unnamed x51, local copies, waits for them, and re-layouts  11.2 us
    all_to_all x1, starting transfers between devices, body(): arrived = lax.all_to_all(sent, 'head', 0, 0, tiled=False)  4.43 us
    dot_general x1, matrix products, body(): jnp.einsum('hcts,cshp->cthp', weights, x_all, preferred_element_type=jnp....  4.01 us
  transfers between devices with their start and end apart: 6, of which 5 were waited for; matrix products, arithmetic and copies ran while one was open for 9% of the time, Pallas kernels for 0%

profile of v9, /device:TPU:32, one launch (start us, length us, event | category | flops | bytes accessed | tf_op | source)
XLA Modules:
  0.0 155.2 jit_solution(12615900076329626872)
XLA Ops:
  1.5 1.2 reduce-window.6
  4.4 1.4 copy.53
  6.0 1.2 fusion.22
  8.5 3.5 %collective-permute-start = (bf16[656,128]{1,0:T(8,128)(2,1)S(1)}, bf16[656,128]{1,0:T(8,128)(2,1)S(1)}, u32[]{:S(2)}, u32[]{:S(2)}) collective-permute-start(bf16[656,128]{1,0:T(8,128)(2,1)S(1)} %pad_maximum_fusion), channel_id=1, source_target_pairs={{0,8},{8,16},{16,24},{24,32},{32,40},{40,48},{48,56},{56,64},{64,7... | collective-permute-start | bytes 503816 | tf_op jit(solution)/shard_map/ppermute | solution.py:15
  12.2 6.4 %collective-permute-done = bf16[656,128]{1,0:T(8,128)(2,1)S(1)} collective-permute-done((bf16[656,128]{1,0:T(8,128)(2,1)S(1)}, bf16[656,128]{1,0:T(8,128)(2,1)S(1)}, u32[]{:S(2)}, u32[]{:S(2)}) %collective-permute-start) | collective-permute-done | bytes 167968 | tf_op jit(solution)/shard_map/ppermute | solution.py:15
  18.8 3.0 %collective-permute-start.1 = (bf16[656,128]{1,0:T(8,128)(2,1)S(1)}, bf16[656,128]{1,0:T(8,128)(2,1)S(1)}, u32[]{:S(2)}, u32[]{:S(2)}) collective-permute-start(bf16[656,128]{1,0:T(8,128)(2,1)S(1)} %pad_maximum_fusion.1), channel_id=1, source_target_pairs={{0,16},{8,24},{16,32},{24,40},{32,48},{40,56},{48,64},{56,72},{64,... | collective-permute-start | bytes 503816 | tf_op jit(solution)/shard_map/ppermute | solution.py:15
  21.8 6.6 %collective-permute-done.1 = bf16[656,128]{1,0:T(8,128)(2,1)S(1)} collective-permute-done((bf16[656,128]{1,0:T(8,128)(2,1)S(1)}, bf16[656,128]{1,0:T(8,128)(2,1)S(1)}, u32[]{:S(2)}, u32[]{:S(2)}) %collective-permute-start.1) | collective-permute-done | bytes 167968 | tf_op jit(solution)/shard_map/ppermute | solution.py:15
  29.7 3.8 %collective-permute-start.2 = (bf16[656,128]{1,0:T(8,128)(2,1)S(1)}, bf16[656,128]{1,0:T(8,128)(2,1)S(1)}, u32[]{:S(2)}, u32[]{:S(2)}) collective-permute-start(bf16[656,128]{1,0:T(8,128)(2,1)S(1)} %pad_maximum_fusion.2), channel_id=1, source_target_pairs={{0,32},{8,40},{16,48},{24,56},{32,64},{40,72},{48,80},{56,88},{64,... | collective-permute-start | bytes 503816 | tf_op jit(solution)/shard_map/ppermute | solution.py:15
  33.7 3.3 %collective-permute-done.2 = bf16[656,128]{1,0:T(8,128)(2,1)S(1)} collective-permute-done((bf16[656,128]{1,0:T(8,128)(2,1)S(1)}, bf16[656,128]{1,0:T(8,128)(2,1)S(1)}, u32[]{:S(2)}, u32[]{:S(2)}) %collective-permute-start.2) | collective-permute-done | bytes 167968 | tf_op jit(solution)/shard_map/ppermute | solution.py:15
  37.6 8.2 %collective-permute-start.3 = (bf16[656,128]{1,0:T(8,128)(2,1)S(1)}, bf16[656,128]{1,0:T(8,128)(2,1)S(1)}, u32[]{:S(2)}, u32[]{:S(2)}) collective-permute-start(bf16[656,128]{1,0:T(8,128)(2,1)S(1)} %pad_maximum_fusion.3), channel_id=1, source_target_pairs={{0,64},{8,72},{16,80},{24,88},{32,96},{40,104},{48,112},{56,120},{... | collective-permute-start | bytes 503816 | tf_op jit(solution)/shard_map/ppermute | solution.py:15
  45.9 1.0 fusion.112
  47.5 1.2 collective-permute-done.3
  49.9 8.8 %collective-permute-start.4 = (bf16[656,128]{1,0:T(8,128)(2,1)}, bf16[656,128]{1,0:T(8,128)(2,1)}, u32[]{:S(2)}, u32[]{:S(2)}) collective-permute-start(bf16[656,128]{1,0:T(8,128)(2,1)} %pad_maximum_fusion.4), channel_id=1, source_target_pairs={{0,128},{8,136},{16,144},{24,152},{32,160},{40,168},{48,176},{56,1... | collective-permute-start | bytes 503816 | tf_op jit(solution)/shard_map/ppermute | solution.py:15
  58.7 4.0 %fusion.11 = f32[2,256,10,64]{1,3,2,0:T(8,128)} fusion(f32[10,2,256]{2,0,1:T(8,128)S(1)} %copy-done.18, f32[10,2,256]{2,0,1:T(8,128)S(1)} %copy.50, f32[2,256,256]{2,1,0:T(8,128)S(1)} %copy-done.14, pred[256,256]{1,0:T(8,128)(4,1)S(1)} %iota_compare_fusion.9, bf16[2,256,10,64]{1,0,3,2:T(2,128)(2,1)} %copy-done.3), kind=kOutput, calls=%fused_computation.15 | convolution fusion | flops 175636480 | bytes 2596864 | tf_op jit(solution)/shard_map/hcts,cshp->cthp/dot_general | solution.py:48
  62.7 2.2 %copy.62 = bf16[512,640]{0,1:T(8,128)(2,1)} copy(bf16[512,640]{1,0:T(8,128)(2,1)} %param.25) | data formatting | bytes 1310720 | tf_op args[1]
  65.0 3.4 %copy.45 = bf16[640,2560]{0,1:T(8,128)(2,1)} copy(bf16[640,2560]{1,0:T(8,128)(2,1)S(1)} %copy-done.1) | data formatting | bytes 6553600 | tf_op args[8]
  70.4 1.1 slice.205
  73.0 1.0 copy.61
  74.6 1.3 copy-done.2
  75.9 4.0 %convert_add_fusion = bf16[8,336,512]{2,1,0:T(8,128)(2,1)} fusion(bf16[8,320,640]{2,1,0:T(8,128)(2,1)S(1)} %bitcast.110, bf16[336,512]{1,0:T(8,128)(2,1)S(1)} %fusion.42, f32[640]{0:T(1024)S(1)} %copy-done.22, f32[512,640]{0,1:T(8,128)S(1)} %bitcast.108, bf16[512,640]{0,1:T(8,128)(2,1)S(1)} %copy-done.5), kind=kOutput, calls=%fused_computation.4 | convolution fusion | flops 1766981632 | bytes 8342016 | tf_op jit(solution)/shard_map/gdk,tk->gdt/dot_general | solution.py:123
  79.9 4.4 %all-to-all-start = ((bf16[8,336,512]{2,1,0:T(8,128)(2,1)}), bf16[8,336,512]{2,1,0:T(8,128)(2,1)S(1)}, u32[]{:S(2)}, u32[]{:S(2)}) async-start(bf16[8,336,512]{2,1,0:T(8,128)(2,1)} %convert_add_fusion), calls=%async_computation | async-start | bytes 5505024 | tf_op jit(solution)/shard_map/all_to_all | solution.py:128
  84.6 34.0 %all-to-all-done = bf16[8,336,512]{2,1,0:T(8,128)(2,1)S(1)} async-done(((bf16[8,336,512]{2,1,0:T(8,128)(2,1)}), bf16[8,336,512]{2,1,0:T(8,128)(2,1)S(1)}, u32[]{:S(2)}, u32[]{:S(2)}) %all-to-all-start) | async-done | bytes 2752544 | tf_op jit(solution)/shard_map/all_to_all | solution.py:128
  119.7 12.7 %all-reduce.9 = (f32[512]{0:T(512)S(1)}, f32[512]{0:T(512)S(1)}) all-reduce(f32[512]{0:T(512)S(1)} %get-tuple-element.79, f32[512]{0:T(512)S(1)} %get-tuple-element.78), channel_id=1, replica_groups=mesh['seq'=32,'head'=8] {'head'}, use_global_device_ids=true, to_apply=%region_13.14 | all-reduce | flops 1024 | bytes 8192 | tf_op jit(solution)/shard_map/psum | solution.py:149
  133.4 21.0 %all_to_all.10 = bf16[320,32,16]{0,2,1:T(8,128)(2,1)S(1)} all-to-all(bf16[320,32,16]{0,2,1:T(8,128)(2,1)S(1)} %bitcast.111), channel_id=1, replica_groups=mesh['seq'=32,'head'=8] {'seq'}, dimensions={1} | all-to-all | bytes 655360 | tf_op jit(solution)/shard_map/all_to_all | solution.py:161
  (139 shorter events, 15.4 us)
Async XLA Ops:
  0.6 45.2 %copy-start = (bf16[512,128]{1,0:T(8,128)(2,1)S(1)}, bf16[512,128]{1,0:T(8,128)(2,1)}, u32[]{:S(2)}) copy-start(bf16[512,128]{1,0:T(8,128)(2,1)} %param.29) | copy-start | bytes 393220
  4.3 1.6 %copy-start.15 = (bf16[512,128]{1,0:T(8,128)(2,1)S(1)}, bf16[512,128]{1,0:T(8,128)(2,1)}, u32[]{:S(2)}) copy-start(bf16[512,128]{1,0:T(8,128)(2,1)} %param.28) | copy-start | bytes 393220
  5.9 2.1 %copy-start.3 = (bf16[2,256,10,64]{1,0,3,2:T(2,128)(2,1)}, bf16[2,256,10,64]{1,0,3,2:T(2,128)(2,1)S(1)}, u32[]{:S(2)}) copy-start(bf16[2,256,10,64]{1,0,3,2:T(2,128)(2,1)S(1)} %reshape.673) | copy-start | bytes 1966084
  8.5 10.0 %collective-permute-start = (bf16[656,128]{1,0:T(8,128)(2,1)S(1)}, bf16[656,128]{1,0:T(8,128)(2,1)S(1)}, u32[]{:S(2)}, u32[]{:S(2)}) collective-permute-start(bf16[656,128]{1,0:T(8,128)(2,1)S(1)} %pad_maximum_fusion), channel_id=1, source_target_pairs={{0,8},{8,16},{16,24},{24,32},{32,40},{40,48},{48,56},{56,64},{64,7... | collective-permute-start | bytes 503816 | tf_op jit(solution)/shard_map/ppermute | solution.py:15
  18.6 3.3 %copy-start.6 = (bf16[656,128]{1,0:T(8,128)(2,1)}, bf16[656,128]{1,0:T(8,128)(2,1)S(1)}, u32[]{:S(2)}) copy-start(bf16[656,128]{1,0:T(8,128)(2,1)S(1)} %collective-permute-done) | copy-start | bytes 503812
  18.8 9.7 %collective-permute-start.1 = (bf16[656,128]{1,0:T(8,128)(2,1)S(1)}, bf16[656,128]{1,0:T(8,128)(2,1)S(1)}, u32[]{:S(2)}, u32[]{:S(2)}) collective-permute-start(bf16[656,128]{1,0:T(8,128)(2,1)S(1)} %pad_maximum_fusion.1), channel_id=1, source_target_pairs={{0,16},{8,24},{16,32},{24,40},{32,48},{40,56},{48,64},{56,72},{64,... | collective-permute-start | bytes 503816 | tf_op jit(solution)/shard_map/ppermute | solution.py:15
  29.7 7.3 %collective-permute-start.2 = (bf16[656,128]{1,0:T(8,128)(2,1)S(1)}, bf16[656,128]{1,0:T(8,128)(2,1)S(1)}, u32[]{:S(2)}, u32[]{:S(2)}) collective-permute-start(bf16[656,128]{1,0:T(8,128)(2,1)S(1)} %pad_maximum_fusion.2), channel_id=1, source_target_pairs={{0,32},{8,40},{16,48},{24,56},{32,64},{40,72},{48,80},{56,88},{64,... | collective-permute-start | bytes 503816 | tf_op jit(solution)/shard_map/ppermute | solution.py:15
  37.6 11.1 %collective-permute-start.3 = (bf16[656,128]{1,0:T(8,128)(2,1)S(1)}, bf16[656,128]{1,0:T(8,128)(2,1)S(1)}, u32[]{:S(2)}, u32[]{:S(2)}) collective-permute-start(bf16[656,128]{1,0:T(8,128)(2,1)S(1)} %pad_maximum_fusion.3), channel_id=1, source_target_pairs={{0,64},{8,72},{16,80},{24,88},{32,96},{40,104},{48,112},{56,120},{... | collective-permute-start | bytes 503816 | tf_op jit(solution)/shard_map/ppermute | solution.py:15
  48.9 9.8 %copy-start.14 = (f32[2,256,256]{2,1,0:T(8,128)S(1)}, f32[2,256,256]{2,1,0:T(8,128)}, u32[]{:S(2)}) copy-start(f32[2,256,256]{2,1,0:T(8,128)} %fusion.112) | copy-start | bytes 1572868
  48.9 9.8 %copy-start.18 = (f32[10,2,256]{2,0,1:T(8,128)S(1)}, f32[10,2,256]{2,0,1:T(8,128)}, u32[]{:S(2)}) copy-start(f32[10,2,256]{2,0,1:T(8,128)} %copy.52) | copy-start | bytes 61444
  49.9 20.5 %collective-permute-start.4 = (bf16[656,128]{1,0:T(8,128)(2,1)}, bf16[656,128]{1,0:T(8,128)(2,1)}, u32[]{:S(2)}, u32[]{:S(2)}) collective-permute-start(bf16[656,128]{1,0:T(8,128)(2,1)} %pad_maximum_fusion.4), channel_id=1, source_target_pairs={{0,128},{8,136},{16,144},{24,152},{32,160},{40,168},{48,176},{56,1... | collective-permute-start | bytes 503816 | tf_op jit(solution)/shard_map/ppermute | solution.py:15
  58.7 6.2 %copy-start.1 = (bf16[640,2560]{1,0:T(8,128)(2,1)S(1)}, bf16[640,2560]{1,0:T(8,128)(2,1)}, u32[]{:S(2)}) copy-start(bf16[640,2560]{1,0:T(8,128)(2,1)} %param.32) | copy-start | bytes 9830404
  68.4 1.9 %copy-start.9 = (bf16[656,128]{1,0:T(8,128)(2,1)S(1)}, bf16[656,128]{1,0:T(8,128)(2,1)}, u32[]{:S(2)}) copy-start(bf16[656,128]{1,0:T(8,128)(2,1)} %copy-done.8) | copy-start | bytes 503812
  68.4 2.0 %copy-start.11 = (bf16[656,128]{1,0:T(8,128)(2,1)S(1)}, bf16[656,128]{1,0:T(8,128)(2,1)}, u32[]{:S(2)}) copy-start(bf16[656,128]{1,0:T(8,128)(2,1)} %copy-done.10) | copy-start | bytes 503812
  70.4 1.4 copy-start.4
  70.4 1.4 copy-start.12
  70.4 1.7 %copy-start.13 = (f32[2,256,10,64]{1,3,2,0:T(8,128)S(1)}, f32[2,256,10,64]{1,3,2,0:T(8,128)}, u32[]{:S(2)}) copy-start(f32[2,256,10,64]{1,3,2,0:T(8,128)} %fusion.11) | copy-start | bytes 3932164
  70.4 1.7 %copy-start.21 = (f32[10]{0:T(128)S(1)}, f32[10]{0:T(128)}, u32[]{:S(2)}) copy-start(f32[10]{0:T(128)} %param.30) | copy-start | bytes 124
  74.0 1.9 %copy-start.2 = (bf16[640,2560]{0,1:T(8,128)(2,1)S(1)}, bf16[640,2560]{0,1:T(8,128)(2,1)}, u32[]{:S(2)}) copy-start(bf16[640,2560]{0,1:T(8,128)(2,1)} %copy.45) | copy-start | bytes 9830404
  74.1 1.8 %copy-start.22 = (f32[640]{0:T(1024)S(1)}, f32[640]{0:T(1024)}, u32[]{:S(2)}) copy-start(f32[640]{0:T(1024)} %param.31) | copy-start | bytes 7684
  79.9 4.4 %copy-start.20 = (s32[256]{0:T(256)S(1)}, s32[256]{0:T(256)}, u32[]{:S(2)}) copy-start(s32[256]{0:T(256)} %param.35) | copy-start | bytes 3076
  79.9 4.6 %copy-start.19 = (s32[256]{0:T(256)S(1)}, s32[256]{0:T(256)}, u32[]{:S(2)}) copy-start(s32[256]{0:T(256)} %param.34) | copy-start | bytes 3076
  79.9 38.6 %all-to-all-start = ((bf16[8,336,512]{2,1,0:T(8,128)(2,1)}), bf16[8,336,512]{2,1,0:T(8,128)(2,1)S(1)}, u32[]{:S(2)}, u32[]{:S(2)}) async-start(bf16[8,336,512]{2,1,0:T(8,128)(2,1)} %convert_add_fusion), calls=%async_computation | async-start | bytes 5505024 | tf_op jit(solution)/shard_map/all_to_all | solution.py:128
  119.7 34.6 %copy-start.17 = (bf16[320,512]{1,0:T(8,128)(2,1)}, bf16[320,512]{1,0:T(8,128)(2,1)S(1)}, u32[]{:S(2)}) copy-start(bf16[320,512]{1,0:T(8,128)(2,1)S(1)} %get-tuple-element.82) | copy-start | bytes 983044
  (5 other events, 4.6 us)

commit v10 on v9

--- a/solution.py
+++ b/solution.py
@@ -111,20 +111,24 @@
     block_rows = w_out.shape[1] // groups
     padded_w = jnp.pad(
         jnp.transpose(w_out.reshape(w_out.shape[0], groups, block_rows), (1, 2, 0)),
-        ((0, 0), (0, 16), (0, 0)),
+        ((0, 0), (0, 16), (0, 16)),
     )
+    out_row = jnp.arange(block_rows + 16)[:, None]
+    in_col = jnp.arange(channels + 16)[None, :]
+    marker = (out_row - block_rows == in_col - channels) & (out_row >= block_rows) & (
+        out_row < block_rows + 3
+    )
+    padded_w = padded_w + marker.astype(jnp.bfloat16)[None]
     high = lax.reduce_precision(local_squares, exponent_bits=8, mantissa_bits=7)
     rest = local_squares - high
     middle = lax.reduce_precision(rest, exponent_bits=8, mantissa_bits=7)
-    extra = jnp.zeros((block_rows + 16, rows_here), jnp.float32).at[block_rows : block_rows + 3].set(
-        jnp.stack([high, middle, rest - middle])
+    parts = jnp.zeros((rows_here, 16), jnp.float32).at[:, 0:3].set(
+        jnp.stack([high, middle, rest - middle], axis=1)
     )
-    sent = (
-        jnp.einsum("gdk,tk->gdt", padded_w, hidden, preferred_element_type=jnp.float32).astype(
-            jnp.bfloat16
-        )
-        + extra.astype(jnp.bfloat16)[None]
-    )
+    widened = jnp.concatenate([hidden, parts.astype(jnp.bfloat16)], axis=1)
+    sent = jnp.einsum(
+        "gdk,tk->gdt", padded_w, widened, preferred_element_type=jnp.float32
+    ).astype(jnp.bfloat16)
     arrived = lax.all_to_all(sent, "head", 0, 0, tiled=False)
     proj = jnp.sum(arrived[:, :block_rows].astype(jnp.float32), axis=0)
     squares = jnp.sum(arrived[:, block_rows : block_rows + 3].astype(jnp.float32), axis=(0, 1))

time: 156 us -> 148 us (0.949)
  starting transfers between devices: 31.8 us -> 26 us
  local copies, waits for them, and re-layouts: 19.1 us -> 14.1 us
  blocking collectives: 33.7 us -> 38.4 us
  waiting for transfers between devices: 51.4 us -> 49.4 us
    ppermute x5, starting transfers between devices: 27.4 us -> 21.5 us  [from_behind(): lax.ppermute(value, axis, [(source, source + steps) for source in range(l...]
    all_to_all x1, blocking collectives: 21 us -> 25.7 us  [body(): lax.all_to_all(buffer.reshape(local_feat, seq_count, slot_cap), 'seq', sp...]
    slice x5, local copies, waits for them, and re-layouts: 3.05 us -> 0.11 us  [unpack(): return (logs, wide[:rows].reshape(heads_here, head_size, state_size))]
    ppermute x5, waiting for transfers between devices: 17.5 us -> 15.4 us  [from_behind(): lax.ppermute(value, axis, [(source, source + steps) for source in range(l...]
    another operation x19, other arithmetic: 2.58 us -> 4.15 us
    unnamed x51 -> x25, local copies, waits for them, and re-layouts: 11.2 us -> 9.65 us
  transfers between devices with their start and end apart: 6 -> 6, of which waited for: 5 -> 4; matrix products, arithmetic and copies ran while one was open for 9% -> 9% of each run, Pallas kernels for 0% -> 0%
where the time goes in v10:
time: 148 us; the launch traced here: 147 us
  waiting for transfers between devices  49.4 us (33%)
  blocking collectives  38.4 us (26%)
  starting transfers between devices  26 us (18%)
  local copies, waits for them, and re-layouts  14.1 us (10%)
  matrix products  11.6 us (8%)
  other arithmetic  6.55 us (4%)
    all_to_all x1, waiting for transfers between devices, body(): arrived = lax.all_to_all(sent, 'head', 0, 0, tiled=False)  33.9 us
    all_to_all x1, blocking collectives, body(): lax.all_to_all(buffer.reshape(local_feat, seq_count, slot_cap), 'seq', sp...  25.7 us
    ppermute x5, starting transfers between devices, from_behind(): lax.ppermute(value, axis, [(source, source + steps) for source in range(l...  21.5 us
    ppermute x5, waiting for transfers between devices, from_behind(): lax.ppermute(value, axis, [(source, source + steps) for source in range(l...  15.4 us
    psum x1, blocking collectives, body(): lax.psum((jnp.sum(out_wide, axis=0), jnp.sum(out_wide * out_wide, axis=0)...  12.7 us
    unnamed x25, local copies, waits for them, and re-layouts  9.65 us
    all_to_all x1, starting transfers between devices, body(): arrived = lax.all_to_all(sent, 'head', 0, 0, tiled=False)  4.44 us
    another operation x19, other arithmetic  4.15 us
  transfers between devices with their start and end apart: 6, of which 4 were waited for; matrix products, arithmetic and copies ran while one was open for 9% of the time, Pallas kernels for 0%

profile of v10, /device:TPU:32, one launch (start us, length us, event | category | flops | bytes accessed | tf_op | source)
XLA Modules:
  0.0 147.2 jit_solution(3021496288816438305)
XLA Ops:
  1.5 1.2 reduce-window.6
  4.4 1.3 copy.54
  5.9 1.2 fusion.26
  7.8 3.5 %collective-permute-start = (bf16[656,128]{1,0:T(8,128)(2,1)S(1)}, bf16[656,128]{1,0:T(8,128)(2,1)S(1)}, u32[]{:S(2)}, u32[]{:S(2)}) collective-permute-start(bf16[656,128]{1,0:T(8,128)(2,1)S(1)} %pad_maximum_fusion), channel_id=1, source_target_pairs={{0,8},{8,16},{16,24},{24,32},{32,40},{40,48},{48,56},{56,64},{64,7... | collective-permute-start | bytes 503816 | tf_op jit(solution)/shard_map/ppermute | solution.py:15
  11.4 6.4 %collective-permute-done = bf16[656,128]{1,0:T(8,128)(2,1)S(1)} collective-permute-done((bf16[656,128]{1,0:T(8,128)(2,1)S(1)}, bf16[656,128]{1,0:T(8,128)(2,1)S(1)}, u32[]{:S(2)}, u32[]{:S(2)}) %collective-permute-start) | collective-permute-done | bytes 167968 | tf_op jit(solution)/shard_map/ppermute | solution.py:15
  18.1 3.0 %collective-permute-start.1 = (bf16[656,128]{1,0:T(8,128)(2,1)S(1)}, bf16[656,128]{1,0:T(8,128)(2,1)S(1)}, u32[]{:S(2)}, u32[]{:S(2)}) collective-permute-start(bf16[656,128]{1,0:T(8,128)(2,1)S(1)} %pad_maximum_fusion.1), channel_id=1, source_target_pairs={{0,16},{8,24},{16,32},{24,40},{32,48},{40,56},{48,64},{56,72},{64,... | collective-permute-start | bytes 503816 | tf_op jit(solution)/shard_map/ppermute | solution.py:15
  21.1 1.0 fusion.116
  22.2 5.6 %collective-permute-done.1 = bf16[656,128]{1,0:T(8,128)(2,1)S(1)} collective-permute-done((bf16[656,128]{1,0:T(8,128)(2,1)S(1)}, bf16[656,128]{1,0:T(8,128)(2,1)S(1)}, u32[]{:S(2)}, u32[]{:S(2)}) %collective-permute-start.1) | collective-permute-done | bytes 167968 | tf_op jit(solution)/shard_map/ppermute | solution.py:15
  28.3 3.8 %collective-permute-start.2 = (bf16[656,128]{1,0:T(8,128)(2,1)S(1)}, bf16[656,128]{1,0:T(8,128)(2,1)S(1)}, u32[]{:S(2)}, u32[]{:S(2)}) collective-permute-start(bf16[656,128]{1,0:T(8,128)(2,1)S(1)} %pad_maximum_fusion.2), channel_id=1, source_target_pairs={{0,32},{8,40},{16,48},{24,56},{32,64},{40,72},{48,80},{56,88},{64,... | collective-permute-start | bytes 503816 | tf_op jit(solution)/shard_map/ppermute | solution.py:15
  32.1 3.7 %fusion.14 = f32[2,256,10,64]{1,3,2,0:T(8,128)} fusion(f32[10,2,256]{2,0,1:T(8,128)S(1)} %copy.53, f32[10,2,256]{2,0,1:T(8,128)S(1)} %copy.51, f32[2,256,256]{2,1,0:T(8,128)} %fusion.116, pred[256,256]{1,0:T(8,128)(4,1)S(1)} %iota_compare_fusion.8, bf16[2,256,10,64]{1,0,3,2:T(2,128)(2,1)S(1)} %reshape.746), kind=kOutput, calls=%fused_computation.17 | convolution fusion | flops 175636480 | bytes 2596864 | tf_op jit(solution)/shard_map/hcts,cshp->cthp/dot_general | solution.py:48
  36.4 8.8 %collective-permute-start.3 = (bf16[656,128]{1,0:T(8,128)(2,1)S(1)}, bf16[656,128]{1,0:T(8,128)(2,1)S(1)}, u32[]{:S(2)}, u32[]{:S(2)}) collective-permute-start(bf16[656,128]{1,0:T(8,128)(2,1)S(1)} %pad_maximum_fusion.3), channel_id=1, source_target_pairs={{0,64},{8,72},{16,80},{24,88},{32,96},{40,104},{48,112},{56,120},{... | collective-permute-start | bytes 503816 | tf_op jit(solution)/shard_map/ppermute | solution.py:15
  45.3 1.3 copy.63
  46.6 5.7 %copy.46 = bf16[640,2560]{0,1:T(8,128)(2,1)} copy(bf16[640,2560]{1,0:T(8,128)(2,1)} %param.32) | data formatting | bytes 6553600 | tf_op args[8]
  53.4 2.4 %collective-permute-start.4 = (bf16[656,128]{1,0:T(8,128)(2,1)S(1)}, bf16[656,128]{1,0:T(8,128)(2,1)S(1)}, u32[]{:S(2)}, u32[]{:S(2)}) collective-permute-start(bf16[656,128]{1,0:T(8,128)(2,1)S(1)} %pad_maximum_fusion.4), channel_id=1, source_target_pairs={{0,128},{8,136},{16,144},{24,152},{32,160},{40,168},{48,176},{56,1... | collective-permute-start | bytes 503816 | tf_op jit(solution)/shard_map/ppermute | solution.py:15
  56.3 3.5 %collective-permute-done.4 = bf16[656,128]{1,0:T(8,128)(2,1)S(1)} collective-permute-done((bf16[656,128]{1,0:T(8,128)(2,1)S(1)}, bf16[656,128]{1,0:T(8,128)(2,1)S(1)}, u32[]{:S(2)}, u32[]{:S(2)}) %collective-permute-start.4) | collective-permute-done | bytes 167968 | tf_op jit(solution)/shard_map/ppermute | solution.py:15
  60.0 0.9 fusion.17
  60.9 1.0 copy.62
  62.6 1.0 fusion.74
  63.8 3.9 %fusion.10 = bf16[8,336,512]{2,1,0:T(8,128)(2,1)} fusion(bf16[8,320,640]{2,1,0:T(8,128)(2,1)S(1)} %bitcast.109, bf16[336,656]{1,0:T(8,128)(2,1)S(1)} %and_convert_fusion, bf16[512,3]{0,1:T(4,128)(2,1)S(1)} %fusion.74, bf16[512,640]{0,1:T(8,128)(2,1)S(1)} %get-tuple-element.95), kind=kOutput, calls=%fused_computation.13 | convolution fusion | flops 1816092672 | bytes 7128576 | tf_op jit(solution)/shard_map/gdk,tk->gdt/dot_general | solution.py:129
  67.7 4.4 %all-to-all-start = ((bf16[8,336,512]{2,1,0:T(8,128)(2,1)}), bf16[8,336,512]{2,1,0:T(8,128)(2,1)S(1)}, u32[]{:S(2)}, u32[]{:S(2)}) async-start(bf16[8,336,512]{2,1,0:T(8,128)(2,1)} %fusion.10), calls=%async_computation | async-start | bytes 5505024 | tf_op jit(solution)/shard_map/all_to_all | solution.py:132
  72.4 33.9 %all-to-all-done = bf16[8,336,512]{2,1,0:T(8,128)(2,1)S(1)} async-done(((bf16[8,336,512]{2,1,0:T(8,128)(2,1)}), bf16[8,336,512]{2,1,0:T(8,128)(2,1)S(1)}, u32[]{:S(2)}, u32[]{:S(2)}) %all-to-all-start) | async-done | bytes 2752544 | tf_op jit(solution)/shard_map/all_to_all | solution.py:132
  106.9 12.7 %all-reduce.9 = (f32[512]{0:T(512)S(1)}, f32[512]{0:T(512)S(1)}) all-reduce(f32[512]{0:T(512)S(1)} %get-tuple-element.79, f32[512]{0:T(512)S(1)} %get-tuple-element.78), channel_id=1, replica_groups=mesh['seq'=32,'head'=8] {'head'}, use_global_device_ids=true, to_apply=%region_14.15 | all-reduce | flops 1024 | bytes 8192 | tf_op jit(solution)/shard_map/psum | solution.py:153
  120.6 25.7 %all_to_all.10 = bf16[320,32,16]{0,2,1:T(8,128)(2,1)S(1)} all-to-all(bf16[320,32,16]{0,2,1:T(8,128)(2,1)S(1)} %bitcast.110), channel_id=1, replica_groups=mesh['seq'=32,'head'=8] {'seq'}, dimensions={1} | all-to-all | bytes 655360 | tf_op jit(solution)/shard_map/all_to_all | solution.py:165
  146.3 0.9 copy.66
  (118 shorter events, 9.2 us)
Async XLA Ops:
  0.6 20.5 %copy-start = (bf16[512,128]{1,0:T(8,128)(2,1)S(1)}, bf16[512,128]{1,0:T(8,128)(2,1)}, u32[]{:S(2)}) copy-start(bf16[512,128]{1,0:T(8,128)(2,1)} %param.29) | copy-start | bytes 393220
  0.6 5.2 %copy-start.3 = (bf16[512,128]{1,0:T(8,128)(2,1)S(1)}, bf16[512,128]{1,0:T(8,128)(2,1)}, u32[]{:S(2)}) copy-start(bf16[512,128]{1,0:T(8,128)(2,1)} %param.28) | copy-start | bytes 393220
  7.8 10.0 %collective-permute-start = (bf16[656,128]{1,0:T(8,128)(2,1)S(1)}, bf16[656,128]{1,0:T(8,128)(2,1)S(1)}, u32[]{:S(2)}, u32[]{:S(2)}) collective-permute-start(bf16[656,128]{1,0:T(8,128)(2,1)S(1)} %pad_maximum_fusion), channel_id=1, source_target_pairs={{0,8},{8,16},{16,24},{24,32},{32,40},{40,48},{48,56},{56,64},{64,7... | collective-permute-start | bytes 503816 | tf_op jit(solution)/shard_map/ppermute | solution.py:15
  18.1 9.7 %collective-permute-start.1 = (bf16[656,128]{1,0:T(8,128)(2,1)S(1)}, bf16[656,128]{1,0:T(8,128)(2,1)S(1)}, u32[]{:S(2)}, u32[]{:S(2)}) collective-permute-start(bf16[656,128]{1,0:T(8,128)(2,1)S(1)} %pad_maximum_fusion.1), channel_id=1, source_target_pairs={{0,16},{8,24},{16,32},{24,40},{32,48},{40,56},{48,64},{56,72},{64,... | collective-permute-start | bytes 503816 | tf_op jit(solution)/shard_map/ppermute | solution.py:15
  28.3 7.7 %collective-permute-start.2 = (bf16[656,128]{1,0:T(8,128)(2,1)S(1)}, bf16[656,128]{1,0:T(8,128)(2,1)S(1)}, u32[]{:S(2)}, u32[]{:S(2)}) collective-permute-start(bf16[656,128]{1,0:T(8,128)(2,1)S(1)} %pad_maximum_fusion.2), channel_id=1, source_target_pairs={{0,32},{8,40},{16,48},{24,56},{32,64},{40,72},{48,80},{56,88},{64,... | collective-permute-start | bytes 503816 | tf_op jit(solution)/shard_map/ppermute | solution.py:15
  36.4 16.5 %collective-permute-start.3 = (bf16[656,128]{1,0:T(8,128)(2,1)S(1)}, bf16[656,128]{1,0:T(8,128)(2,1)S(1)}, u32[]{:S(2)}, u32[]{:S(2)}) collective-permute-start(bf16[656,128]{1,0:T(8,128)(2,1)S(1)} %pad_maximum_fusion.3), channel_id=1, source_target_pairs={{0,64},{8,72},{16,80},{24,88},{32,96},{40,104},{48,112},{56,120},{... | collective-permute-start | bytes 503816 | tf_op jit(solution)/shard_map/ppermute | solution.py:15
  53.4 6.3 %collective-permute-start.4 = (bf16[656,128]{1,0:T(8,128)(2,1)S(1)}, bf16[656,128]{1,0:T(8,128)(2,1)S(1)}, u32[]{:S(2)}, u32[]{:S(2)}) collective-permute-start(bf16[656,128]{1,0:T(8,128)(2,1)S(1)} %pad_maximum_fusion.4), channel_id=1, source_target_pairs={{0,128},{8,136},{16,144},{24,152},{32,160},{40,168},{48,176},{56,1... | collective-permute-start | bytes 503816 | tf_op jit(solution)/shard_map/ppermute | solution.py:15
  55.9 4.1 %copy-start.2 = (f32[2,256,10,64]{1,3,2,0:T(8,128)S(1)}, f32[2,256,10,64]{1,3,2,0:T(8,128)}, u32[]{:S(2)}) copy-start(f32[2,256,10,64]{1,3,2,0:T(8,128)} %fusion.14) | copy-start | bytes 3932164
  55.9 4.1 %copy-start.9 = (f32[10]{0:T(128)S(1)}, f32[10]{0:T(128)}, u32[]{:S(2)}) copy-start(f32[10]{0:T(128)} %param.30) | copy-start | bytes 124
  60.9 1.1 copy-start.6
  61.9 1.9 %copy-start.1 = (bf16[640,2560]{0,1:T(8,128)(2,1)S(1)}, bf16[640,2560]{0,1:T(8,128)(2,1)}, u32[]{:S(2)}) copy-start(bf16[640,2560]{0,1:T(8,128)(2,1)} %copy.46) | copy-start | bytes 9830404
  67.7 4.4 %copy-start.8 = (s32[256]{0:T(256)S(1)}, s32[256]{0:T(256)}, u32[]{:S(2)}) copy-start(s32[256]{0:T(256)} %param.35) | copy-start | bytes 3076
  67.7 4.7 %copy-start.7 = (s32[256]{0:T(256)S(1)}, s32[256]{0:T(256)}, u32[]{:S(2)}) copy-start(s32[256]{0:T(256)} %param.34) | copy-start | bytes 3076
  67.7 38.6 %all-to-all-start = ((bf16[8,336,512]{2,1,0:T(8,128)(2,1)}), bf16[8,336,512]{2,1,0:T(8,128)(2,1)S(1)}, u32[]{:S(2)}, u32[]{:S(2)}) async-start(bf16[8,336,512]{2,1,0:T(8,128)(2,1)} %fusion.10), calls=%async_computation | async-start | bytes 5505024 | tf_op jit(solution)/shard_map/all_to_all | solution.py:132
  72.2 34.6 %copy-start.4 = (bf16[320,512]{1,0:T(8,128)(2,1)S(1)}, bf16[320,512]{1,0:T(8,128)(2,1)}, u32[]{:S(2)}) copy-start(bf16[320,512]{1,0:T(8,128)(2,1)} %param.33) | copy-start | bytes 983044
  106.9 40.3 %copy-start.5 = (bf16[320,512]{1,0:T(8,128)(2,1)}, bf16[320,512]{1,0:T(8,128)(2,1)S(1)}, u32[]{:S(2)}) copy-start(bf16[320,512]{1,0:T(8,128)(2,1)S(1)} %get-tuple-element.82) | copy-start | bytes 983044

commit v11 on v10

--- a/solution.py
+++ b/solution.py
@@ -1,7 +1,7 @@
 import jax
 import jax.numpy as jnp
 from jax import lax
-from jax.sharding import PartitionSpec as P
+from jax.sharding import Mesh, PartitionSpec as P
 
 BLOCK = 256
 
@@ -107,7 +107,7 @@
     gated = mixed * jax.nn.silu(z_gate.astype(jnp.float32))
     local_squares = jnp.sum(gated * gated, axis=-1)
     hidden = (gated * norm_weight[None, :]).astype(jnp.bfloat16)
-    groups = lax.axis_size("head")
+    groups = lax.axis_size("x") * lax.axis_size("core")
     block_rows = w_out.shape[1] // groups
     padded_w = jnp.pad(
         jnp.transpose(w_out.reshape(w_out.shape[0], groups, block_rows), (1, 2, 0)),
@@ -129,13 +129,25 @@
     sent = jnp.einsum(
         "gdk,tk->gdt", padded_w, widened, preferred_element_type=jnp.float32
     ).astype(jnp.bfloat16)
-    arrived = lax.all_to_all(sent, "head", 0, 0, tiled=False)
+    cores = lax.axis_size("core")
+    paired = lax.all_to_all(
+        sent.reshape(groups // cores, cores, block_rows + 16, rows_here), "core", 1, 1, tiled=False
+    )
+    paired = jnp.sum(paired.astype(jnp.float32), axis=1)
+    pair_squares = jnp.sum(paired[:, block_rows : block_rows + 3], axis=1)
+    pair_high = lax.reduce_precision(pair_squares, exponent_bits=8, mantissa_bits=7)
+    pair_rest = pair_squares - pair_high
+    pair_middle = lax.reduce_precision(pair_rest, exponent_bits=8, mantissa_bits=7)
+    paired = paired.at[:, block_rows : block_rows + 3].set(
+        jnp.stack([pair_high, pair_middle, pair_rest - pair_middle], axis=1)
+    )
+    arrived = lax.all_to_all(paired.astype(jnp.bfloat16), "x", 0, 0, tiled=False)
     proj = jnp.sum(arrived[:, :block_rows].astype(jnp.float32), axis=0)
     squares = jnp.sum(arrived[:, block_rows : block_rows + 3].astype(jnp.float32), axis=(0, 1))
     mean_sq = squares / (channels * groups)
     proj = proj * lax.rsqrt(mean_sq + EPS)[None, :]
     block_out = (resid.astype(jnp.float32) + proj).astype(jnp.bfloat16)
-    features = resid.shape[0] * lax.axis_size("head")
+    features = resid.shape[0] * groups
     masked_here = masked_pos.shape[0]
     slot_cap = 2 * masked_here // seq_count
     local_pos = masked_pos % rows_here
@@ -150,7 +162,7 @@
     placed = owner * slot_cap + ranks
     local_feat = resid.shape[0]
     out_wide = block_out.astype(jnp.float32)
-    totals = lax.psum((jnp.sum(out_wide, axis=0), jnp.sum(out_wide * out_wide, axis=0)), "head")
+    totals = lax.psum((jnp.sum(out_wide, axis=0), jnp.sum(out_wide * out_wide, axis=0)), ("x", "core"))
     mean_col = totals[0] / features
     variance = totals[1] / features - mean_col * mean_col
     normed = ((out_wide - mean_col[None, :]) * lax.rsqrt(variance + EPS)[None, :]).astype(
@@ -174,24 +186,28 @@
 
 
 def solution(mesh):
+    heads = mesh.shape["head"]
+    split_mesh = Mesh(
+        mesh.devices.reshape(mesh.shape["seq"], heads // 2, 2), ("seq", "x", "core")
+    )
     placed = (
-        P("seq", "head"),
-        P("seq", "head"),
-        P("head", "seq"),
-        P("head", "seq"),
+        P("seq", ("x", "core")),
+        P("seq", ("x", "core")),
+        P(("x", "core"), "seq"),
+        P(("x", "core"), "seq"),
         P("seq", None),
         P("seq", None),
-        P("head"),
-        P("head"),
-        P("head", None),
-        P("head", "seq"),
+        P(("x", "core")),
+        P(("x", "core")),
+        P(("x", "core"), None),
+        P(("x", "core"), "seq"),
         P("seq"),
         P("seq"),
     )
     return jax.shard_map(
         body,
-        mesh=mesh,
+        mesh=split_mesh,
         in_specs=placed,
-        out_specs=(P("head", "seq"), P("head", "seq")),
+        out_specs=(P(("x", "core"), "seq"), P(("x", "core"), "seq")),
         check_vma=False,
     )

time: 148 us -> 139 us (0.939)
  waiting for transfers between devices: 49.4 us -> 34.1 us
  blocking collectives: 38.4 us -> 44.4 us
  other arithmetic: 6.55 us -> 8.27 us
  matrix products: 11.6 us -> 10 us
    all_to_all x1, waiting for transfers between devices: 33.9 us -> 18.7 us  [body(): lax.all_to_all(paired.astype(jnp.bfloat16), 'x', 0, 0, tiled=False)]
    all_to_all x0 -> x1, blocking collectives: none -> 5.94 us  [body(): lax.all_to_all(sent.reshape(groups // cores, cores, block_rows + 16, rows...]
    dot_general x1, matrix products: 3.88 us -> 2.31 us  [body(): jnp.einsum('gdk,tk->gdt', padded_w, widened, preferred_element_type=jnp.f...]
    another operation x19 -> x20, other arithmetic: 4.15 us -> 4.17 us
  transfers between devices with their start and end apart: 6 -> 6, of which waited for: 4 -> 4; matrix products, arithmetic and copies ran while one was open for 9% -> 10% of each run, Pallas kernels for 0% -> 0%
where the time goes in v11:
time: 139 us
  blocking collectives  44.4 us (32%)
  waiting for transfers between devices  34.1 us (25%)
  starting transfers between devices  26 us (19%)
  local copies, waits for them, and re-layouts  14.6 us (11%)
  matrix products  10 us (7%)
  other arithmetic  8.27 us (6%)
    all_to_all x1, blocking collectives, body(): lax.all_to_all(buffer.reshape(local_feat, seq_count, slot_cap), 'seq', sp...  26 us
    ppermute x5, starting transfers between devices, from_behind(): lax.ppermute(value, axis, [(source, source + steps) for source in range(l...  21.5 us
    all_to_all x1, waiting for transfers between devices, body(): lax.all_to_all(paired.astype(jnp.bfloat16), 'x', 0, 0, tiled=False)  18.7 us
    ppermute x5, waiting for transfers between devices, from_behind(): lax.ppermute(value, axis, [(source, source + steps) for source in range(l...  15.4 us
    psum x1, blocking collectives, body(): lax.psum((jnp.sum(out_wide, axis=0), jnp.sum(out_wide * out_wide, axis=0)...  12.4 us
    unnamed x25, local copies, waits for them, and re-layouts  9.65 us
    all_to_all x1, blocking collectives, body(): lax.all_to_all(sent.reshape(groups // cores, cores, block_rows + 16, rows...  5.94 us
    all_to_all x1, starting transfers between devices, body(): lax.all_to_all(paired.astype(jnp.bfloat16), 'x', 0, 0, tiled=False)  4.43 us
  transfers between devices with their start and end apart: 6, of which 4 were waited for; matrix products, arithmetic and copies ran while one was open for 10% of the time, Pallas kernels for 0%

profile of v11, /device:TPU:32, one launch (start us, length us, event | category | flops | bytes accessed | tf_op | source)
XLA Modules:
  0.0 138.6 jit_solution(5793890819712279123)
XLA Ops:
  1.5 1.2 reduce-window.6
  4.4 1.3 copy.123
  5.9 1.2 fusion.26
  7.8 3.5 %collective-permute-start = (bf16[656,128]{1,0:T(8,128)(2,1)S(1)}, bf16[656,128]{1,0:T(8,128)(2,1)S(1)}, u32[]{:S(2)}, u32[]{:S(2)}) collective-permute-start(bf16[656,128]{1,0:T(8,128)(2,1)S(1)} %pad_maximum_fusion), channel_id=1, source_target_pairs={{0,8},{8,16},{16,24},{24,32},{32,40},{40,48},{48,56},{56,64},{64,7... | collective-permute-start | bytes 503816 | tf_op jit(solution)/shard_map/ppermute | solution.py:15
  11.4 6.4 %collective-permute-done = bf16[656,128]{1,0:T(8,128)(2,1)S(1)} collective-permute-done((bf16[656,128]{1,0:T(8,128)(2,1)S(1)}, bf16[656,128]{1,0:T(8,128)(2,1)S(1)}, u32[]{:S(2)}, u32[]{:S(2)}) %collective-permute-start) | collective-permute-done | bytes 167968 | tf_op jit(solution)/shard_map/ppermute | solution.py:15
  18.1 3.0 %collective-permute-start.1 = (bf16[656,128]{1,0:T(8,128)(2,1)S(1)}, bf16[656,128]{1,0:T(8,128)(2,1)S(1)}, u32[]{:S(2)}, u32[]{:S(2)}) collective-permute-start(bf16[656,128]{1,0:T(8,128)(2,1)S(1)} %pad_maximum_fusion.1), channel_id=1, source_target_pairs={{0,16},{8,24},{16,32},{24,40},{32,48},{40,56},{48,64},{56,72},{64,... | collective-permute-start | bytes 503816 | tf_op jit(solution)/shard_map/ppermute | solution.py:15
  21.1 1.0 fusion.118
  22.2 5.6 %collective-permute-done.1 = bf16[656,128]{1,0:T(8,128)(2,1)S(1)} collective-permute-done((bf16[656,128]{1,0:T(8,128)(2,1)S(1)}, bf16[656,128]{1,0:T(8,128)(2,1)S(1)}, u32[]{:S(2)}, u32[]{:S(2)}) %collective-permute-start.1) | collective-permute-done | bytes 167968 | tf_op jit(solution)/shard_map/ppermute | solution.py:15
  28.3 3.8 %collective-permute-start.2 = (bf16[656,128]{1,0:T(8,128)(2,1)S(1)}, bf16[656,128]{1,0:T(8,128)(2,1)S(1)}, u32[]{:S(2)}, u32[]{:S(2)}) collective-permute-start(bf16[656,128]{1,0:T(8,128)(2,1)S(1)} %pad_maximum_fusion.2), channel_id=1, source_target_pairs={{0,32},{8,40},{16,48},{24,56},{32,64},{40,72},{48,80},{56,88},{64,... | collective-permute-start | bytes 503816 | tf_op jit(solution)/shard_map/ppermute | solution.py:15
  32.1 3.7 %fusion.14 = f32[2,256,10,64]{1,3,2,0:T(8,128)} fusion(f32[10,2,256]{2,0,1:T(8,128)S(1)} %copy.122, f32[10,2,256]{2,0,1:T(8,128)S(1)} %copy.120, f32[2,256,256]{2,1,0:T(8,128)} %fusion.118, pred[256,256]{1,0:T(8,128)(4,1)S(1)} %iota_compare_fusion.8, bf16[2,256,10,64]{1,0,3,2:T(2,128)(2,1)S(1)} %reshape.802), kind=kOutput, calls=%fused_computation.18 | convolution fusion | flops 175636480 | bytes 2596864 | tf_op jit(solution)/shard_map/hcts,cshp->cthp/dot_general | solution.py:48
  36.4 8.8 %collective-permute-start.3 = (bf16[656,128]{1,0:T(8,128)(2,1)S(1)}, bf16[656,128]{1,0:T(8,128)(2,1)S(1)}, u32[]{:S(2)}, u32[]{:S(2)}) collective-permute-start(bf16[656,128]{1,0:T(8,128)(2,1)S(1)} %pad_maximum_fusion.3), channel_id=1, source_target_pairs={{0,64},{8,72},{16,80},{24,88},{32,96},{40,104},{48,112},{56,120},{... | collective-permute-start | bytes 503816 | tf_op jit(solution)/shard_map/ppermute | solution.py:15
  45.3 1.3 copy.132
  46.6 5.7 %copy.115 = bf16[640,2560]{0,1:T(8,128)(2,1)} copy(bf16[640,2560]{1,0:T(8,128)(2,1)} %param.34) | data formatting | bytes 6553600 | tf_op args[8]
  53.4 2.4 %collective-permute-start.4 = (bf16[656,128]{1,0:T(8,128)(2,1)S(1)}, bf16[656,128]{1,0:T(8,128)(2,1)S(1)}, u32[]{:S(2)}, u32[]{:S(2)}) collective-permute-start(bf16[656,128]{1,0:T(8,128)(2,1)S(1)} %pad_maximum_fusion.4), channel_id=1, source_target_pairs={{0,128},{8,136},{16,144},{24,152},{32,160},{40,168},{48,176},{56,1... | collective-permute-start | bytes 503816 | tf_op jit(solution)/shard_map/ppermute | solution.py:15
  56.3 3.5 %collective-permute-done.4 = bf16[656,128]{1,0:T(8,128)(2,1)S(1)} collective-permute-done((bf16[656,128]{1,0:T(8,128)(2,1)S(1)}, bf16[656,128]{1,0:T(8,128)(2,1)S(1)}, u32[]{:S(2)}, u32[]{:S(2)}) %collective-permute-start.4) | collective-permute-done | bytes 167968 | tf_op jit(solution)/shard_map/ppermute | solution.py:15
  60.9 1.0 copy.131
  62.6 1.0 fusion.74
  63.8 2.3 %fusion.10 = bf16[8,336,512]{2,1,0:T(8,128)(2,1)S(1)} fusion(bf16[8,320,640]{2,1,0:T(8,128)(2,1)S(1)} %bitcast.110, bf16[336,656]{1,0:T(8,128)(2,1)S(1)} %and_convert_fusion, bf16[512,3]{0,1:T(4,128)(2,1)S(1)} %fusion.74, bf16[512,640]{0,1:T(8,128)(2,1)S(1)} %get-tuple-element.113), kind=kOutput, calls=%fused_computation.14 | convolution fusion | flops 1816092672 | bytes 7128576 | tf_op jit(solution)/shard_map/gdk,tk->gdt/dot_general | solution.py:129
  66.4 5.9 %all_to_all.15 = bf16[4,2,336,512]{3,2,0,1:T(8,128)(2,1)S(1)} all-to-all(bf16[4,2,336,512]{3,2,0,1:T(8,128)(2,1)S(1)} %copy.134), channel_id=1, replica_groups=mesh['seq'=32,'x'=4,'core'=2] {'core'}, dimensions={1} | all-to-all | bytes 5505024 | tf_op jit(solution)/shard_map/all_to_all | solution.py:133
  73.2 1.3 convert_element_type.110
  74.5 4.4 %all-to-all-start.1 = ((bf16[4,336,512]{2,1,0:T(8,128)(2,1)}), bf16[4,336,512]{2,1,0:T(8,128)(2,1)S(1)}, u32[]{:S(2)}, u32[]{:S(2)}) async-start(bf16[4,336,512]{2,1,0:T(8,128)(2,1)} %convert_element_type.110), calls=%async_computation.1 | async-start | bytes 2752512 | tf_op jit(solution)/shard_map/all_to_all | solution.py:144
  79.2 18.7 %all-to-all-done.1 = bf16[4,336,512]{2,1,0:T(8,128)(2,1)S(1)} async-done(((bf16[4,336,512]{2,1,0:T(8,128)(2,1)}), bf16[4,336,512]{2,1,0:T(8,128)(2,1)S(1)}, u32[]{:S(2)}, u32[]{:S(2)}) %all-to-all-start.1) | async-done | bytes 1376288 | tf_op jit(solution)/shard_map/all_to_all | solution.py:144
  98.3 12.4 %all-reduce.9 = (f32[512]{0:T(512)S(1)}, f32[512]{0:T(512)S(1)}) all-reduce(f32[512]{0:T(512)S(1)} %get-tuple-element.97, f32[512]{0:T(512)S(1)} %get-tuple-element.96), channel_id=1, replica_groups=mesh['seq'=32,'x'=4,'core'=2] {'x','core'}, use_global_device_ids=true, to_apply=%region_16.17 | all-reduce | flops 1024 | bytes 8192 | tf_op jit(solution)/shard_map/psum | solution.py:165
  111.6 26.0 %all_to_all.16 = bf16[320,32,16]{0,2,1:T(8,128)(2,1)S(1)} all-to-all(bf16[320,32,16]{0,2,1:T(8,128)(2,1)S(1)} %bitcast.112), channel_id=1, replica_groups=mesh['seq'=32,'x'=4,'core'=2] {'seq'}, dimensions={1} | all-to-all | bytes 655360 | tf_op jit(solution)/shard_map/all_to_all | solution.py:177
  (127 shorter events, 11.9 us)
Async XLA Ops:
  0.6 20.5 %copy-start = (bf16[512,128]{1,0:T(8,128)(2,1)S(1)}, bf16[512,128]{1,0:T(8,128)(2,1)}, u32[]{:S(2)}) copy-start(bf16[512,128]{1,0:T(8,128)(2,1)} %param.31) | copy-start | bytes 393220
  0.6 5.2 %copy-start.3 = (bf16[512,128]{1,0:T(8,128)(2,1)S(1)}, bf16[512,128]{1,0:T(8,128)(2,1)}, u32[]{:S(2)}) copy-start(bf16[512,128]{1,0:T(8,128)(2,1)} %param.30) | copy-start | bytes 393220
  7.8 10.0 %collective-permute-start = (bf16[656,128]{1,0:T(8,128)(2,1)S(1)}, bf16[656,128]{1,0:T(8,128)(2,1)S(1)}, u32[]{:S(2)}, u32[]{:S(2)}) collective-permute-start(bf16[656,128]{1,0:T(8,128)(2,1)S(1)} %pad_maximum_fusion), channel_id=1, source_target_pairs={{0,8},{8,16},{16,24},{24,32},{32,40},{40,48},{48,56},{56,64},{64,7... | collective-permute-start | bytes 503816 | tf_op jit(solution)/shard_map/ppermute | solution.py:15
  18.1 9.7 %collective-permute-start.1 = (bf16[656,128]{1,0:T(8,128)(2,1)S(1)}, bf16[656,128]{1,0:T(8,128)(2,1)S(1)}, u32[]{:S(2)}, u32[]{:S(2)}) collective-permute-start(bf16[656,128]{1,0:T(8,128)(2,1)S(1)} %pad_maximum_fusion.1), channel_id=1, source_target_pairs={{0,16},{8,24},{16,32},{24,40},{32,48},{40,56},{48,64},{56,72},{64,... | collective-permute-start | bytes 503816 | tf_op jit(solution)/shard_map/ppermute | solution.py:15
  28.3 7.7 %collective-permute-start.2 = (bf16[656,128]{1,0:T(8,128)(2,1)S(1)}, bf16[656,128]{1,0:T(8,128)(2,1)S(1)}, u32[]{:S(2)}, u32[]{:S(2)}) collective-permute-start(bf16[656,128]{1,0:T(8,128)(2,1)S(1)} %pad_maximum_fusion.2), channel_id=1, source_target_pairs={{0,32},{8,40},{16,48},{24,56},{32,64},{40,72},{48,80},{56,88},{64,... | collective-permute-start | bytes 503816 | tf_op jit(solution)/shard_map/ppermute | solution.py:15
  36.4 16.5 %collective-permute-start.3 = (bf16[656,128]{1,0:T(8,128)(2,1)S(1)}, bf16[656,128]{1,0:T(8,128)(2,1)S(1)}, u32[]{:S(2)}, u32[]{:S(2)}) collective-permute-start(bf16[656,128]{1,0:T(8,128)(2,1)S(1)} %pad_maximum_fusion.3), channel_id=1, source_target_pairs={{0,64},{8,72},{16,80},{24,88},{32,96},{40,104},{48,112},{56,120},{... | collective-permute-start | bytes 503816 | tf_op jit(solution)/shard_map/ppermute | solution.py:15
  53.4 6.3 %collective-permute-start.4 = (bf16[656,128]{1,0:T(8,128)(2,1)S(1)}, bf16[656,128]{1,0:T(8,128)(2,1)S(1)}, u32[]{:S(2)}, u32[]{:S(2)}) collective-permute-start(bf16[656,128]{1,0:T(8,128)(2,1)S(1)} %pad_maximum_fusion.4), channel_id=1, source_target_pairs={{0,128},{8,136},{16,144},{24,152},{32,160},{40,168},{48,176},{56,1... | collective-permute-start | bytes 503816 | tf_op jit(solution)/shard_map/ppermute | solution.py:15
  55.9 4.1 %copy-start.2 = (f32[2,256,10,64]{1,3,2,0:T(8,128)S(1)}, f32[2,256,10,64]{1,3,2,0:T(8,128)}, u32[]{:S(2)}) copy-start(f32[2,256,10,64]{1,3,2,0:T(8,128)} %fusion.14) | copy-start | bytes 3932164
  55.9 4.1 %copy-start.9 = (f32[10]{0:T(128)S(1)}, f32[10]{0:T(128)}, u32[]{:S(2)}) copy-start(f32[10]{0:T(128)} %param.32) | copy-start | bytes 124
  60.9 1.1 copy-start.6
  61.9 1.9 %copy-start.1 = (bf16[640,2560]{0,1:T(8,128)(2,1)S(1)}, bf16[640,2560]{0,1:T(8,128)(2,1)}, u32[]{:S(2)}) copy-start(bf16[640,2560]{0,1:T(8,128)(2,1)} %copy.115) | copy-start | bytes 9830404
  73.2 5.7 %copy-start.8 = (s32[256]{0:T(256)S(1)}, s32[256]{0:T(256)}, u32[]{:S(2)}) copy-start(s32[256]{0:T(256)} %param.37) | copy-start | bytes 3076
  73.2 5.9 %copy-start.7 = (s32[256]{0:T(256)S(1)}, s32[256]{0:T(256)}, u32[]{:S(2)}) copy-start(s32[256]{0:T(256)} %param.36) | copy-start | bytes 3076
  74.5 23.6 %copy-start.4 = (bf16[320,512]{1,0:T(8,128)(2,1)S(1)}, bf16[320,512]{1,0:T(8,128)(2,1)}, u32[]{:S(2)}) copy-start(bf16[320,512]{1,0:T(8,128)(2,1)} %param.35) | copy-start | bytes 983044
  74.5 23.3 %all-to-all-start.1 = ((bf16[4,336,512]{2,1,0:T(8,128)(2,1)}), bf16[4,336,512]{2,1,0:T(8,128)(2,1)S(1)}, u32[]{:S(2)}, u32[]{:S(2)}) async-start(bf16[4,336,512]{2,1,0:T(8,128)(2,1)} %convert_element_type.110), calls=%async_computation.1 | async-start | bytes 2752512 | tf_op jit(solution)/shard_map/all_to_all | solution.py:144
  98.3 40.3 %copy-start.5 = (bf16[320,512]{1,0:T(8,128)(2,1)}, bf16[320,512]{1,0:T(8,128)(2,1)S(1)}, u32[]{:S(2)}) copy-start(bf16[320,512]{1,0:T(8,128)(2,1)S(1)} %get-tuple-element.100) | copy-start | bytes 983044

commit v12 on v11

--- a/solution.py
+++ b/solution.py
@@ -162,7 +162,9 @@
     placed = owner * slot_cap + ranks
     local_feat = resid.shape[0]
     out_wide = block_out.astype(jnp.float32)
-    totals = lax.psum((jnp.sum(out_wide, axis=0), jnp.sum(out_wide * out_wide, axis=0)), ("x", "core"))
+    totals = lax.psum(
+        lax.psum((jnp.sum(out_wide, axis=0), jnp.sum(out_wide * out_wide, axis=0)), "core"), "x"
+    )
     mean_col = totals[0] / features
     variance = totals[1] / features - mean_col * mean_col
     normed = ((out_wide - mean_col[None, :]) * lax.rsqrt(variance + EPS)[None, :]).astype(

time: 139 us -> 137 us (0.986)
  blocking collectives: 44.4 us -> 41.6 us
    psum x1, blocking collectives: 12.4 us -> 2.47 us  [body(): lax.psum((jnp.sum(out_wide, axis=0), jnp.sum(out_wide * out_wide, axis=0)...]
    psum x0 -> x1, blocking collectives: none -> 8.87 us  [body(): lax.psum(lax.psum((jnp.sum(out_wide, axis=0), jnp.sum(out_wide * out_wide...]
    all_to_all x1, blocking collectives: 26 us -> 24.3 us  [body(): lax.all_to_all(buffer.reshape(local_feat, seq_count, slot_cap), 'seq', sp...]
where the time goes in v12:
time: 137 us; the launch traced here: 136 us
  blocking collectives  41.6 us (30%)
  waiting for transfers between devices  34.1 us (25%)
  starting transfers between devices  26 us (19%)
  local copies, waits for them, and re-layouts  14.6 us (11%)
  matrix products  10 us (7%)
  other arithmetic  8.27 us (6%)
    all_to_all x1, blocking collectives, body(): lax.all_to_all(buffer.reshape(local_feat, seq_count, slot_cap), 'seq', sp...  24.3 us
    ppermute x5, starting transfers between devices, from_behind(): lax.ppermute(value, axis, [(source, source + steps) for source in range(l...  21.5 us
    all_to_all x1, waiting for transfers between devices, body(): lax.all_to_all(paired.astype(jnp.bfloat16), 'x', 0, 0, tiled=False)  18.7 us
    ppermute x5, waiting for transfers between devices, from_behind(): lax.ppermute(value, axis, [(source, source + steps) for source in range(l...  15.4 us
    unnamed x25, local copies, waits for them, and re-layouts  9.65 us
    psum x1, blocking collectives, body(): lax.psum(lax.psum((jnp.sum(out_wide, axis=0), jnp.sum(out_wide * out_wide...  8.87 us
    all_to_all x1, blocking collectives, body(): lax.all_to_all(sent.reshape(groups // cores, cores, block_rows + 16, rows...  5.94 us
    all_to_all x1, starting transfers between devices, body(): lax.all_to_all(paired.astype(jnp.bfloat16), 'x', 0, 0, tiled=False)  4.43 us
  transfers between devices with their start and end apart: 6, of which 4 were waited for; matrix products, arithmetic and copies ran while one was open for 10% of the time, Pallas kernels for 0%

profile of v12, /device:TPU:32, one launch (start us, length us, event | category | flops | bytes accessed | tf_op | source)
XLA Modules:
  0.0 135.8 jit_solution(7556171215490367218)
XLA Ops:
  1.5 1.2 reduce-window.6
  4.4 1.3 copy.123
  5.9 1.2 fusion.26
  7.8 3.5 %collective-permute-start = (bf16[656,128]{1,0:T(8,128)(2,1)S(1)}, bf16[656,128]{1,0:T(8,128)(2,1)S(1)}, u32[]{:S(2)}, u32[]{:S(2)}) collective-permute-start(bf16[656,128]{1,0:T(8,128)(2,1)S(1)} %pad_maximum_fusion), channel_id=1, source_target_pairs={{0,8},{8,16},{16,24},{24,32},{32,40},{40,48},{48,56},{56,64},{64,7... | collective-permute-start | bytes 503816 | tf_op jit(solution)/shard_map/ppermute | solution.py:15
  11.4 6.4 %collective-permute-done = bf16[656,128]{1,0:T(8,128)(2,1)S(1)} collective-permute-done((bf16[656,128]{1,0:T(8,128)(2,1)S(1)}, bf16[656,128]{1,0:T(8,128)(2,1)S(1)}, u32[]{:S(2)}, u32[]{:S(2)}) %collective-permute-start) | collective-permute-done | bytes 167968 | tf_op jit(solution)/shard_map/ppermute | solution.py:15
  18.1 3.0 %collective-permute-start.1 = (bf16[656,128]{1,0:T(8,128)(2,1)S(1)}, bf16[656,128]{1,0:T(8,128)(2,1)S(1)}, u32[]{:S(2)}, u32[]{:S(2)}) collective-permute-start(bf16[656,128]{1,0:T(8,128)(2,1)S(1)} %pad_maximum_fusion.1), channel_id=1, source_target_pairs={{0,16},{8,24},{16,32},{24,40},{32,48},{40,56},{48,64},{56,72},{64,... | collective-permute-start | bytes 503816 | tf_op jit(solution)/shard_map/ppermute | solution.py:15
  21.1 1.0 fusion.118
  22.2 5.6 %collective-permute-done.1 = bf16[656,128]{1,0:T(8,128)(2,1)S(1)} collective-permute-done((bf16[656,128]{1,0:T(8,128)(2,1)S(1)}, bf16[656,128]{1,0:T(8,128)(2,1)S(1)}, u32[]{:S(2)}, u32[]{:S(2)}) %collective-permute-start.1) | collective-permute-done | bytes 167968 | tf_op jit(solution)/shard_map/ppermute | solution.py:15
  28.3 3.8 %collective-permute-start.2 = (bf16[656,128]{1,0:T(8,128)(2,1)S(1)}, bf16[656,128]{1,0:T(8,128)(2,1)S(1)}, u32[]{:S(2)}, u32[]{:S(2)}) collective-permute-start(bf16[656,128]{1,0:T(8,128)(2,1)S(1)} %pad_maximum_fusion.2), channel_id=1, source_target_pairs={{0,32},{8,40},{16,48},{24,56},{32,64},{40,72},{48,80},{56,88},{64,... | collective-permute-start | bytes 503816 | tf_op jit(solution)/shard_map/ppermute | solution.py:15
  32.1 3.7 %fusion.14 = f32[2,256,10,64]{1,3,2,0:T(8,128)} fusion(f32[10,2,256]{2,0,1:T(8,128)S(1)} %copy.122, f32[10,2,256]{2,0,1:T(8,128)S(1)} %copy.120, f32[2,256,256]{2,1,0:T(8,128)} %fusion.118, pred[256,256]{1,0:T(8,128)(4,1)S(1)} %iota_compare_fusion.8, bf16[2,256,10,64]{1,0,3,2:T(2,128)(2,1)S(1)} %reshape.802), kind=kOutput, calls=%fused_computation.18 | convolution fusion | flops 175636480 | bytes 2596864 | tf_op jit(solution)/shard_map/hcts,cshp->cthp/dot_general | solution.py:48
  36.4 8.8 %collective-permute-start.3 = (bf16[656,128]{1,0:T(8,128)(2,1)S(1)}, bf16[656,128]{1,0:T(8,128)(2,1)S(1)}, u32[]{:S(2)}, u32[]{:S(2)}) collective-permute-start(bf16[656,128]{1,0:T(8,128)(2,1)S(1)} %pad_maximum_fusion.3), channel_id=1, source_target_pairs={{0,64},{8,72},{16,80},{24,88},{32,96},{40,104},{48,112},{56,120},{... | collective-permute-start | bytes 503816 | tf_op jit(solution)/shard_map/ppermute | solution.py:15
  45.3 1.3 copy.132
  46.6 5.7 %copy.115 = bf16[640,2560]{0,1:T(8,128)(2,1)} copy(bf16[640,2560]{1,0:T(8,128)(2,1)} %param.34) | data formatting | bytes 6553600 | tf_op args[8]
  53.4 2.4 %collective-permute-start.4 = (bf16[656,128]{1,0:T(8,128)(2,1)S(1)}, bf16[656,128]{1,0:T(8,128)(2,1)S(1)}, u32[]{:S(2)}, u32[]{:S(2)}) collective-permute-start(bf16[656,128]{1,0:T(8,128)(2,1)S(1)} %pad_maximum_fusion.4), channel_id=1, source_target_pairs={{0,128},{8,136},{16,144},{24,152},{32,160},{40,168},{48,176},{56,1... | collective-permute-start | bytes 503816 | tf_op jit(solution)/shard_map/ppermute | solution.py:15
  56.3 3.5 %collective-permute-done.4 = bf16[656,128]{1,0:T(8,128)(2,1)S(1)} collective-permute-done((bf16[656,128]{1,0:T(8,128)(2,1)S(1)}, bf16[656,128]{1,0:T(8,128)(2,1)S(1)}, u32[]{:S(2)}, u32[]{:S(2)}) %collective-permute-start.4) | collective-permute-done | bytes 167968 | tf_op jit(solution)/shard_map/ppermute | solution.py:15
  60.9 1.0 copy.131
  63.8 2.3 %fusion.10 = bf16[8,336,512]{2,1,0:T(8,128)(2,1)S(1)} fusion(bf16[8,320,640]{2,1,0:T(8,128)(2,1)S(1)} %bitcast.110, bf16[336,656]{1,0:T(8,128)(2,1)S(1)} %and_convert_fusion, bf16[512,3]{0,1:T(4,128)(2,1)S(1)} %fusion.74, bf16[512,640]{0,1:T(8,128)(2,1)S(1)} %get-tuple-element.115), kind=kOutput, calls=%fused_computation.14 | convolution fusion | flops 1816092672 | bytes 7128576 | tf_op jit(solution)/shard_map/gdk,tk->gdt/dot_general | solution.py:129
  66.4 5.9 %all_to_all.15 = bf16[4,2,336,512]{3,2,0,1:T(8,128)(2,1)S(1)} all-to-all(bf16[4,2,336,512]{3,2,0,1:T(8,128)(2,1)S(1)} %copy.134), channel_id=1, replica_groups=mesh['seq'=32,'x'=4,'core'=2] {'core'}, dimensions={1} | all-to-all | bytes 5505024 | tf_op jit(solution)/shard_map/all_to_all | solution.py:133
  73.2 1.3 convert_element_type.110
  74.5 4.4 %all-to-all-start.1 = ((bf16[4,336,512]{2,1,0:T(8,128)(2,1)}), bf16[4,336,512]{2,1,0:T(8,128)(2,1)S(1)}, u32[]{:S(2)}, u32[]{:S(2)}) async-start(bf16[4,336,512]{2,1,0:T(8,128)(2,1)} %convert_element_type.110), calls=%async_computation.1 | async-start | bytes 2752512 | tf_op jit(solution)/shard_map/all_to_all | solution.py:144
  79.2 18.7 %all-to-all-done.1 = bf16[4,336,512]{2,1,0:T(8,128)(2,1)S(1)} async-done(((bf16[4,336,512]{2,1,0:T(8,128)(2,1)}), bf16[4,336,512]{2,1,0:T(8,128)(2,1)S(1)}, u32[]{:S(2)}, u32[]{:S(2)}) %all-to-all-start.1) | async-done | bytes 1376288 | tf_op jit(solution)/shard_map/all_to_all | solution.py:144
  98.3 2.5 %all-reduce.10 = (f32[512]{0:T(512)S(1)}, f32[512]{0:T(512)S(1)}) all-reduce(f32[512]{0:T(512)S(1)} %get-tuple-element.97, f32[512]{0:T(512)S(1)} %get-tuple-element.96), channel_id=1, replica_groups=mesh['seq'=32,'x'=4,'core'=2] {'core'}, use_global_device_ids=true, to_apply=%region_17.18 | all-reduce | flops 1024 | bytes 8192 | tf_op jit(solution)/shard_map/psum | solution.py:166
  100.8 8.9 %all-reduce.9 = (f32[512]{0:T(512)S(1)}, f32[512]{0:T(512)S(1)}) all-reduce(f32[512]{0:T(512)S(1)} %get-tuple-element.100, f32[512]{0:T(512)S(1)} %get-tuple-element.101), channel_id=1, replica_groups=mesh['seq'=32,'x'=4,'core'=2] {'x'}, use_global_device_ids=true, to_apply=%region_18.19 | all-reduce | flops 1024 | bytes 8192 | tf_op jit(solution)/shard_map/psum | solution.py:165
  110.6 24.3 %all_to_all.16 = bf16[320,32,16]{0,2,1:T(8,128)(2,1)S(1)} all-to-all(bf16[320,32,16]{0,2,1:T(8,128)(2,1)S(1)} %bitcast.112), channel_id=1, replica_groups=mesh['seq'=32,'x'=4,'core'=2] {'seq'}, dimensions={1} | all-to-all | bytes 655360 | tf_op jit(solution)/shard_map/all_to_all | solution.py:179
  (128 shorter events, 12.8 us)
Async XLA Ops:
  0.6 20.5 %copy-start = (bf16[512,128]{1,0:T(8,128)(2,1)S(1)}, bf16[512,128]{1,0:T(8,128)(2,1)}, u32[]{:S(2)}) copy-start(bf16[512,128]{1,0:T(8,128)(2,1)} %param.31) | copy-start | bytes 393220
  0.6 5.2 %copy-start.3 = (bf16[512,128]{1,0:T(8,128)(2,1)S(1)}, bf16[512,128]{1,0:T(8,128)(2,1)}, u32[]{:S(2)}) copy-start(bf16[512,128]{1,0:T(8,128)(2,1)} %param.30) | copy-start | bytes 393220
  7.8 10.0 %collective-permute-start = (bf16[656,128]{1,0:T(8,128)(2,1)S(1)}, bf16[656,128]{1,0:T(8,128)(2,1)S(1)}, u32[]{:S(2)}, u32[]{:S(2)}) collective-permute-start(bf16[656,128]{1,0:T(8,128)(2,1)S(1)} %pad_maximum_fusion), channel_id=1, source_target_pairs={{0,8},{8,16},{16,24},{24,32},{32,40},{40,48},{48,56},{56,64},{64,7... | collective-permute-start | bytes 503816 | tf_op jit(solution)/shard_map/ppermute | solution.py:15
  18.1 9.7 %collective-permute-start.1 = (bf16[656,128]{1,0:T(8,128)(2,1)S(1)}, bf16[656,128]{1,0:T(8,128)(2,1)S(1)}, u32[]{:S(2)}, u32[]{:S(2)}) collective-permute-start(bf16[656,128]{1,0:T(8,128)(2,1)S(1)} %pad_maximum_fusion.1), channel_id=1, source_target_pairs={{0,16},{8,24},{16,32},{24,40},{32,48},{40,56},{48,64},{56,72},{64,... | collective-permute-start | bytes 503816 | tf_op jit(solution)/shard_map/ppermute | solution.py:15
  28.3 7.7 %collective-permute-start.2 = (bf16[656,128]{1,0:T(8,128)(2,1)S(1)}, bf16[656,128]{1,0:T(8,128)(2,1)S(1)}, u32[]{:S(2)}, u32[]{:S(2)}) collective-permute-start(bf16[656,128]{1,0:T(8,128)(2,1)S(1)} %pad_maximum_fusion.2), channel_id=1, source_target_pairs={{0,32},{8,40},{16,48},{24,56},{32,64},{40,72},{48,80},{56,88},{64,... | collective-permute-start | bytes 503816 | tf_op jit(solution)/shard_map/ppermute | solution.py:15
  36.4 16.5 %collective-permute-start.3 = (bf16[656,128]{1,0:T(8,128)(2,1)S(1)}, bf16[656,128]{1,0:T(8,128)(2,1)S(1)}, u32[]{:S(2)}, u32[]{:S(2)}) collective-permute-start(bf16[656,128]{1,0:T(8,128)(2,1)S(1)} %pad_maximum_fusion.3), channel_id=1, source_target_pairs={{0,64},{8,72},{16,80},{24,88},{32,96},{40,104},{48,112},{56,120},{... | collective-permute-start | bytes 503816 | tf_op jit(solution)/shard_map/ppermute | solution.py:15
  53.4 6.3 %collective-permute-start.4 = (bf16[656,128]{1,0:T(8,128)(2,1)S(1)}, bf16[656,128]{1,0:T(8,128)(2,1)S(1)}, u32[]{:S(2)}, u32[]{:S(2)}) collective-permute-start(bf16[656,128]{1,0:T(8,128)(2,1)S(1)} %pad_maximum_fusion.4), channel_id=1, source_target_pairs={{0,128},{8,136},{16,144},{24,152},{32,160},{40,168},{48,176},{56,1... | collective-permute-start | bytes 503816 | tf_op jit(solution)/shard_map/ppermute | solution.py:15
  55.9 4.1 %copy-start.2 = (f32[2,256,10,64]{1,3,2,0:T(8,128)S(1)}, f32[2,256,10,64]{1,3,2,0:T(8,128)}, u32[]{:S(2)}) copy-start(f32[2,256,10,64]{1,3,2,0:T(8,128)} %fusion.14) | copy-start | bytes 3932164
  55.9 4.1 %copy-start.9 = (f32[10]{0:T(128)S(1)}, f32[10]{0:T(128)}, u32[]{:S(2)}) copy-start(f32[10]{0:T(128)} %param.32) | copy-start | bytes 124
  60.9 1.1 copy-start.6
  61.9 1.9 %copy-start.1 = (bf16[640,2560]{0,1:T(8,128)(2,1)S(1)}, bf16[640,2560]{0,1:T(8,128)(2,1)}, u32[]{:S(2)}) copy-start(bf16[640,2560]{0,1:T(8,128)(2,1)} %copy.115) | copy-start | bytes 9830404
  73.2 5.7 %copy-start.8 = (s32[256]{0:T(256)S(1)}, s32[256]{0:T(256)}, u32[]{:S(2)}) copy-start(s32[256]{0:T(256)} %param.37) | copy-start | bytes 3076
  73.2 5.9 %copy-start.7 = (s32[256]{0:T(256)S(1)}, s32[256]{0:T(256)}, u32[]{:S(2)}) copy-start(s32[256]{0:T(256)} %param.36) | copy-start | bytes 3076
  74.5 23.6 %copy-start.4 = (bf16[320,512]{1,0:T(8,128)(2,1)S(1)}, bf16[320,512]{1,0:T(8,128)(2,1)}, u32[]{:S(2)}) copy-start(bf16[320,512]{1,0:T(8,128)(2,1)} %param.35) | copy-start | bytes 983044
  74.5 23.3 %all-to-all-start.1 = ((bf16[4,336,512]{2,1,0:T(8,128)(2,1)}), bf16[4,336,512]{2,1,0:T(8,128)(2,1)S(1)}, u32[]{:S(2)}, u32[]{:S(2)}) async-start(bf16[4,336,512]{2,1,0:T(8,128)(2,1)} %convert_element_type.110), calls=%async_computation.1 | async-start | bytes 2752512 | tf_op jit(solution)/shard_map/all_to_all | solution.py:144
  98.3 37.5 %copy-start.5 = (bf16[320,512]{1,0:T(8,128)(2,1)}, bf16[320,512]{1,0:T(8,128)(2,1)S(1)}, u32[]{:S(2)}) copy-start(bf16[320,512]{1,0:T(8,128)(2,1)S(1)} %get-tuple-element.102) | copy-start | bytes 983044

commit v13 on v12

--- a/solution.py
+++ b/solution.py
@@ -126,14 +126,19 @@
         jnp.stack([high, middle, rest - middle], axis=1)
     )
     widened = jnp.concatenate([hidden, parts.astype(jnp.bfloat16)], axis=1)
-    sent = jnp.einsum(
-        "gdk,tk->gdt", padded_w, widened, preferred_element_type=jnp.float32
+    cores = lax.axis_size("core")
+    core = lax.axis_index("core")
+    by_core = padded_w.reshape(groups // cores, cores, block_rows + 16, channels + 16)
+    other_w = lax.dynamic_index_in_dim(by_core, cores - 1 - core, axis=1, keepdims=False)
+    own_w = lax.dynamic_index_in_dim(by_core, core, axis=1, keepdims=False)
+    to_partner = jnp.einsum(
+        "gdk,tk->gdt", other_w, widened, preferred_element_type=jnp.float32
     ).astype(jnp.bfloat16)
-    cores = lax.axis_size("core")
-    paired = lax.all_to_all(
-        sent.reshape(groups // cores, cores, block_rows + 16, rows_here), "core", 1, 1, tiled=False
-    )
-    paired = jnp.sum(paired.astype(jnp.float32), axis=1)
+    from_partner = lax.ppermute(to_partner, "core", [(0, 1), (1, 0)])
+    own_part = jnp.einsum(
+        "gdk,tk->gdt", own_w, widened, preferred_element_type=jnp.float32
+    ).astype(jnp.bfloat16)
+    paired = own_part.astype(jnp.float32) + from_partner.astype(jnp.float32)
     pair_squares = jnp.sum(paired[:, block_rows : block_rows + 3], axis=1)
     pair_high = lax.reduce_precision(pair_squares, exponent_bits=8, mantissa_bits=7)
     pair_rest = pair_squares - pair_high

time: 137 us -> 150 us (1.095)
  blocking collectives: 41.6 us -> 31.3 us
  other arithmetic: 8.27 us -> 17.1 us
  local copies, waits for them, and re-layouts: 14.6 us -> 23 us
  starting transfers between devices: 26 us -> 31.5 us
    add x0 -> x1, local copies, waits for them, and re-layouts: none -> 6.31 us  [body(): padded_w = padded_w + marker.astype(jnp.bfloat16)[None]]
    all_to_all x1 -> x0, blocking collectives: 5.94 us -> none  [body(): lax.all_to_all(sent.reshape(groups // cores, cores, block_rows + 16, rows...]
    ppermute x5, starting transfers between devices: 21.5 us -> 26.8 us  [from_behind(): lax.ppermute(value, axis, [(source, source + steps) for source in range(l...]
    all_to_all x1, blocking collectives: 24.3 us -> 20 us  [body(): lax.all_to_all(buffer.reshape(local_feat, seq_count, slot_cap), 'seq', sp...]
    ppermute x5, waiting for transfers between devices: 15.4 us -> 11.7 us  [from_behind(): lax.ppermute(value, axis, [(source, source + steps) for source in range(l...]
    ppermute x0 -> x1, waiting for transfers between devices: none -> 3.25 us  [body(): from_partner = lax.ppermute(to_partner, 'core', [(0, 1), (1, 0)])]
    another operation x19, other arithmetic: 4.15 us -> 7.08 us
    add x0 -> x1, other arithmetic: none -> 2.64 us  [body(): padded_w = padded_w + marker.astype(jnp.bfloat16)[None]]
  transfers between devices with their start and end apart: 6 -> 7, of which waited for: 4 -> 5; matrix products, arithmetic and copies ran while one was open for 10% -> 13% of each run, Pallas kernels for 0% -> 0%
where the time goes in v13:
time: 150 us; the launch traced here: 148 us
  waiting for transfers between devices  33.6 us (22%)
  starting transfers between devices  31.5 us (21%)
  blocking collectives  31.3 us (21%)
  local copies, waits for them, and re-layouts  23 us (15%)
  other arithmetic  17.1 us (11%)
  matrix products  10.5 us (7%)
    ppermute x5, starting transfers between devices, from_behind(): lax.ppermute(value, axis, [(source, source + steps) for source in range(l...  26.8 us
    all_to_all x1, blocking collectives, body(): lax.all_to_all(buffer.reshape(local_feat, seq_count, slot_cap), 'seq', sp...  20 us
    all_to_all x1, waiting for transfers between devices, body(): lax.all_to_all(paired.astype(jnp.bfloat16), 'x', 0, 0, tiled=False)  18.7 us
    ppermute x5, waiting for transfers between devices, from_behind(): lax.ppermute(value, axis, [(source, source + steps) for source in range(l...  11.7 us
    unnamed x55, local copies, waits for them, and re-layouts  10.1 us
    psum x1, blocking collectives, body(): lax.psum(lax.psum((jnp.sum(out_wide, axis=0), jnp.sum(out_wide * out_wide...  8.87 us
    another operation x19, other arithmetic  7.08 us
    add x1, local copies, waits for them, and re-layouts, body(): padded_w = padded_w + marker.astype(jnp.bfloat16)[None]  6.31 us
  transfers between devices with their start and end apart: 7, of which 5 were waited for; matrix products, arithmetic and copies ran while one was open for 13% of the time, Pallas kernels for 0%

profile of v13, /device:TPU:32, one launch (start us, length us, event | category | flops | bytes accessed | tf_op | source)
XLA Modules:
  0.0 148.4 jit_solution(5837764693925837137)
XLA Ops:
  3.8 1.4 copy.54
  8.5 3.5 %collective-permute-start = (bf16[656,128]{1,0:T(8,128)(2,1)S(1)}, bf16[656,128]{1,0:T(8,128)(2,1)S(1)}, u32[]{:S(2)}, u32[]{:S(2)}) collective-permute-start(bf16[656,128]{1,0:T(8,128)(2,1)S(1)} %pad_maximum_fusion), channel_id=1, source_target_pairs={{0,8},{8,16},{16,24},{24,32},{32,40},{40,48},{48,56},{56,64},{64,7... | collective-permute-start | bytes 503816 | tf_op jit(solution)/shard_map/ppermute | solution.py:15
  12.5 6.1 %collective-permute-done = bf16[656,128]{1,0:T(8,128)(2,1)S(1)} collective-permute-done((bf16[656,128]{1,0:T(8,128)(2,1)S(1)}, bf16[656,128]{1,0:T(8,128)(2,1)S(1)}, u32[]{:S(2)}, u32[]{:S(2)}) %collective-permute-start) | collective-permute-done | bytes 167968 | tf_op jit(solution)/shard_map/ppermute | solution.py:15
  18.8 3.0 %collective-permute-start.1 = (bf16[656,128]{1,0:T(8,128)(2,1)S(1)}, bf16[656,128]{1,0:T(8,128)(2,1)S(1)}, u32[]{:S(2)}, u32[]{:S(2)}) collective-permute-start(bf16[656,128]{1,0:T(8,128)(2,1)S(1)} %pad_maximum_fusion.1), channel_id=1, source_target_pairs={{0,16},{8,24},{16,32},{24,40},{32,48},{40,56},{48,64},{56,72},{64,... | collective-permute-start | bytes 503816 | tf_op jit(solution)/shard_map/ppermute | solution.py:15
  21.8 2.9 %fusion.21 = f32[2,256,10,64]{1,3,2,0:T(8,128)} fusion(f32[10,2,256]{2,0,1:T(8,128)S(1)} %copy.53, f32[10,2,256]{2,0,1:T(8,128)S(1)} %copy.51, f32[2,256,256]{2,1,0:T(8,128)S(1)} %fusion.129, pred[256,256]{1,0:T(8,128)(4,1)S(1)} %iota_compare_fusion.8, bf16[2,256,10,64]{1,0,3,2:T(2,128)(2,1)S(1)} %reshape.803), kind=kOutput, calls=%fused_computation.22 | convolution fusion | flops 175636480 | bytes 2596864 | tf_op jit(solution)/shard_map/hcts,cshp->cthp/dot_general | solution.py:48
  24.7 3.8 %collective-permute-done.1 = bf16[656,128]{1,0:T(8,128)(2,1)S(1)} collective-permute-done((bf16[656,128]{1,0:T(8,128)(2,1)S(1)}, bf16[656,128]{1,0:T(8,128)(2,1)S(1)}, u32[]{:S(2)}, u32[]{:S(2)}) %collective-permute-start.1) | collective-permute-done | bytes 167968 | tf_op jit(solution)/shard_map/ppermute | solution.py:15
  30.4 3.8 %collective-permute-start.2 = (bf16[656,128]{1,0:T(8,128)(2,1)}, bf16[656,128]{1,0:T(8,128)(2,1)}, u32[]{:S(2)}, u32[]{:S(2)}) collective-permute-start(bf16[656,128]{1,0:T(8,128)(2,1)} %pad_maximum_fusion.2), channel_id=1, source_target_pairs={{0,32},{8,40},{16,48},{24,56},{32,64},{40,72},{48,80},{56,88},{64,... | collective-permute-start | bytes 503816 | tf_op jit(solution)/shard_map/ppermute | solution.py:15
  34.2 4.2 %copy.45 = bf16[640,2560]{0,1:T(8,128)(2,1)S(1)} copy(bf16[640,2560]{1,0:T(8,128)(2,1)} %param.34) | data formatting | bytes 6553600 | tf_op args[8]
  39.5 2.2 %add_convert_fusion.2 = (bf16[640,128]{1,0:T(8,128)(2,1)S(1)}, f32[640,128]{1,0:T(8,128)}) fusion(f32[640,128]{1,0:T(8,128)} %copy-done.1, f32[640]{0:T(1024)S(1)} %mul.287, f32[656,128]{1,0:T(8,128)} %copy-done.2, f32[656,128]{1,0:T(8,128)} %copy-done.4, f32[640]{0:T(1024)S(1)} %mul.291, f32[656,128]{1,0:T(8,128)S(1)} %convert_element_type.109, ...), kind=kLoop, calls=%fused_computation.72 | loop fusion | flops 573440 | bytes 1809920 | tf_op jit(solution)/shard_map/convert.11
  41.8 8.8 %collective-permute-start.3 = (bf16[656,128]{1,0:T(8,128)(2,1)S(1)}, bf16[656,128]{1,0:T(8,128)(2,1)S(1)}, u32[]{:S(2)}, u32[]{:S(2)}) collective-permute-start(bf16[656,128]{1,0:T(8,128)(2,1)S(1)} %pad_maximum_fusion.3), channel_id=1, source_target_pairs={{0,64},{8,72},{16,80},{24,88},{32,96},{40,104},{48,112},{56,120},{... | collective-permute-start | bytes 503816 | tf_op jit(solution)/shard_map/ppermute | solution.py:15
  51.7 1.8 %collective-permute-done.3 = bf16[656,128]{1,0:T(8,128)(2,1)S(1)} collective-permute-done((bf16[656,128]{1,0:T(8,128)(2,1)S(1)}, bf16[656,128]{1,0:T(8,128)(2,1)S(1)}, u32[]{:S(2)}, u32[]{:S(2)}) %collective-permute-start.3) | collective-permute-done | bytes 167968 | tf_op jit(solution)/shard_map/ppermute | solution.py:15
  55.1 1.5 add_convert_fusion.1
  57.3 7.7 %collective-permute-start.4 = (bf16[656,128]{1,0:T(8,128)(2,1)}, bf16[656,128]{1,0:T(8,128)(2,1)}, u32[]{:S(2)}, u32[]{:S(2)}) collective-permute-start(bf16[656,128]{1,0:T(8,128)(2,1)} %pad_maximum_fusion.4), channel_id=1, source_target_pairs={{0,128},{8,136},{16,144},{24,152},{32,160},{40,168},{48,176},{56,1... | collective-permute-start | bytes 503816 | tf_op jit(solution)/shard_map/ppermute | solution.py:15
  65.0 2.6 %pad_add_fusion = bf16[8,336,656]{2,1,0:T(8,128)(2,1)} fusion(bf16[8,320,640]{2,1,0:T(8,128)(2,1)S(1)} %bitcast.121, bf16[336,656]{1,0:T(8,128)(2,1)S(1)} %copy-done.7), kind=kLoop, calls=%fused_computation.1 | loop fusion | flops 7053312 | bytes 7244288 | tf_op jit(solution)/shard_map/add | solution.py:121
  67.7 6.3 %copy.46 = bf16[8,336,656]{1,2,0:T(8,128)(2,1)} copy(bf16[8,336,656]{2,1,0:T(8,128)(2,1)} %pad_add_fusion) | data formatting | bytes 7053312 | tf_op jit(solution)/shard_map/add | solution.py:121
  81.8 1.3 fusion.16
  83.4 3.2 %collective-permute-done.5 = bf16[4,336,512]{2,1,0:T(8,128)(2,1)} collective-permute-done((bf16[4,336,512]{2,1,0:T(8,128)(2,1)S(1)}, bf16[4,336,512]{2,1,0:T(8,128)(2,1)}, u32[]{:S(2)}, u32[]{:S(2)}) %collective-permute-start.5) | collective-permute-done | bytes 1376288 | tf_op jit(solution)/shard_map/ppermute | solution.py:137
  86.6 3.2 %convert_add_fusion = f32[4,336,512]{2,1,0:T(8,128)S(1)} fusion(bf16[4,336,512]{2,1,0:T(8,128)(2,1)} %collective-permute-done.5, bf16[4,2,336,656]{2,3,1,0:T(8,128)(2,1)} %bitcast.124, s32[]{:T(128)S(6)} %select_n.21, bf16[512,3]{0,1:T(4,128)(2,1)S(1)} %fusion.80, bf16[512,640]{0,1:T(8,128)(2,1)S(1)} %get-tuple-element.109), kind=kOutput, calls=%fused_computation.2 | convolution fusion | flops 907591680 | bytes 6802436 | tf_op jit(solution)/shard_map/gdk,tk->gdt/dot_general | solution.py:138
  90.2 1.3 convert_element_type.118
  91.5 4.4 %all-to-all-start = ((bf16[4,336,512]{2,1,0:T(8,128)(2,1)}), bf16[4,336,512]{2,1,0:T(8,128)(2,1)S(1)}, u32[]{:S(2)}, u32[]{:S(2)}) async-start(bf16[4,336,512]{2,1,0:T(8,128)(2,1)} %convert_element_type.118), calls=%async_computation | async-start | bytes 2752512 | tf_op jit(solution)/shard_map/all_to_all | solution.py:149
  96.1 18.7 %all-to-all-done = bf16[4,336,512]{2,1,0:T(8,128)(2,1)S(1)} async-done(((bf16[4,336,512]{2,1,0:T(8,128)(2,1)}), bf16[4,336,512]{2,1,0:T(8,128)(2,1)S(1)}, u32[]{:S(2)}, u32[]{:S(2)}) %all-to-all-start) | async-done | bytes 1376288 | tf_op jit(solution)/shard_map/all_to_all | solution.py:149
  115.2 2.5 %all-reduce.10 = (f32[512]{0:T(512)S(1)}, f32[512]{0:T(512)S(1)}) all-reduce(f32[512]{0:T(512)S(1)} %get-tuple-element.91, f32[512]{0:T(512)S(1)} %get-tuple-element.90), channel_id=1, replica_groups=mesh['seq'=32,'x'=4,'core'=2] {'core'}, use_global_device_ids=true, to_apply=%region_16.17 | all-reduce | flops 1024 | bytes 8192 | tf_op jit(solution)/shard_map/psum | solution.py:171
  117.7 8.9 %all-reduce.9 = (f32[512]{0:T(512)S(1)}, f32[512]{0:T(512)S(1)}) all-reduce(f32[512]{0:T(512)S(1)} %get-tuple-element.94, f32[512]{0:T(512)S(1)} %get-tuple-element.95), channel_id=1, replica_groups=mesh['seq'=32,'x'=4,'core'=2] {'x'}, use_global_device_ids=true, to_apply=%region_17.18 | all-reduce | flops 1024 | bytes 8192 | tf_op jit(solution)/shard_map/psum | solution.py:170
  127.5 20.0 %all_to_all.10 = bf16[320,32,16]{0,2,1:T(8,128)(2,1)S(1)} all-to-all(bf16[320,32,16]{0,2,1:T(8,128)(2,1)S(1)} %bitcast.126), channel_id=1, replica_groups=mesh['seq'=32,'x'=4,'core'=2] {'seq'}, dimensions={1} | all-to-all | bytes 655360 | tf_op jit(solution)/shard_map/all_to_all | solution.py:184
  (159 shorter events, 24.0 us)
Async XLA Ops:
  0.6 11.4 %copy-start = (bf16[512,128]{1,0:T(8,128)(2,1)S(1)}, bf16[512,128]{1,0:T(8,128)(2,1)}, u32[]{:S(2)}) copy-start(bf16[512,128]{1,0:T(8,128)(2,1)} %param.31) | copy-start | bytes 393220
  3.7 2.0 %copy-start.18 = (bf16[512,128]{1,0:T(8,128)(2,1)S(1)}, bf16[512,128]{1,0:T(8,128)(2,1)}, u32[]{:S(2)}) copy-start(bf16[512,128]{1,0:T(8,128)(2,1)} %param.30) | copy-start | bytes 393220
  5.3 16.5 %copy-start.5 = (bf16[2,256,10,64]{1,0,3,2:T(2,128)(2,1)}, bf16[2,256,10,64]{1,0,3,2:T(2,128)(2,1)S(1)}, u32[]{:S(2)}) copy-start(bf16[2,256,10,64]{1,0,3,2:T(2,128)(2,1)S(1)} %reshape.803) | copy-start | bytes 1966084
  8.5 20.9 %copy-start.1 = (f32[640,128]{1,0:T(8,128)}, f32[640,128]{1,0:T(8,128)S(1)}, u32[]{:S(2)}) copy-start(f32[640,128]{1,0:T(8,128)S(1)} %get-tuple-element.108) | copy-start | bytes 983044
  8.5 10.0 %collective-permute-start = (bf16[656,128]{1,0:T(8,128)(2,1)S(1)}, bf16[656,128]{1,0:T(8,128)(2,1)S(1)}, u32[]{:S(2)}, u32[]{:S(2)}) collective-permute-start(bf16[656,128]{1,0:T(8,128)(2,1)S(1)} %pad_maximum_fusion), channel_id=1, source_target_pairs={{0,8},{8,16},{16,24},{24,32},{32,40},{40,48},{48,56},{56,64},{64,7... | collective-permute-start | bytes 503816 | tf_op jit(solution)/shard_map/ppermute | solution.py:15
  18.6 6.2 %copy-start.8 = (bf16[656,128]{1,0:T(8,128)(2,1)}, bf16[656,128]{1,0:T(8,128)(2,1)S(1)}, u32[]{:S(2)}) copy-start(bf16[656,128]{1,0:T(8,128)(2,1)S(1)} %collective-permute-done) | copy-start | bytes 503812
  18.6 10.8 %copy-start.2 = (f32[656,128]{1,0:T(8,128)}, f32[656,128]{1,0:T(8,128)S(1)}, u32[]{:S(2)}) copy-start(f32[656,128]{1,0:T(8,128)S(1)} %convert_element_type.107) | copy-start | bytes 1007620
  18.8 9.7 %collective-permute-start.1 = (bf16[656,128]{1,0:T(8,128)(2,1)S(1)}, bf16[656,128]{1,0:T(8,128)(2,1)S(1)}, u32[]{:S(2)}, u32[]{:S(2)}) collective-permute-start(bf16[656,128]{1,0:T(8,128)(2,1)S(1)} %pad_maximum_fusion.1), channel_id=1, source_target_pairs={{0,16},{8,24},{16,32},{24,40},{32,48},{40,56},{48,64},{56,72},{64,... | collective-permute-start | bytes 503816 | tf_op jit(solution)/shard_map/ppermute | solution.py:15
  29.2 5.0 %copy-start.4 = (f32[656,128]{1,0:T(8,128)}, f32[656,128]{1,0:T(8,128)S(1)}, u32[]{:S(2)}) copy-start(f32[656,128]{1,0:T(8,128)S(1)} %convert_element_type.108) | copy-start | bytes 1007620
  30.4 8.2 %collective-permute-start.2 = (bf16[656,128]{1,0:T(8,128)(2,1)}, bf16[656,128]{1,0:T(8,128)(2,1)}, u32[]{:S(2)}, u32[]{:S(2)}) collective-permute-start(bf16[656,128]{1,0:T(8,128)(2,1)} %pad_maximum_fusion.2), channel_id=1, source_target_pairs={{0,32},{8,40},{16,48},{24,56},{32,64},{40,72},{48,80},{56,88},{64,... | collective-permute-start | bytes 503816 | tf_op jit(solution)/shard_map/ppermute | solution.py:15
  41.8 11.7 %collective-permute-start.3 = (bf16[656,128]{1,0:T(8,128)(2,1)S(1)}, bf16[656,128]{1,0:T(8,128)(2,1)S(1)}, u32[]{:S(2)}, u32[]{:S(2)}) collective-permute-start(bf16[656,128]{1,0:T(8,128)(2,1)S(1)} %pad_maximum_fusion.3), channel_id=1, source_target_pairs={{0,64},{8,72},{16,80},{24,88},{32,96},{40,104},{48,112},{56,120},{... | collective-permute-start | bytes 503816 | tf_op jit(solution)/shard_map/ppermute | solution.py:15
  55.1 9.9 %copy-start.7 = (bf16[336,656]{1,0:T(8,128)(2,1)S(1)}, bf16[336,656]{1,0:T(8,128)(2,1)}, u32[]{:S(2)}) copy-start(bf16[336,656]{1,0:T(8,128)(2,1)} %and_convert_fusion) | copy-start | bytes 1322500
  57.3 18.8 %collective-permute-start.4 = (bf16[656,128]{1,0:T(8,128)(2,1)}, bf16[656,128]{1,0:T(8,128)(2,1)}, u32[]{:S(2)}, u32[]{:S(2)}) collective-permute-start(bf16[656,128]{1,0:T(8,128)(2,1)} %pad_maximum_fusion.4), channel_id=1, source_target_pairs={{0,128},{8,136},{16,144},{24,152},{32,160},{40,168},{48,176},{56,1... | collective-permute-start | bytes 503816 | tf_op jit(solution)/shard_map/ppermute | solution.py:15
  67.6 6.3 %copy-start.17 = (bf16[512,640]{1,0:T(8,128)(2,1)S(1)}, bf16[512,640]{1,0:T(8,128)(2,1)}, u32[]{:S(2)}) copy-start(bf16[512,640]{1,0:T(8,128)(2,1)} %param.27) | copy-start | bytes 1966084
  74.0 2.0 %copy-start.13 = (bf16[656,128]{1,0:T(8,128)(2,1)S(1)}, bf16[656,128]{1,0:T(8,128)(2,1)}, u32[]{:S(2)}) copy-start(bf16[656,128]{1,0:T(8,128)(2,1)} %copy-done.12) | copy-start | bytes 503812
  76.0 1.7 %copy-start.16 = (f32[2,256,10,64]{1,3,2,0:T(8,128)S(1)}, f32[2,256,10,64]{1,3,2,0:T(8,128)}, u32[]{:S(2)}) copy-start(f32[2,256,10,64]{1,3,2,0:T(8,128)} %fusion.21) | copy-start | bytes 3932164
  76.0 1.7 %copy-start.24 = (f32[10]{0:T(128)S(1)}, f32[10]{0:T(128)}, u32[]{:S(2)}) copy-start(f32[10]{0:T(128)} %param.32) | copy-start | bytes 124
  79.6 2.1 %copy-start.3 = (bf16[8,336,656]{1,2,0:T(8,128)(2,1)S(1)}, bf16[8,336,656]{1,2,0:T(8,128)(2,1)}, u32[]{:S(2)}) copy-start(bf16[8,336,656]{1,2,0:T(8,128)(2,1)} %copy.46) | copy-start | bytes 10579972
  83.1 3.5 %collective-permute-start.5 = (bf16[4,336,512]{2,1,0:T(8,128)(2,1)S(1)}, bf16[4,336,512]{2,1,0:T(8,128)(2,1)}, u32[]{:S(2)}, u32[]{:S(2)}) collective-permute-start(bf16[4,336,512]{2,1,0:T(8,128)(2,1)S(1)} %fusion.16), channel_id=1, source_target_pairs={{0,1},{1,0},{2,3},{3,2},{4,5},{5,4},{6,7},{7,6},{8,9},{9,8},{10,11... | collective-permute-start | bytes 4128776 | tf_op jit(solution)/shard_map/ppermute | solution.py:137
  91.5 4.4 %copy-start.23 = (s32[256]{0:T(256)S(1)}, s32[256]{0:T(256)}, u32[]{:S(2)}) copy-start(s32[256]{0:T(256)} %param.37) | copy-start | bytes 3076
  91.5 4.7 %copy-start.22 = (s32[256]{0:T(256)S(1)}, s32[256]{0:T(256)}, u32[]{:S(2)}) copy-start(s32[256]{0:T(256)} %param.36) | copy-start | bytes 3076
  91.5 23.3 %all-to-all-start = ((bf16[4,336,512]{2,1,0:T(8,128)(2,1)}), bf16[4,336,512]{2,1,0:T(8,128)(2,1)S(1)}, u32[]{:S(2)}, u32[]{:S(2)}) async-start(bf16[4,336,512]{2,1,0:T(8,128)(2,1)} %convert_element_type.118), calls=%async_computation | async-start | bytes 2752512 | tf_op jit(solution)/shard_map/all_to_all | solution.py:149
  95.9 19.1 %copy-start.19 = (bf16[320,512]{1,0:T(8,128)(2,1)S(1)}, bf16[320,512]{1,0:T(8,128)(2,1)}, u32[]{:S(2)}) copy-start(bf16[320,512]{1,0:T(8,128)(2,1)} %param.35) | copy-start | bytes 983044
  115.2 32.3 %copy-start.20 = (bf16[320,512]{1,0:T(8,128)(2,1)}, bf16[320,512]{1,0:T(8,128)(2,1)S(1)}, u32[]{:S(2)}) copy-start(bf16[320,512]{1,0:T(8,128)(2,1)S(1)} %get-tuple-element.96) | copy-start | bytes 983044
  (8 other events, 7.6 us)
